TPU v7x, 32 devices: a whole 2x2x4 slice. The times are simulated.
32 devices in a mesh: seq: 16 (over z, x, core), batch: 2 (over y).
Axes of the slice: x: 2, y: 2, z: 4, core: 2. Of those that a mesh axis runs over, the one named last changes fastest.
Arguments:
- activations: bfloat16 [2, 8192, 1536], P('batch', 'seq'), may hold values from -60 to 60
- cotangent: bfloat16 [2, 8192, 1536], P('batch', 'seq'), may hold values from -6 to 6
- contig_lengths: int32 [2, 4], P('batch'), may hold values from 1 to 4096, 8192 in all within a row
- gain_input: float32 [1536], replicated, may hold values from 0.1 to 1.9
- tap_weights: bfloat16 [3, 1536, 768], replicated, may hold values from -0.09375 to 0.09375
- gain_middle: float32 [768], replicated, may hold values from 0.1 to 1.9
- point_weights: bfloat16 [768, 1536], replicated, may hold values from -0.21875 to 0.21875
Outputs:
- block_output: bfloat16 [2, 8192, 1536], P('batch', 'seq')
- input_grad: bfloat16 [2, 8192, 1536], P('batch', 'seq')
- gain_input_grad: float32 [1536], replicated
- gain_middle_grad: float32 [768], replicated
Inputs may be any that keep to these rules, and one draw needn't show every extreme that they name: `contig_lengths`: row w lists in order the lengths of the 4 contigs packed into window w; they sum to 8192.
All inputs are finite; a program needn't handle non-finite values.
Results may differ from a plain program's by a relative error of at most 0.0065.
Values may be sent and summed in bfloat16 or wider, within the bound.
No kernel may reach another device: no remote copies, remote signals or barrier semaphores. Data moves between devices by JAX's collectives and lax.ppermute only.
A program may use at most 64 MiB of HBM per device.

v0:
```python
import math

import jax
import jax.numpy as jnp
from jax import lax
from jax.sharding import PartitionSpec as P

SPAN = 2


epsilon = 1e-06


def shifted(x, axis, by):
    peers = lax.axis_size(axis)
    pairs = [(i, i + by) for i in range(peers) if 0 <= i + by < peers]
    return lax.ppermute(x, axis, pairs)


def norm_activate(values, scales):
    mean_square = jnp.mean(values * values, axis=-1, keepdims=True)
    return jax.nn.gelu(values * lax.rsqrt(mean_square + epsilon) * scales, approximate=True)


def contig_owner(lengths, positions):
    bounds = jnp.cumsum(lengths)
    return jnp.sum((positions[:, None] >= bounds[None, :]).astype(jnp.int32), axis=1)


def body(
    activations, cotangent, contig_lengths, gain_input, tap_weights, gain_middle, point_weights
):
    signal = activations[0]
    upstream = cotangent[0]
    lengths = contig_lengths[0]
    shard_rows = signal.shape[0]
    seq_count = lax.axis_size("seq")
    tap_reach = SPAN * shard_rows
    total_length = shard_rows * seq_count
    positions = lax.axis_index("seq") * shard_rows + jnp.arange(shard_rows, dtype=jnp.int32)
    owners = contig_owner(lengths, positions)
    before_valid = (
        (positions >= tap_reach) & (contig_owner(lengths, positions - tap_reach) == owners)
    ).astype(jnp.float32)[:, None]
    after_valid = (
        (positions < total_length - tap_reach)
        & (contig_owner(lengths, positions + tap_reach) == owners)
    ).astype(jnp.float32)[:, None]
    tap_before = tap_weights[0]
    tap_center = tap_weights[1]
    tap_after = tap_weights[2]
    normed, input_vjp = jax.vjp(norm_activate, signal.astype(jnp.float32), gain_input)
    hidden = normed.astype(jnp.bfloat16)
    hidden_before = shifted(hidden, "seq", SPAN)
    hidden_after = shifted(hidden, "seq", -SPAN)
    combined = jnp.dot(hidden, tap_center, preferred_element_type=jnp.float32)
    combined = combined + before_valid * jnp.dot(
        hidden_before, tap_before, preferred_element_type=jnp.float32
    )
    combined = combined + after_valid * jnp.dot(
        hidden_after, tap_after, preferred_element_type=jnp.float32
    )
    middle_f, middle_vjp = jax.vjp(norm_activate, combined, gain_middle)
    middle = middle_f.astype(jnp.bfloat16)
    output = (
        signal.astype(jnp.float32)
        + jnp.dot(middle, point_weights, preferred_element_type=jnp.float32)
    ).astype(jnp.bfloat16)
    grad_middle = jnp.dot(upstream, point_weights.T, preferred_element_type=jnp.float32)
    grad_combined_f, middle_terms = middle_vjp(grad_middle)
    grad_combined = grad_combined_f.astype(jnp.bfloat16)
    grad_hidden = jnp.dot(grad_combined, tap_center.T, preferred_element_type=jnp.float32)
    forward_terms = jnp.dot(grad_combined, tap_after.T, preferred_element_type=jnp.float32)
    backward_terms = jnp.dot(grad_combined, tap_before.T, preferred_element_type=jnp.float32)
    terms_before = shifted(forward_terms.astype(jnp.bfloat16), "seq", SPAN).astype(
        forward_terms.dtype
    )
    terms_after = shifted(backward_terms.astype(jnp.bfloat16), "seq", -SPAN).astype(
        backward_terms.dtype
    )
    grad_hidden = grad_hidden + before_valid * terms_before + after_valid * terms_after
    grad_signal, input_terms = input_vjp(grad_hidden)
    grad_output = (upstream.astype(jnp.float32) + grad_signal).astype(jnp.bfloat16)
    summed = lax.psum((input_terms, middle_terms), ("seq", "batch"))
    factor = 1.0 / math.sqrt(lax.axis_size("batch") * seq_count * shard_rows)
    return (output[None], grad_output[None], summed[0] * factor, summed[1] * factor)


def solution(mesh):
    placed = (
        P("batch", "seq", None),
        P("batch", "seq", None),
        P("batch", None),
        P(),
        P(),
        P(),
        P(),
    )
    return jax.shard_map(
        body,
        mesh=mesh,
        in_specs=placed,
        out_specs=(P("batch", "seq", None), P("batch", "seq", None), P(), P()),
        check_vma=False,
    )
```

profile of v0, /device:TPU:0, one launch (start us, length us, event | category | flops | bytes accessed | tf_op | source)
XLA Modules:
  0.0 216.5 jit_solution(4614288820705404492)
XLA Ops:
  0.6 0.0 copy-start
  0.6 0.0 copy-start.1
  0.7 0.0 copy-start.4
  0.7 1.9 fusion.16
  2.6 0.1 copy-done.1
  2.7 3.2 %fusion.12 = bf16[512,1536]{1,0:T(8,128)(2,1)} fusion(bf16[1,512,1536]{2,1,0:T(8,128)(2,1)S(1)} %copy-done.1, f32[1536]{0:T(1024)} %param.10, f32[512]{0:T(512)S(1)} %fusion.88), kind=kLoop, calls=%fused_computation.18 | loop fusion | flops 9437184 | bytes 3153920 | tf_op jit(solution)/shard_map/convert_element_type | solution.py:53
  5.9 6.0 %collective-permute-start = (bf16[512,1536]{1,0:T(8,128)(2,1)}, bf16[512,1536]{1,0:T(8,128)(2,1)}, u32[]{:S(2)}, u32[]{:S(2)}) collective-permute-start(bf16[512,1536]{1,0:T(8,128)(2,1)} %fusion.12), channel_id=1, source_target_pairs={{0,4},{2,6},{4,8},{6,10},{8,12},{10,14},{12,16},{14,18},{16,20},{1... | collective-permute-start | bytes 4718600 | tf_op jit(solution)/shard_map/ppermute | solution.py:17
  11.9 1.3 collective-permute-start.1
  13.2 0.2 reduce-window.8
  13.4 0.1 convert_reduce_fusion.2
  13.5 4.4 %fusion.42 = f32[512,768]{1,0:T(8,128)S(1)} fusion(bf16[3,1536,768]{2,1,0:T(8,128)(2,1)} %param.11, bf16[1,512,1536]{2,1,0:T(8,128)(2,1)} %param.7, f32[1536]{0:T(1024)S(1)} %copy-done.4, f32[512]{0:T(512)S(1)} %fusion.88), kind=kOutput, calls=%fused_computation.51 | convolution fusion | flops 1217396736 | bytes 5513216 | tf_op jit(solution)/shard_map/dot_general | solution.py:56
  17.9 60.5 %collective-permute-done = bf16[512,1536]{1,0:T(8,128)(2,1)} collective-permute-done((bf16[512,1536]{1,0:T(8,128)(2,1)}, bf16[512,1536]{1,0:T(8,128)(2,1)}, u32[]{:S(2)}, u32[]{:S(2)}) %collective-permute-start) | collective-permute-done | bytes 1572896 | tf_op jit(solution)/shard_map/ppermute | solution.py:17
  78.4 3.5 %fusion.38 = f32[512,768]{1,0:T(8,128)S(1)} fusion(bf16[512,1536]{1,0:T(8,128)(2,1)} %collective-permute-done, bf16[3,1536,768]{2,1,0:T(8,128)(2,1)} %param.11), kind=kOutput, calls=%fused_computation.47 | convolution fusion | flops 1207959552 | bytes 5505024 | tf_op jit(solution)/shard_map/dot_general | solution.py:57
  81.9 0.0 copy-start.3
  82.0 0.0 copy-start.5
  82.0 3.8 %multiply_reduce_fusion.2 = (f32[512]{0:T(512)S(1)}, f32[512,768]{1,0:T(8,128)S(1)}) fusion(bf16[512,1536]{1,0:T(8,128)(2,1)} %collective-permute-done.1, bf16[3,1536,768]{2,1,0:T(8,128)(2,1)} %param.11, f32[512]{0:T(512)S(1)} %get-tuple-element.14, f32[512,768]{1,0:T(8,128)S(1)} %fusion.42, f32[512,768]{1,0:T(8,128)S(1)} %fusion.38, ...), kind=kOutput, calls=%fused_computation.75 | convolution fusion | flops 1210318336 | bytes 8656896 | tf_op jit(solution)/shard_map/dot_general | solution.py:60
  85.8 0.0 slice-start
  85.9 2.5 %multiply_reduce_fusion = (f32[768]{0:T(1024)S(1)}, f32[512]{0:T(512)S(1)}, f32[512,768]{1,0:T(8,128)S(1)}) fusion(f32[512,768]{1,0:T(8,128)S(1)} %get-tuple-element.16, f32[512]{0:T(512)S(1)} %fusion.89, f32[768]{0:T(1024)S(1)} %copy-done.5, bf16[768,1536]{1,0:T(8,128)(2,1)S(1)} %copy-done, bf16[1,512,1536]{2,1,0:T(8,128)(2,1)S(1)} %copy-done.3), kind=kOutput, calls=%fused_computation.72 | convolution fusion | flops 1218181888 | bytes 7088128 | tf_op jit(solution)/shard_map/dot_general | solution.py:69
  88.4 0.4 fusion.58
  88.8 0.1 slice-done.1
  88.9 1.4 convolution_convert_fusion
  90.3 0.0 copy-start.2
  90.4 1.4 convolution_convert_fusion.1
  91.8 4.5 %collective-permute-start.2 = (bf16[512,1536]{1,0:T(8,128)(2,1)S(1)}, bf16[512,1536]{1,0:T(8,128)(2,1)S(1)}, u32[]{:S(2)}, u32[]{:S(2)}) collective-permute-start(bf16[512,1536]{1,0:T(8,128)(2,1)S(1)} %convolution_convert_fusion.1), channel_id=1, source_target_pairs={{0,4},{2,6},{4,8},{6,10},{8,12},{10,14},{12,16},{14,18},{16,20},{1... | collective-permute-start | bytes 4718600 | tf_op jit(solution)/shard_map/ppermute | solution.py:17
  96.3 1.5 collective-permute-start.3
  97.8 2.8 %fusion.33 = bf16[1,512,1536]{2,1,0:T(8,128)(2,1)} fusion(bf16[768,1536]{1,0:T(8,128)(2,1)S(1)} %copy-done, bf16[1,512,1536]{2,1,0:T(8,128)(2,1)S(1)} %copy-done.2, f32[512,768]{1,0:T(8,128)S(1)} %get-tuple-element.16, f32[768]{0:T(1024)S(1)} %copy-done.5, f32[512]{0:T(512)S(1)} %fusion.89), kind=kOutput, calls=%fused_computation.41 | convolution fusion | flops 1214644224 | bytes 7083008 | tf_op jit(solution)/shard_map/dot_general | solution.py:67
  100.6 62.0 %collective-permute-done.2 = bf16[512,1536]{1,0:T(8,128)(2,1)S(1)} collective-permute-done((bf16[512,1536]{1,0:T(8,128)(2,1)S(1)}, bf16[512,1536]{1,0:T(8,128)(2,1)S(1)}, u32[]{:S(2)}, u32[]{:S(2)}) %collective-permute-start.2) | collective-permute-done | bytes 1572896 | tf_op jit(solution)/shard_map/ppermute | solution.py:17
  162.7 6.1 %fusion.15 = (f32[1536]{0:T(1024)S(1)}, f32[512]{0:T(512)S(1)}, f32[512,1536]{1,0:T(8,128)}) fusion(bf16[1,512,1536]{2,1,0:T(8,128)(2,1)S(1)} %copy-done.2, f32[512]{0:T(512)S(1)} %fusion.88, f32[1536]{0:T(1024)S(1)} %copy-done.4, bf16[512,1536]{1,0:T(8,128)(2,1)S(1)} %collective-permute-done.3, f32[512]{0:T(512)S(1)} %get-tuple-element.14, ...), kind=kOutput, calls=%fused_computation.21 | convolution fusion | flops 1233909760 | bytes 11032576 | tf_op jit(solution)/shard_map/dot_general | solution.py:72
  168.8 41.6 %all-reduce = (f32[1536]{0:T(1024)S(1)}, f32[768]{0:T(1024)S(1)}) all-reduce(f32[1536]{0:T(1024)S(1)} %get-tuple-element.4, f32[768]{0:T(1024)S(1)} %get-tuple-element.6), channel_id=1, replica_groups=mesh['seq'=16,'batch'=2] {'seq','batch'}, use_global_device_ids=true, to_apply=%region_9.10 | all-reduce | flops 2304 | bytes 18432 | tf_op jit(solution)/shard_map/psum | solution.py:84
  210.4 0.6 broadcast_multiply_fusion
  211.0 0.6 broadcast_multiply_fusion.1
  211.6 4.9 %fusion.59 = bf16[1,512,1536]{2,1,0:T(8,128)(2,1)} fusion(bf16[1,512,1536]{2,1,0:T(8,128)(2,1)} %param.7, f32[512,1536]{1,0:T(8,128)} %get-tuple-element.18, bf16[1,512,1536]{2,1,0:T(8,128)(2,1)} %param.8, f32[512]{0:T(512)S(1)} %multiply_multiply_fusion.6, f32[1536]{0:T(1024)S(1)} %copy-done.4, f32[512]{0:T(512)S(1)} %fusion.88), kind=kLoop, calls=%fused_computation.68 | loop fusion | flops 7077888 | bytes 7874560 | tf_op jit(solution)/shard_map/broadcast_in_dim | solution.py:86
  (19 shorter events, 0.1 us)
Async XLA Ops:
  0.6 85.2 %copy-start = (bf16[768,1536]{1,0:T(8,128)(2,1)S(1)}, bf16[768,1536]{1,0:T(8,128)(2,1)}, u32[]{:S(2)}) copy-start(bf16[768,1536]{1,0:T(8,128)(2,1)} %param.13) | copy-start | bytes 7077892
  0.6 2.0 copy-start.1
  0.7 12.8 %copy-start.4 = (f32[1536]{0:T(1024)S(1)}, f32[1536]{0:T(1024)}, u32[]{:S(2)}) copy-start(f32[1536]{0:T(1024)} %param.10) | copy-start | bytes 18436
  0.7 12.5 %copy-start.6 = (s32[1,4]{1,0:T(1,128)S(1)}, s32[1,4]{1,0:T(1,128)}, u32[]{:S(2)}) copy-start(s32[1,4]{1,0:T(1,128)} %param.9) | copy-start | bytes 52
  5.9 72.5 %collective-permute-start = (bf16[512,1536]{1,0:T(8,128)(2,1)}, bf16[512,1536]{1,0:T(8,128)(2,1)}, u32[]{:S(2)}, u32[]{:S(2)}) collective-permute-start(bf16[512,1536]{1,0:T(8,128)(2,1)} %fusion.12), channel_id=1, source_target_pairs={{0,4},{2,6},{4,8},{6,10},{8,12},{10,14},{12,16},{14,18},{16,20},{1... | collective-permute-start | bytes 4718600 | tf_op jit(solution)/shard_map/ppermute | solution.py:17
  11.9 70.0 %collective-permute-start.1 = (bf16[512,1536]{1,0:T(8,128)(2,1)}, bf16[512,1536]{1,0:T(8,128)(2,1)}, u32[]{:S(2)}, u32[]{:S(2)}) collective-permute-start(bf16[512,1536]{1,0:T(8,128)(2,1)} %fusion.12), channel_id=1, source_target_pairs={{4,0},{6,2},{8,4},{10,6},{12,8},{14,10},{16,12},{18,14},{20,16},{2... | collective-permute-start | bytes 4718600 | tf_op jit(solution)/shard_map/ppermute | solution.py:17
  81.9 3.9 %copy-start.3 = (bf16[1,512,1536]{2,1,0:T(8,128)(2,1)S(1)}, bf16[1,512,1536]{2,1,0:T(8,128)(2,1)}, u32[]{:S(2)}) copy-start(bf16[1,512,1536]{2,1,0:T(8,128)(2,1)} %param.8) | copy-start | bytes 4718596
  82.0 3.9 %copy-start.5 = (f32[768]{0:T(1024)S(1)}, f32[768]{0:T(1024)}, u32[]{:S(2)}) copy-start(f32[768]{0:T(1024)} %param.12) | copy-start | bytes 9220
  85.8 3.0 %slice-start = ((s8[7077888]{0:T(1024)(128)(4,1)}), s8[4194304]{0:T(1024)(128)(4,1)S(1)}, s32[]{:S(2)}) async-start(s8[7077888]{0:T(1024)(128)(4,1)} %bitcast.116), calls=%async_computation | async-start | bytes 8388608
  85.9 3.1 %slice-start.1 = ((s8[7077888]{0:T(1024)(128)(4,1)}), s8[2883584]{0:T(1024)(128)(4,1)S(1)}, s32[]{:S(2)}) async-start(s8[7077888]{0:T(1024)(128)(4,1)} %bitcast.116), calls=%async_computation.1 | async-start | bytes 5767168
  90.3 7.4 %copy-start.2 = (bf16[1,512,1536]{2,1,0:T(8,128)(2,1)S(1)}, bf16[1,512,1536]{2,1,0:T(8,128)(2,1)}, u32[]{:S(2)}) copy-start(bf16[1,512,1536]{2,1,0:T(8,128)(2,1)} %param.7) | copy-start | bytes 4718596
  91.8 70.9 %collective-permute-start.2 = (bf16[512,1536]{1,0:T(8,128)(2,1)S(1)}, bf16[512,1536]{1,0:T(8,128)(2,1)S(1)}, u32[]{:S(2)}, u32[]{:S(2)}) collective-permute-start(bf16[512,1536]{1,0:T(8,128)(2,1)S(1)} %convolution_convert_fusion.1), channel_id=1, source_target_pairs={{0,4},{2,6},{4,8},{6,10},{8,12},{10,14},{12,16},{14,18},{16,20},{1... | collective-permute-start | bytes 4718600 | tf_op jit(solution)/shard_map/ppermute | solution.py:17
  96.3 66.4 %collective-permute-start.3 = (bf16[512,1536]{1,0:T(8,128)(2,1)S(1)}, bf16[512,1536]{1,0:T(8,128)(2,1)S(1)}, u32[]{:S(2)}, u32[]{:S(2)}) collective-permute-start(bf16[512,1536]{1,0:T(8,128)(2,1)S(1)} %convolution_convert_fusion), channel_id=1, source_target_pairs={{4,0},{6,2},{8,4},{10,6},{12,8},{14,10},{16,12},{18,14},{20,16},{2... | collective-permute-start | bytes 4718600 | tf_op jit(solution)/shard_map/ppermute | solution.py:17
where the time goes:
time: 217 us
  waiting for transfers between devices  123 us (57%)
  blocking collectives  41.6 us (19%)
  matrix products  26.1 us (12%)
  starting transfers between devices  13.2 us (6%)
  other arithmetic  11.9 us (5%)
    ppermute x4, waiting for transfers between devices, shifted(): return lax.ppermute(x, axis, pairs)  123 us
    psum x1, blocking collectives, body(): summed = lax.psum((input_terms, middle_terms), ('seq', 'batch'))  41.6 us
    ppermute x4, starting transfers between devices, shifted(): return lax.ppermute(x, axis, pairs)  13.2 us
    dot_general x1, matrix products, body(): jnp.dot(grad_combined, tap_center.T, preferred_element_type=jnp.float32)  6.12 us
    broadcast_in_dim x1, other arithmetic, body(): grad_output[None]  4.9 us
    dot_general x1, matrix products, body(): combined = jnp.dot(hidden, tap_center, preferred_element_type=jnp.float32)  4.44 us
  transfers between devices with their start and end apart: 4, of which 2 were waited for; matrix products, arithmetic and copies ran while one was open for 5% of the time, Pallas kernels for 0%

commit v1 on v0

--- a/solution.py
+++ b/solution.py
@@ -6,6 +6,7 @@
 from jax.sharding import PartitionSpec as P
 
 SPAN = 2
+REDUCE = "butterfly"
 
 
 epsilon = 1e-06
@@ -25,6 +26,28 @@
 def contig_owner(lengths, positions):
     bounds = jnp.cumsum(lengths)
     return jnp.sum((positions[:, None] >= bounds[None, :]).astype(jnp.int32), axis=1)
+
+
+def reduce_all(x):
+    if REDUCE == "psum_flat":
+        return lax.psum(x, ("seq", "batch"))
+    if REDUCE == "psum_nested":
+        return lax.psum(lax.psum(x, "seq"), "batch")
+    if REDUCE == "scatter_gather":
+        part = lax.psum_scatter(x, ("seq", "batch"), scatter_dimension=0, tiled=True)
+        return lax.all_gather(part, ("seq", "batch"), axis=0, tiled=True)
+    if REDUCE == "gather_sum":
+        return jnp.sum(lax.all_gather(x, ("seq", "batch"), axis=0), axis=0)
+    if REDUCE == "butterfly":
+        for axis in ("seq", "batch"):
+            size = lax.axis_size(axis)
+            step = 1
+            while step < size:
+                pairs = [(i, i ^ step) for i in range(size)]
+                x = x + lax.ppermute(x, axis, pairs)
+                step *= 2
+        return x
+    raise ValueError(REDUCE)
 
 
 def body(
@@ -51,39 +74,43 @@
     tap_after = tap_weights[2]
     normed, input_vjp = jax.vjp(norm_activate, signal.astype(jnp.float32), gain_input)
     hidden = normed.astype(jnp.bfloat16)
-    hidden_before = shifted(hidden, "seq", SPAN)
-    hidden_after = shifted(hidden, "seq", -SPAN)
+    sent_before = jnp.dot(hidden, tap_before, preferred_element_type=jnp.float32)
+    sent_after = jnp.dot(hidden, tap_after, preferred_element_type=jnp.float32)
+    product_before = shifted(sent_before.astype(jnp.bfloat16), "seq", SPAN)
+    product_after = shifted(sent_after.astype(jnp.bfloat16), "seq", -SPAN)
     combined = jnp.dot(hidden, tap_center, preferred_element_type=jnp.float32)
-    combined = combined + before_valid * jnp.dot(
-        hidden_before, tap_before, preferred_element_type=jnp.float32
-    )
-    combined = combined + after_valid * jnp.dot(
-        hidden_after, tap_after, preferred_element_type=jnp.float32
-    )
+    grad_middle = jnp.dot(upstream, point_weights.T, preferred_element_type=jnp.float32)
+    combined = combined + before_valid * product_before.astype(jnp.float32)
+    combined = combined + after_valid * product_after.astype(jnp.float32)
     middle_f, middle_vjp = jax.vjp(norm_activate, combined, gain_middle)
     middle = middle_f.astype(jnp.bfloat16)
+    grad_combined_f, middle_terms = middle_vjp(grad_middle)
+    grad_combined = grad_combined_f.astype(jnp.bfloat16)
+    combined_before = shifted(grad_combined, "seq", SPAN)
+    combined_after = shifted(grad_combined, "seq", -SPAN)
     output = (
         signal.astype(jnp.float32)
         + jnp.dot(middle, point_weights, preferred_element_type=jnp.float32)
     ).astype(jnp.bfloat16)
-    grad_middle = jnp.dot(upstream, point_weights.T, preferred_element_type=jnp.float32)
-    grad_combined_f, middle_terms = middle_vjp(grad_middle)
-    grad_combined = grad_combined_f.astype(jnp.bfloat16)
     grad_hidden = jnp.dot(grad_combined, tap_center.T, preferred_element_type=jnp.float32)
-    forward_terms = jnp.dot(grad_combined, tap_after.T, preferred_element_type=jnp.float32)
-    backward_terms = jnp.dot(grad_combined, tap_before.T, preferred_element_type=jnp.float32)
-    terms_before = shifted(forward_terms.astype(jnp.bfloat16), "seq", SPAN).astype(
-        forward_terms.dtype
+    grad_hidden = grad_hidden + before_valid * jnp.dot(
+        combined_before, tap_after.T, preferred_element_type=jnp.float32
     )
-    terms_after = shifted(backward_terms.astype(jnp.bfloat16), "seq", -SPAN).astype(
-        backward_terms.dtype
+    grad_hidden = grad_hidden + after_valid * jnp.dot(
+        combined_after, tap_before.T, preferred_element_type=jnp.float32
     )
-    grad_hidden = grad_hidden + before_valid * terms_before + after_valid * terms_after
     grad_signal, input_terms = input_vjp(grad_hidden)
     grad_output = (upstream.astype(jnp.float32) + grad_signal).astype(jnp.bfloat16)
-    summed = lax.psum((input_terms, middle_terms), ("seq", "batch"))
+    terms = jnp.concatenate([input_terms, middle_terms])
+    summed = reduce_all(terms)
     factor = 1.0 / math.sqrt(lax.axis_size("batch") * seq_count * shard_rows)
-    return (output[None], grad_output[None], summed[0] * factor, summed[1] * factor)
+    channels = input_terms.shape[0]
+    return (
+        output[None],
+        grad_output[None],
+        summed[:channels] * factor,
+        summed[channels:] * factor,
+    )
 
 
 def solution(mesh):

time: 217 us -> 120 us (0.55)
  waiting for transfers between devices: 123 us -> 61.9 us
  blocking collectives: 41.6 us -> 0 us
  starting transfers between devices: 13.2 us -> 23.1 us
  other arithmetic: 11.9 us -> 5.97 us
    ppermute x4, waiting for transfers between devices: 123 us -> 57 us  [shifted(): return lax.ppermute(x, axis, pairs)]
    psum x1 -> x0, blocking collectives: 41.6 us -> none  [body(): summed = lax.psum((input_terms, middle_terms), ('seq', 'batch'))]
    ppermute x0 -> x5, starting transfers between devices: none -> 10.4 us  [reduce_all(): x = x + lax.ppermute(x, axis, pairs)]
    dot_general x4, matrix products: 10.2 us -> 16 us  [the longest x1 5.44 us: body(): jnp.dot(hidden, tap_before, preferred_element_type=jnp.float32)]
    ppermute x0 -> x5, waiting for transfers between devices: none -> 4.88 us  [reduce_all(): x = x + lax.ppermute(x, axis, pairs)]
    dot_general x1, matrix products: 6.12 us -> 1.41 us  [body(): jnp.dot(grad_combined, tap_center.T, preferred_element_type=jnp.float32)]
    convert_element_type x1 -> x0, other arithmetic: 3.21 us -> none  [body(): hidden = normed.astype(jnp.bfloat16)]
    broadcast_in_dim x1, other arithmetic: 4.9 us -> 2.11 us  [body(): grad_output[None]]
  transfers between devices with their start and end apart: 4 -> 9, of which waited for: 2 -> 7; matrix products, arithmetic and copies ran while one was open for 5% -> 11% of each run, Pallas kernels for 0% -> 0%
where the time goes in v1:
time: 120 us
  waiting for transfers between devices  61.9 us (52%)
  matrix products  27.8 us (23%)
  starting transfers between devices  23.1 us (19%)
  other arithmetic  5.97 us (5%)
    ppermute x4, waiting for transfers between devices, shifted(): return lax.ppermute(x, axis, pairs)  57 us
    ppermute x4, starting transfers between devices, shifted(): return lax.ppermute(x, axis, pairs)  12.7 us
    ppermute x5, starting transfers between devices, reduce_all(): x = x + lax.ppermute(x, axis, pairs)  10.4 us
    dot_general x1, matrix products, body(): jnp.dot(hidden, tap_before, preferred_element_type=jnp.float32)  5.44 us
    dot_general x1, matrix products, body(): combined = jnp.dot(hidden, tap_center, preferred_element_type=jnp.float32)  4.92 us
    ppermute x5, waiting for transfers between devices, reduce_all(): x = x + lax.ppermute(x, axis, pairs)  4.88 us
    dot_general x1, matrix products, body(): sent_after = jnp.dot(hidden, tap_after, preferred_element_type=jnp.float32)  4.86 us
    dot_general x1, matrix products, body(): jnp.dot(combined_before, tap_after.T, preferred_element_type=jnp.float32)  4.32 us
  transfers between devices with their start and end apart: 9, of which 7 were waited for; matrix products, arithmetic and copies ran while one was open for 11% of the time, Pallas kernels for 0%

profile of v1, /device:TPU:0, one launch (start us, length us, event | category | flops | bytes accessed | tf_op | source)
XLA Modules:
  0.0 119.7 jit_solution(6860679687643067313)
XLA Ops:
  0.6 0.0 copy-start
  0.6 1.9 %fusion.16 = f32[512]{0:T(512)S(1)} fusion(bf16[1,512,1536]{2,1,0:T(8,128)(2,1)} %param.7), kind=kLoop, calls=%fused_computation.24 | loop fusion | flops 2358784 | bytes 1574912 | tf_op jit(solution)/shard_map/jvp()/reduce_sum | solution.py:22
  2.6 5.4 %fusion.63 = bf16[512,768]{1,0:T(8,128)(2,1)} fusion(bf16[3,1536,768]{2,1,0:T(8,128)(2,1)} %param.11, bf16[1,512,1536]{2,1,0:T(8,128)(2,1)} %param.7, f32[1536]{0:T(1024)} %param.10, f32[512]{0:T(512)S(1)} %fusion.83), kind=kOutput, calls=%fused_computation.78 | convolution fusion | flops 1217789952 | bytes 4728832 | tf_op jit(solution)/shard_map/dot_general | solution.py:77
  8.1 5.0 %collective-permute-start = (bf16[512,768]{1,0:T(8,128)(2,1)}, bf16[512,768]{1,0:T(8,128)(2,1)S(1)}, u32[]{:S(2)}, u32[]{:S(2)}) collective-permute-start(bf16[512,768]{1,0:T(8,128)(2,1)} %fusion.63), channel_id=1, source_target_pairs={{0,4},{2,6},{4,8},{6,10},{8,12},{10,14},{12,16},{14,18},{16,20},{1... | collective-permute-start | bytes 2359304 | tf_op jit(solution)/shard_map/ppermute | solution.py:18
  13.1 4.9 %fusion.66 = bf16[512,768]{1,0:T(8,128)(2,1)} fusion(bf16[3,1536,768]{2,1,0:T(8,128)(2,1)} %param.11, bf16[1,512,1536]{2,1,0:T(8,128)(2,1)S(1)} %copy-done.1, f32[1536]{0:T(1024)S(1)} %copy-done.4, f32[512]{0:T(512)S(1)} %fusion.83), kind=kOutput, calls=%fused_computation.79 | convolution fusion | flops 1217789952 | bytes 4726784 | tf_op jit(solution)/shard_map/dot_general | solution.py:78
  18.0 1.3 %collective-permute-start.1 = (bf16[512,768]{1,0:T(8,128)(2,1)}, bf16[512,768]{1,0:T(8,128)(2,1)}, u32[]{:S(2)}, u32[]{:S(2)}) collective-permute-start(bf16[512,768]{1,0:T(8,128)(2,1)} %fusion.66), channel_id=1, source_target_pairs={{4,0},{6,2},{8,4},{10,6},{12,8},{14,10},{16,12},{18,14},{20,16},{2... | collective-permute-start | bytes 2359304 | tf_op jit(solution)/shard_map/ppermute | solution.py:18
  19.3 0.2 reduce-window.8
  19.5 0.1 convert_reduce_fusion.2
  19.6 27.4 %collective-permute-done = bf16[512,768]{1,0:T(8,128)(2,1)S(1)} collective-permute-done((bf16[512,768]{1,0:T(8,128)(2,1)}, bf16[512,768]{1,0:T(8,128)(2,1)S(1)}, u32[]{:S(2)}, u32[]{:S(2)}) %collective-permute-start) | collective-permute-done | bytes 786464 | tf_op jit(solution)/shard_map/ppermute | solution.py:18
  47.0 4.9 %multiply_reduce_fusion.2 = (f32[512]{0:T(512)S(1)}, f32[512,768]{1,0:T(8,128)S(1)}) fusion(bf16[512,768]{1,0:T(8,128)(2,1)} %collective-permute-done.1, f32[512]{0:T(512)S(1)} %get-tuple-element.12, bf16[512,768]{1,0:T(8,128)(2,1)S(1)} %collective-permute-done, f32[512]{0:T(512)S(1)} %get-tuple-element.11, bf16[3,1536,768]{2,1,0:T(8,128)(2,1)} %param.11, ...), kind=kOutput, calls=%fused_computation.75 | convolution fusion | flops 1220541952 | bytes 7092224 | tf_op jit(solution)/shard_map/dot_general | solution.py:81
  52.0 2.6 %multiply_reduce_fusion = (f32[768]{0:T(1024)S(1)}, f32[512]{0:T(512)S(1)}, f32[512,768]{1,0:T(8,128)S(1)}) fusion(f32[512,768]{1,0:T(8,128)S(1)} %get-tuple-element.14, f32[512]{0:T(512)S(1)} %fusion.84, f32[768]{0:T(1024)S(1)} %copy-done.5, bf16[768,1536]{1,0:T(8,128)(2,1)S(1)} %copy-done, bf16[1,512,1536]{2,1,0:T(8,128)(2,1)S(1)} %copy-done.3), kind=kOutput, calls=%fused_computation.72 | convolution fusion | flops 1218181888 | bytes 7088128 | tf_op jit(solution)/shard_map/dot_general | solution.py:82
  54.6 0.4 fusion.56
  54.9 1.3 %collective-permute-start.3 = (bf16[512,768]{1,0:T(8,128)(2,1)S(1)}, bf16[512,768]{1,0:T(8,128)(2,1)S(1)}, u32[]{:S(2)}, u32[]{:S(2)}) collective-permute-start(bf16[512,768]{1,0:T(8,128)(2,1)S(1)} %fusion.56), channel_id=1, source_target_pairs={{4,0},{6,2},{8,4},{10,6},{12,8},{14,10},{16,12},{18,14},{20,16},{2... | collective-permute-start | bytes 2359304 | tf_op jit(solution)/shard_map/ppermute | solution.py:18
  56.2 5.1 %collective-permute-start.2 = (bf16[512,768]{1,0:T(8,128)(2,1)S(1)}, bf16[512,768]{1,0:T(8,128)(2,1)S(1)}, u32[]{:S(2)}, u32[]{:S(2)}) collective-permute-start(bf16[512,768]{1,0:T(8,128)(2,1)S(1)} %fusion.56), channel_id=1, source_target_pairs={{0,4},{2,6},{4,8},{6,10},{8,12},{10,14},{12,16},{14,18},{16,20},{1... | collective-permute-start | bytes 2359304 | tf_op jit(solution)/shard_map/ppermute | solution.py:18
  61.4 1.4 %fusion.40 = f32[512,1536]{1,0:T(8,128)S(1)} fusion(bf16[512,768]{1,0:T(8,128)(2,1)S(1)} %fusion.56, bf16[3,1536,768]{2,1,0:T(8,128)(2,1)S(1)} %bitcast.117), kind=kOutput, calls=%fused_computation.49 | convolution fusion | flops 1207959552 | bytes 6291456 | tf_op jit(solution)/shard_map/dot_general | solution.py:95
  62.8 13.0 %collective-permute-done.3 = bf16[512,768]{1,0:T(8,128)(2,1)S(1)} collective-permute-done((bf16[512,768]{1,0:T(8,128)(2,1)S(1)}, bf16[512,768]{1,0:T(8,128)(2,1)S(1)}, u32[]{:S(2)}, u32[]{:S(2)}) %collective-permute-start.3) | collective-permute-done | bytes 786464 | tf_op jit(solution)/shard_map/ppermute | solution.py:18
  75.9 1.4 %convolution_multiply_fusion = f32[512,1536]{1,0:T(8,128)S(1)} fusion(bf16[512,768]{1,0:T(8,128)(2,1)S(1)} %collective-permute-done.3, bf16[3,1536,768]{2,1,0:T(8,128)(2,1)S(1)} %bitcast.117, f32[512]{0:T(512)S(1)} %get-tuple-element.12), kind=kOutput, calls=%fused_computation.15 | convolution fusion | flops 1208745984 | bytes 6293504 | tf_op jit(solution)/shard_map/dot_general | solution.py:99
  77.3 16.5 %collective-permute-done.2 = bf16[512,768]{1,0:T(8,128)(2,1)S(1)} collective-permute-done((bf16[512,768]{1,0:T(8,128)(2,1)S(1)}, bf16[512,768]{1,0:T(8,128)(2,1)S(1)}, u32[]{:S(2)}, u32[]{:S(2)}) %collective-permute-start.2) | collective-permute-done | bytes 786464 | tf_op jit(solution)/shard_map/ppermute | solution.py:18
  93.9 4.3 %fusion.15 = (f32[1536]{0:T(1024)S(1)}, f32[512]{0:T(512)S(1)}, f32[512,1536]{1,0:T(8,128)S(1)}) fusion(bf16[1,512,1536]{2,1,0:T(8,128)(2,1)S(1)} %copy-done.2, f32[512]{0:T(512)S(1)} %fusion.83, f32[1536]{0:T(1024)S(1)} %copy-done.4, f32[512,1536]{1,0:T(8,128)S(1)} %convolution_multiply_fusion, f32[512,1536]{1,0:T(8,128)S(1)} %fusion.40, ...), kind=kOutput, calls=%fused_computation.23 | convolution fusion | flops 1231550464 | bytes 14176256 | tf_op jit(solution)/shard_map/dot_general | solution.py:96
  98.2 0.1 collective-permute-start.4
  98.3 1.2 collective-permute-done.4
  99.4 2.5 %collective-permute-start.5 = (f32[2304]{0:T(1024)S(1)}, f32[2304]{0:T(1024)S(1)}, u32[]{:S(2)}, u32[]{:S(2)}) collective-permute-start(f32[2304]{0:T(1024)S(1)} %fusion.89), channel_id=1, source_target_pairs={{0,4},{2,6},{4,0},{6,2},{8,12},{10,14},{12,8},{14,10},{16,20},{18,... | collective-permute-start | bytes 27656 | tf_op jit(solution)/shard_map/ppermute | solution.py:47
  101.9 1.7 %collective-permute-done.5 = f32[2304]{0:T(1024)S(1)} collective-permute-done((f32[2304]{0:T(1024)S(1)}, f32[2304]{0:T(1024)S(1)}, u32[]{:S(2)}, u32[]{:S(2)}) %collective-permute-start.5) | collective-permute-done | bytes 9248 | tf_op jit(solution)/shard_map/ppermute | solution.py:47
  103.6 3.7 %collective-permute-start.6 = (f32[2304]{0:T(1024)S(1)}, f32[2304]{0:T(1024)S(1)}, u32[]{:S(2)}, u32[]{:S(2)}) collective-permute-start(f32[2304]{0:T(1024)S(1)} %add.129), channel_id=1, source_target_pairs={{0,8},{2,10},{4,12},{6,14},{8,0},{10,2},{12,4},{14,6},{16,24},{18,... | collective-permute-start | bytes 27656 | tf_op jit(solution)/shard_map/ppermute | solution.py:47
  107.3 2.8 %fusion.33 = bf16[1,512,1536]{2,1,0:T(8,128)(2,1)} fusion(bf16[768,1536]{1,0:T(8,128)(2,1)S(1)} %copy-done, bf16[1,512,1536]{2,1,0:T(8,128)(2,1)S(1)} %copy-done.2, f32[512,768]{1,0:T(8,128)S(1)} %get-tuple-element.14, f32[768]{0:T(1024)S(1)} %copy-done.5, f32[512]{0:T(512)S(1)} %fusion.84), kind=kOutput, calls=%fused_computation.41 | convolution fusion | flops 1214644224 | bytes 7083008 | tf_op jit(solution)/shard_map/dot_general | solution.py:93
  110.2 2.6 %collective-permute-start.7 = (f32[2304]{0:T(1024)S(1)}, f32[2304]{0:T(1024)S(1)}, u32[]{:S(2)}, u32[]{:S(2)}) collective-permute-start(f32[2304]{0:T(1024)S(1)} %add.130), channel_id=1, source_target_pairs={{0,16},{2,18},{4,20},{6,22},{8,24},{10,26},{12,28},{14,30},{16,0},... | collective-permute-start | bytes 27656 | tf_op jit(solution)/shard_map/ppermute | solution.py:47
  112.8 2.0 %collective-permute-done.7 = f32[2304]{0:T(1024)S(1)} collective-permute-done((f32[2304]{0:T(1024)S(1)}, f32[2304]{0:T(1024)S(1)}, u32[]{:S(2)}, u32[]{:S(2)}) %collective-permute-start.7) | collective-permute-done | bytes 9248 | tf_op jit(solution)/shard_map/ppermute | solution.py:47
  114.8 1.5 %collective-permute-start.8 = (f32[2304]{0:T(1024)S(1)}, f32[2304]{0:T(1024)S(1)}, u32[]{:S(2)}, u32[]{:S(2)}) collective-permute-start(f32[2304]{0:T(1024)S(1)} %add.131), channel_id=1, source_target_pairs={{0,1},{1,0},{2,3},{3,2},{4,5},{5,4},{6,7},{7,6},{8,9},{9,8},{10,11... | collective-permute-start | bytes 27656 | tf_op jit(solution)/shard_map/ppermute | solution.py:47
  116.3 2.1 %fusion.57 = bf16[1,512,1536]{2,1,0:T(8,128)(2,1)} fusion(bf16[1,512,1536]{2,1,0:T(8,128)(2,1)S(1)} %copy-done.2, f32[512,1536]{1,0:T(8,128)S(1)} %get-tuple-element.16, bf16[1,512,1536]{2,1,0:T(8,128)(2,1)S(1)} %copy-done.3, f32[512]{0:T(512)S(1)} %multiply_multiply_fusion.6, f32[1536]{0:T(1024)S(1)} %copy-done.4, f32[512]{0:T(512)S(1)} %fusion.83), kind=kLoop, calls=%fused_computation.68 | loop fusion | flops 7077888 | bytes 7874560 | tf_op jit(solution)/shard_map/broadcast_in_dim | solution.py:110
  118.4 0.1 collective-permute-done.8
  118.5 0.6 slice_multiply_fusion.1
  119.1 0.6 slice_multiply_fusion
  (33 shorter events, 0.1 us)
Async XLA Ops:
  0.6 51.3 %copy-start = (bf16[768,1536]{1,0:T(8,128)(2,1)S(1)}, bf16[768,1536]{1,0:T(8,128)(2,1)}, u32[]{:S(2)}) copy-start(bf16[768,1536]{1,0:T(8,128)(2,1)} %param.13) | copy-start | bytes 7077892
  2.6 10.5 %copy-start.1 = (bf16[1,512,1536]{2,1,0:T(8,128)(2,1)S(1)}, bf16[1,512,1536]{2,1,0:T(8,128)(2,1)}, u32[]{:S(2)}) copy-start(bf16[1,512,1536]{2,1,0:T(8,128)(2,1)} %param.7) | copy-start | bytes 4718596
  2.6 10.5 %copy-start.4 = (f32[1536]{0:T(1024)S(1)}, f32[1536]{0:T(1024)}, u32[]{:S(2)}) copy-start(f32[1536]{0:T(1024)} %param.10) | copy-start | bytes 18436
  8.1 11.2 %copy-start.6 = (s32[1,4]{1,0:T(1,128)S(1)}, s32[1,4]{1,0:T(1,128)}, u32[]{:S(2)}) copy-start(s32[1,4]{1,0:T(1,128)} %param.9) | copy-start | bytes 52
  8.1 38.9 %collective-permute-start = (bf16[512,768]{1,0:T(8,128)(2,1)}, bf16[512,768]{1,0:T(8,128)(2,1)S(1)}, u32[]{:S(2)}, u32[]{:S(2)}) collective-permute-start(bf16[512,768]{1,0:T(8,128)(2,1)} %fusion.63), channel_id=1, source_target_pairs={{0,4},{2,6},{4,8},{6,10},{8,12},{10,14},{12,16},{14,18},{16,20},{1... | collective-permute-start | bytes 2359304 | tf_op jit(solution)/shard_map/ppermute | solution.py:18
  18.0 29.0 %collective-permute-start.1 = (bf16[512,768]{1,0:T(8,128)(2,1)}, bf16[512,768]{1,0:T(8,128)(2,1)}, u32[]{:S(2)}, u32[]{:S(2)}) collective-permute-start(bf16[512,768]{1,0:T(8,128)(2,1)} %fusion.66), channel_id=1, source_target_pairs={{4,0},{6,2},{8,4},{10,6},{12,8},{14,10},{16,12},{18,14},{20,16},{2... | collective-permute-start | bytes 2359304 | tf_op jit(solution)/shard_map/ppermute | solution.py:18
  47.0 5.0 %copy-start.3 = (bf16[1,512,1536]{2,1,0:T(8,128)(2,1)S(1)}, bf16[1,512,1536]{2,1,0:T(8,128)(2,1)}, u32[]{:S(2)}) copy-start(bf16[1,512,1536]{2,1,0:T(8,128)(2,1)} %param.8) | copy-start | bytes 4718596
  47.0 5.0 %copy-start.5 = (f32[768]{0:T(1024)S(1)}, f32[768]{0:T(1024)}, u32[]{:S(2)}) copy-start(f32[768]{0:T(1024)} %param.12) | copy-start | bytes 9220
  51.9 9.5 %slice-start = ((s8[7077888]{0:T(1024)(128)(4,1)}), s8[4194304]{0:T(1024)(128)(4,1)S(1)}, s32[]{:S(2)}) async-start(s8[7077888]{0:T(1024)(128)(4,1)} %bitcast.116), calls=%async_computation | async-start | bytes 8388608
  52.0 9.4 %slice-start.1 = ((s8[7077888]{0:T(1024)(128)(4,1)}), s8[2883584]{0:T(1024)(128)(4,1)S(1)}, s32[]{:S(2)}) async-start(s8[7077888]{0:T(1024)(128)(4,1)} %bitcast.116), calls=%async_computation.1 | async-start | bytes 5767168
  54.9 21.0 %collective-permute-start.3 = (bf16[512,768]{1,0:T(8,128)(2,1)S(1)}, bf16[512,768]{1,0:T(8,128)(2,1)S(1)}, u32[]{:S(2)}, u32[]{:S(2)}) collective-permute-start(bf16[512,768]{1,0:T(8,128)(2,1)S(1)} %fusion.56), channel_id=1, source_target_pairs={{4,0},{6,2},{8,4},{10,6},{12,8},{14,10},{16,12},{18,14},{20,16},{2... | collective-permute-start | bytes 2359304 | tf_op jit(solution)/shard_map/ppermute | solution.py:18
  56.2 37.6 %collective-permute-start.2 = (bf16[512,768]{1,0:T(8,128)(2,1)S(1)}, bf16[512,768]{1,0:T(8,128)(2,1)S(1)}, u32[]{:S(2)}, u32[]{:S(2)}) collective-permute-start(bf16[512,768]{1,0:T(8,128)(2,1)S(1)} %fusion.56), channel_id=1, source_target_pairs={{0,4},{2,6},{4,8},{6,10},{8,12},{10,14},{12,16},{14,18},{16,20},{1... | collective-permute-start | bytes 2359304 | tf_op jit(solution)/shard_map/ppermute | solution.py:18
  62.8 31.0 %copy-start.2 = (bf16[1,512,1536]{2,1,0:T(8,128)(2,1)S(1)}, bf16[1,512,1536]{2,1,0:T(8,128)(2,1)}, u32[]{:S(2)}) copy-start(bf16[1,512,1536]{2,1,0:T(8,128)(2,1)} %param.7) | copy-start | bytes 4718596
  98.2 1.2 %collective-permute-start.4 = (f32[2304]{0:T(1024)S(1)}, f32[2304]{0:T(1024)S(1)}, u32[]{:S(2)}, u32[]{:S(2)}) collective-permute-start(f32[2304]{0:T(1024)S(1)} %pad_maximum_fusion), channel_id=1, source_target_pairs={{0,2},{2,0},{4,6},{6,4},{8,10},{10,8},{12,14},{14,12},{16,18},{18,... | collective-permute-start | bytes 27656 | tf_op jit(solution)/shard_map/ppermute | solution.py:47
  99.4 4.2 %collective-permute-start.5 = (f32[2304]{0:T(1024)S(1)}, f32[2304]{0:T(1024)S(1)}, u32[]{:S(2)}, u32[]{:S(2)}) collective-permute-start(f32[2304]{0:T(1024)S(1)} %fusion.89), channel_id=1, source_target_pairs={{0,4},{2,6},{4,0},{6,2},{8,12},{10,14},{12,8},{14,10},{16,20},{18,... | collective-permute-start | bytes 27656 | tf_op jit(solution)/shard_map/ppermute | solution.py:47
  103.6 6.6 %collective-permute-start.6 = (f32[2304]{0:T(1024)S(1)}, f32[2304]{0:T(1024)S(1)}, u32[]{:S(2)}, u32[]{:S(2)}) collective-permute-start(f32[2304]{0:T(1024)S(1)} %add.129), channel_id=1, source_target_pairs={{0,8},{2,10},{4,12},{6,14},{8,0},{10,2},{12,4},{14,6},{16,24},{18,... | collective-permute-start | bytes 27656 | tf_op jit(solution)/shard_map/ppermute | solution.py:47
  110.2 4.6 %collective-permute-start.7 = (f32[2304]{0:T(1024)S(1)}, f32[2304]{0:T(1024)S(1)}, u32[]{:S(2)}, u32[]{:S(2)}) collective-permute-start(f32[2304]{0:T(1024)S(1)} %add.130), channel_id=1, source_target_pairs={{0,16},{2,18},{4,20},{6,22},{8,24},{10,26},{12,28},{14,30},{16,0},... | collective-permute-start | bytes 27656 | tf_op jit(solution)/shard_map/ppermute | solution.py:47
  114.8 3.7 %collective-permute-start.8 = (f32[2304]{0:T(1024)S(1)}, f32[2304]{0:T(1024)S(1)}, u32[]{:S(2)}, u32[]{:S(2)}) collective-permute-start(f32[2304]{0:T(1024)S(1)} %add.131), channel_id=1, source_target_pairs={{0,1},{1,0},{2,3},{3,2},{4,5},{5,4},{6,7},{7,6},{8,9},{9,8},{10,11... | collective-permute-start | bytes 27656 | tf_op jit(solution)/shard_map/ppermute | solution.py:47

commit v2 on v0

v2 whole, which is shorter than its diff:
```python
import math

import jax
import jax.numpy as jnp
from jax import lax
from jax.sharding import PartitionSpec as P

SPAN = 2
CHUNKS = 2
RADIX = 4


epsilon = 1e-06


def shifted(x, axis, by):
    peers = lax.axis_size(axis)
    pairs = [(i, i + by) for i in range(peers) if 0 <= i + by < peers]
    return lax.ppermute(x, axis, pairs)


def norm_activate(values, scales):
    mean_square = jnp.mean(values * values, axis=-1, keepdims=True)
    return jax.nn.gelu(values * lax.rsqrt(mean_square + epsilon) * scales, approximate=True)


def contig_owner(lengths, positions):
    bounds = jnp.cumsum(lengths)
    return jnp.sum((positions[:, None] >= bounds[None, :]).astype(jnp.int32), axis=1)


def group_sum(x, axis, stride, radix):
    size = lax.axis_size(axis)
    parts = [x]
    for step in range(1, radix):
        pairs = [(i, i ^ (step * stride)) for i in range(size)]
        parts.append(lax.ppermute(x, axis, pairs))
    while len(parts) > 1:
        parts = [parts[k] + parts[k + 1] for k in range(0, len(parts), 2)]
    return parts[0]


def reduce_all(x):
    axes = ("seq", "batch")
    sizes = [lax.axis_size(a) for a in axes]
    if any(s & (s - 1) for s in sizes):
        return lax.psum(x, axes)
    for axis, size in zip(axes, sizes):
        stride = 1
        while stride < size:
            radix = min(RADIX, size // stride)
            x = group_sum(x, axis, stride, radix)
            stride *= radix
    return x


def body(
    activations, cotangent, contig_lengths, gain_input, tap_weights, gain_middle, point_weights
):
    lengths = contig_lengths[0]
    shard_rows = activations.shape[1]
    seq_count = lax.axis_size("seq")
    tap_reach = SPAN * shard_rows
    total_length = shard_rows * seq_count
    tap_before = tap_weights[0]
    tap_center = tap_weights[1]
    tap_after = tap_weights[2]
    rows = shard_rows // CHUNKS
    first_row = lax.axis_index("seq") * shard_rows

    chunks = []
    for c in range(CHUNKS):
        signal = activations[0, c * rows:(c + 1) * rows]
        upstream = cotangent[0, c * rows:(c + 1) * rows]
        positions = first_row + c * rows + jnp.arange(rows, dtype=jnp.int32)
        owners = contig_owner(lengths, positions)
        before_valid = (
            (positions >= tap_reach) & (contig_owner(lengths, positions - tap_reach) == owners)
        ).astype(jnp.float32)[:, None]
        after_valid = (
            (positions < total_length - tap_reach)
            & (contig_owner(lengths, positions + tap_reach) == owners)
        ).astype(jnp.float32)[:, None]
        normed, input_vjp = jax.vjp(norm_activate, signal.astype(jnp.float32), gain_input)
        hidden = normed.astype(jnp.bfloat16)
        sent_before = jnp.dot(hidden, tap_before, preferred_element_type=jnp.float32)
        sent_after = jnp.dot(hidden, tap_after, preferred_element_type=jnp.float32)
        chunks.append(dict(
            signal=signal, upstream=upstream, before_valid=before_valid,
            after_valid=after_valid, hidden=hidden, input_vjp=input_vjp,
            product_before=shifted(sent_before.astype(jnp.bfloat16), "seq", SPAN),
            product_after=shifted(sent_after.astype(jnp.bfloat16), "seq", -SPAN),
        ))
    for ch in chunks:
        combined = jnp.dot(ch["hidden"], tap_center, preferred_element_type=jnp.float32)
        grad_middle = jnp.dot(ch["upstream"], point_weights.T, preferred_element_type=jnp.float32)
        combined = combined + ch["before_valid"] * ch["product_before"].astype(jnp.float32)
        combined = combined + ch["after_valid"] * ch["product_after"].astype(jnp.float32)
        middle_f, middle_vjp = jax.vjp(norm_activate, combined, gain_middle)
        ch["middle"] = middle_f.astype(jnp.bfloat16)
        grad_combined_f, ch["middle_terms"] = middle_vjp(grad_middle)
        grad_combined = grad_combined_f.astype(jnp.bfloat16)
        ch["grad_combined"] = grad_combined
        ch["combined_before"] = shifted(grad_combined, "seq", SPAN)
        ch["combined_after"] = shifted(grad_combined, "seq", -SPAN)
    outputs, grads = [], []
    input_terms, middle_terms = None, None
    for ch in chunks:
        outputs.append((
            ch["signal"].astype(jnp.float32)
            + jnp.dot(ch["middle"], point_weights, preferred_element_type=jnp.float32)
        ).astype(jnp.bfloat16))
        grad_hidden = jnp.dot(ch["grad_combined"], tap_center.T, preferred_element_type=jnp.float32)
        grad_hidden = grad_hidden + ch["before_valid"] * jnp.dot(
            ch["combined_before"], tap_after.T, preferred_element_type=jnp.float32
        )
        grad_hidden = grad_hidden + ch["after_valid"] * jnp.dot(
            ch["combined_after"], tap_before.T, preferred_element_type=jnp.float32
        )
        grad_signal, terms = ch["input_vjp"](grad_hidden)
        grads.append((ch["upstream"].astype(jnp.float32) + grad_signal).astype(jnp.bfloat16))
        input_terms = terms if input_terms is None else input_terms + terms
        middle_terms = ch["middle_terms"] if middle_terms is None else middle_terms + ch["middle_terms"]
    summed = reduce_all(jnp.concatenate([input_terms, middle_terms]))
    factor = 1.0 / math.sqrt(lax.axis_size("batch") * seq_count * shard_rows)
    channels = input_terms.shape[0]
    return (
        jnp.concatenate(outputs)[None],
        jnp.concatenate(grads)[None],
        summed[:channels] * factor,
        summed[channels:] * factor,
    )


def solution(mesh):
    placed = (
        P("batch", "seq", None),
        P("batch", "seq", None),
        P("batch", None),
        P(),
        P(),
        P(),
        P(),
    )
    return jax.shard_map(
        body,
        mesh=mesh,
        in_specs=placed,
        out_specs=(P("batch", "seq", None), P("batch", "seq", None), P(), P()),
        check_vma=False,
    )
```

time: 217 us -> 118 us (0.54)
  waiting for transfers between devices: 123 us -> 45 us
  blocking collectives: 41.6 us -> 0 us
  starting transfers between devices: 13.2 us -> 34.9 us
  other arithmetic: 11.9 us -> 7.31 us
  matrix products: 26.1 us -> 28.4 us
    ppermute x4 -> x8, waiting for transfers between devices: 123 us -> 39.7 us  [shifted(): return lax.ppermute(x, axis, pairs)]
    psum x1 -> x0, blocking collectives: 41.6 us -> none  [body(): summed = lax.psum((input_terms, middle_terms), ('seq', 'batch'))]
    ppermute x4 -> x8, starting transfers between devices: 13.2 us -> 26.1 us  [shifted(): return lax.ppermute(x, axis, pairs)]
    ppermute x0 -> x7, starting transfers between devices: none -> 8.72 us  [group_sum(): parts.append(lax.ppermute(x, axis, pairs))]
    ppermute x0 -> x7, waiting for transfers between devices: none -> 5.27 us  [group_sum(): parts.append(lax.ppermute(x, axis, pairs))]
    broadcast_in_dim x1 -> x2, other arithmetic: 4.9 us -> 2.49 us  [the longest x1 1.25 us: body(): jnp.concatenate(outputs)[None]]
    dot_general x8 -> x16, matrix products: 26.1 us -> 28.4 us  [the longest x2 6.5 us: body(): jnp.dot(ch['hidden'], tap_center, preferred_element_type=jnp.float32)]
    convert_element_type x1, other arithmetic: 3.21 us -> 0.93 us  [body(): (ch['upstream'].astype(jnp.float32) + grad_signal).astype(jnp.bfloat16)]
  transfers between devices with their start and end apart: 4 -> 15, of which waited for: 2 -> 8; matrix products, arithmetic and copies ran while one was open for 5% -> 16% of each run, Pallas kernels for 0% -> 0%
where the time goes in v2:
time: 118 us; the launch traced here: 117 us
  waiting for transfers between devices  45 us (38%)
  starting transfers between devices  34.9 us (30%)
  matrix products  28.4 us (24%)
  other arithmetic  7.31 us (6%)
    ppermute x8, waiting for transfers between devices, shifted(): return lax.ppermute(x, axis, pairs)  39.7 us
    ppermute x8, starting transfers between devices, shifted(): return lax.ppermute(x, axis, pairs)  26.1 us
    ppermute x7, starting transfers between devices, group_sum(): parts.append(lax.ppermute(x, axis, pairs))  8.72 us
    dot_general x2, matrix products, body(): jnp.dot(ch['hidden'], tap_center, preferred_element_type=jnp.float32)  6.5 us
    dot_general x2, matrix products, body(): sent_after = jnp.dot(hidden, tap_after, preferred_element_type=jnp.float32)  5.84 us
    ppermute x7, waiting for transfers between devices, group_sum(): parts.append(lax.ppermute(x, axis, pairs))  5.27 us
    dot_general x2, matrix products, body(): jnp.dot(ch['combined_after'], tap_before.T, preferred_element_type=jnp.fl...  4.19 us
    dot_general x2, matrix products, body(): jnp.dot(hidden, tap_before, preferred_element_type=jnp.float32)  4.02 us
  transfers between devices with their start and end apart: 15, of which 8 were waited for; matrix products, arithmetic and copies ran while one was open for 16% of the time, Pallas kernels for 0%

profile of v2, /device:TPU:0, one launch (start us, length us, event | category | flops | bytes accessed | tf_op | source)
XLA Modules:
  0.0 117.2 jit_solution(13030217046848133924)
XLA Ops:
  0.7 1.9 %fusion.52 = (f32[256]{0:T(256)S(1)}, f32[256]{0:T(256)S(1)}) fusion(bf16[1,512,1536]{2,1,0:T(8,128)(2,1)} %param.7), kind=kLoop, calls=%fused_computation.70 | loop fusion | flops 2358784 | bytes 1574912 | tf_op jit(solution)/shard_map/jvp()/reduce_sum | solution.py:23
  2.7 3.8 %fusion.109 = bf16[256,768]{1,0:T(8,128)(2,1)} fusion(bf16[3,1536,768]{2,1,0:T(8,128)(2,1)} %param.11, f32[256]{0:T(256)S(1)} %fusion.156, f32[1536]{0:T(1024)} %param.10, bf16[1,512,1536]{2,1,0:T(8,128)(2,1)S(1)} %copy-done.1), kind=kOutput, calls=%fused_computation.119 | convolution fusion | flops 608894976 | bytes 3548160 | tf_op jit(solution)/shard_map/dot_general | solution.py:87
  6.5 1.3 %collective-permute-start.3 = (bf16[256,768]{1,0:T(8,128)(2,1)}, bf16[256,768]{1,0:T(8,128)(2,1)S(1)}, u32[]{:S(2)}, u32[]{:S(2)}) collective-permute-start(bf16[256,768]{1,0:T(8,128)(2,1)} %fusion.109), channel_id=1, source_target_pairs={{4,0},{6,2},{8,4},{10,6},{12,8},{14,10},{16,12},{18,14},{20,16},{2... | collective-permute-start | bytes 1179656 | tf_op jit(solution)/shard_map/ppermute | solution.py:19
  7.8 2.0 %fusion.103 = bf16[256,768]{1,0:T(8,128)(2,1)} fusion(bf16[3,1536,768]{2,1,0:T(8,128)(2,1)S(1)} %copy-done.3, f32[256]{0:T(256)S(1)} %fusion.156, f32[1536]{0:T(1024)S(1)} %copy-done.5, bf16[1,512,1536]{2,1,0:T(8,128)(2,1)S(1)} %copy-done.1), kind=kOutput, calls=%fused_computation.117 | convolution fusion | flops 608894976 | bytes 3548160 | tf_op jit(solution)/shard_map/dot_general | solution.py:86
  9.8 6.2 %collective-permute-start.2 = (bf16[256,768]{1,0:T(8,128)(2,1)}, bf16[256,768]{1,0:T(8,128)(2,1)}, u32[]{:S(2)}, u32[]{:S(2)}) collective-permute-start(bf16[256,768]{1,0:T(8,128)(2,1)} %fusion.103), channel_id=1, source_target_pairs={{0,4},{2,6},{4,8},{6,10},{8,12},{10,14},{12,16},{14,18},{16,20},{1... | collective-permute-start | bytes 1179656 | tf_op jit(solution)/shard_map/ppermute | solution.py:19
  16.0 2.0 %fusion.100 = bf16[256,768]{1,0:T(8,128)(2,1)} fusion(bf16[3,1536,768]{2,1,0:T(8,128)(2,1)S(1)} %copy-done.3, f32[1536]{0:T(1024)S(1)} %copy-done.5, f32[256]{0:T(256)S(1)} %fusion.154, bf16[1,512,1536]{2,1,0:T(8,128)(2,1)S(1)} %copy-done.1), kind=kOutput, calls=%fused_computation.116 | convolution fusion | flops 608894976 | bytes 3548160 | tf_op jit(solution)/shard_map/dot_general | solution.py:86
  18.1 4.2 %collective-permute-start = (bf16[256,768]{1,0:T(8,128)(2,1)}, bf16[256,768]{1,0:T(8,128)(2,1)S(1)}, u32[]{:S(2)}, u32[]{:S(2)}) collective-permute-start(bf16[256,768]{1,0:T(8,128)(2,1)} %fusion.100), channel_id=1, source_target_pairs={{0,4},{2,6},{4,8},{6,10},{8,12},{10,14},{12,16},{14,18},{16,20},{1... | collective-permute-start | bytes 1179656 | tf_op jit(solution)/shard_map/ppermute | solution.py:19
  22.3 2.0 %fusion.106 = bf16[256,768]{1,0:T(8,128)(2,1)} fusion(bf16[3,1536,768]{2,1,0:T(8,128)(2,1)S(1)} %copy-done.3, f32[1536]{0:T(1024)S(1)} %copy-done.5, f32[256]{0:T(256)S(1)} %fusion.154, bf16[1,512,1536]{2,1,0:T(8,128)(2,1)S(1)} %copy-done.1), kind=kOutput, calls=%fused_computation.118 | convolution fusion | flops 608894976 | bytes 3548160 | tf_op jit(solution)/shard_map/dot_general | solution.py:87
  24.3 1.3 %collective-permute-start.1 = (bf16[256,768]{1,0:T(8,128)(2,1)}, bf16[256,768]{1,0:T(8,128)(2,1)}, u32[]{:S(2)}, u32[]{:S(2)}) collective-permute-start(bf16[256,768]{1,0:T(8,128)(2,1)} %fusion.106), channel_id=1, source_target_pairs={{4,0},{6,2},{8,4},{10,6},{12,8},{14,10},{16,12},{18,14},{20,16},{2... | collective-permute-start | bytes 1179656 | tf_op jit(solution)/shard_map/ppermute | solution.py:19
  26.0 11.9 %collective-permute-done.2 = bf16[256,768]{1,0:T(8,128)(2,1)} collective-permute-done((bf16[256,768]{1,0:T(8,128)(2,1)}, bf16[256,768]{1,0:T(8,128)(2,1)}, u32[]{:S(2)}, u32[]{:S(2)}) %collective-permute-start.2) | collective-permute-done | bytes 393248 | tf_op jit(solution)/shard_map/ppermute | solution.py:19
  37.9 3.4 %multiply_reduce_fusion.4 = (f32[256]{0:T(256)S(1)}, f32[256,768]{1,0:T(8,128)S(1)}) fusion(bf16[256,768]{1,0:T(8,128)(2,1)S(1)} %collective-permute-done.3, f32[256]{0:T(256)S(1)} %get-tuple-element.31, bf16[256,768]{1,0:T(8,128)(2,1)} %collective-permute-done.2, f32[256]{0:T(256)S(1)} %get-tuple-element.30, bf16[3,1536,768]{2,1,0:T(8,128)(2,1)} %param.11, ...), kind=kOutput, calls=%fused_computation.151 | convolution fusion | flops 610270976 | bytes 4728832 | tf_op jit(solution)/shard_map/dot_general | solution.py:95
  41.3 4.9 %collective-permute-done = bf16[256,768]{1,0:T(8,128)(2,1)S(1)} collective-permute-done((bf16[256,768]{1,0:T(8,128)(2,1)}, bf16[256,768]{1,0:T(8,128)(2,1)S(1)}, u32[]{:S(2)}, u32[]{:S(2)}) %collective-permute-start) | collective-permute-done | bytes 393248 | tf_op jit(solution)/shard_map/ppermute | solution.py:19
  46.2 3.1 %multiply_reduce_fusion.5 = (f32[256]{0:T(256)S(1)}, f32[256,768]{1,0:T(8,128)S(1)}) fusion(bf16[256,768]{1,0:T(8,128)(2,1)} %collective-permute-done.1, f32[256]{0:T(256)S(1)} %get-tuple-element.29, bf16[256,768]{1,0:T(8,128)(2,1)S(1)} %collective-permute-done, f32[256]{0:T(256)S(1)} %get-tuple-element.28, bf16[3,1536,768]{2,1,0:T(8,128)(2,1)} %param.11, ...), kind=kOutput, calls=%fused_computation.154 | convolution fusion | flops 610270976 | bytes 4730880 | tf_op jit(solution)/shard_map/dot_general | solution.py:95
  49.3 1.0 fusion.5
  50.7 1.1 fusion.123
  52.9 1.5 %multiply_reduce_fusion.1 = (f32[768]{0:T(1024)S(1)}, f32[256]{0:T(256)S(1)}, f32[256]{0:T(256)S(1)}, f32[768]{0:T(1024)S(1)}, f32[256,768]{1,0:T(8,128)S(1)}) fusion(f32[256,768]{1,0:T(8,128)S(1)} %get-tuple-element.35, f32[256]{0:T(256)S(1)} %fusion.155, f32[768]{0:T(1024)S(1)} %copy-done.6, f32[256,768]{1,0:T(8,128)S(1)} %get-tuple-element.33, ...), kind=kOutput, calls=%fused_computation.147 | convolution fusion | flops 610269184 | bytes 6305792 | tf_op jit(solution)/shard_map/dot_general | solution.py:96
  54.8 1.3 %collective-permute-start.5 = (bf16[256,768]{1,0:T(8,128)(2,1)S(1)}, bf16[256,768]{1,0:T(8,128)(2,1)S(1)}, u32[]{:S(2)}, u32[]{:S(2)}) collective-permute-start(bf16[256,768]{1,0:T(8,128)(2,1)S(1)} %get-tuple-element.24), channel_id=1, source_target_pairs={{4,0},{6,2},{8,4},{10,6},{12,8},{14,10},{16,12},{18,14},{20,16},{2... | collective-permute-start | bytes 1179656 | tf_op jit(solution)/shard_map/ppermute | solution.py:19
  56.1 4.9 %collective-permute-start.4 = (bf16[256,768]{1,0:T(8,128)(2,1)S(1)}, bf16[256,768]{1,0:T(8,128)(2,1)S(1)}, u32[]{:S(2)}, u32[]{:S(2)}) collective-permute-start(bf16[256,768]{1,0:T(8,128)(2,1)S(1)} %get-tuple-element.24), channel_id=1, source_target_pairs={{0,4},{2,6},{4,8},{6,10},{8,12},{10,14},{12,16},{14,18},{16,20},{1... | collective-permute-start | bytes 1179656 | tf_op jit(solution)/shard_map/ppermute | solution.py:19
  61.0 1.5 %collective-permute-start.7 = (bf16[256,768]{1,0:T(8,128)(2,1)S(1)}, bf16[256,768]{1,0:T(8,128)(2,1)S(1)}, u32[]{:S(2)}, u32[]{:S(2)}) collective-permute-start(bf16[256,768]{1,0:T(8,128)(2,1)S(1)} %get-tuple-element.25), channel_id=1, source_target_pairs={{4,0},{6,2},{8,4},{10,6},{12,8},{14,10},{16,12},{18,14},{20,16},{2... | collective-permute-start | bytes 1179656 | tf_op jit(solution)/shard_map/ppermute | solution.py:19
  62.5 5.4 %collective-permute-start.6 = (bf16[256,768]{1,0:T(8,128)(2,1)S(1)}, bf16[256,768]{1,0:T(8,128)(2,1)S(1)}, u32[]{:S(2)}, u32[]{:S(2)}) collective-permute-start(bf16[256,768]{1,0:T(8,128)(2,1)S(1)} %get-tuple-element.25), channel_id=1, source_target_pairs={{0,4},{2,6},{4,8},{6,10},{8,12},{10,14},{12,16},{14,18},{16,20},{1... | collective-permute-start | bytes 1179656 | tf_op jit(solution)/shard_map/ppermute | solution.py:19
  69.6 1.2 %maximum_bitcast_fusion = bf16[1,512,1536]{2,1,0:T(8,128)(2,1)} fusion(bf16[256,1536]{1,0:T(8,128)(2,1)S(1)} %fusion.5, bf16[256,1536]{1,0:T(8,128)(2,1)S(1)} %fusion.4), kind=kLoop, calls=%fused_computation.102 | loop fusion | flops 3145728 | bytes 3145728 | tf_op jit(solution)/shard_map/broadcast_in_dim | solution.py:128
  70.9 22.9 %collective-permute-done.6 = bf16[256,768]{1,0:T(8,128)(2,1)S(1)} collective-permute-done((bf16[256,768]{1,0:T(8,128)(2,1)S(1)}, bf16[256,768]{1,0:T(8,128)(2,1)S(1)}, u32[]{:S(2)}, u32[]{:S(2)}) %collective-permute-start.6) | collective-permute-done | bytes 393248 | tf_op jit(solution)/shard_map/ppermute | solution.py:19
  94.7 1.7 %fusion.77 = f32[256,1536]{1,0:T(8,128)S(1)} fusion(f32[256,1536]{1,0:T(8,128)S(1)} %fusion.1, bf16[256,768]{1,0:T(8,128)(2,1)S(1)} %collective-permute-done.7, bf16[3,1536,768]{2,1,0:T(8,128)(2,1)S(1)} %bitcast.210, f32[256]{0:T(256)S(1)} %fusion.156, f32[256]{0:T(256)S(1)} %get-tuple-element.31, f32[1536]{0:T(1024)S(1)} %copy-done.5, ...), kind=kOutput, calls=%fused_computation.95 | convolution fusion | flops 613416960 | bytes 6694912 | tf_op jit(solution)/shard_map/dot_general | solution.py:117
  97.2 2.5 %fusion.51 = (f32[1536]{0:T(1024)S(1)}, f32[256]{0:T(256)S(1)}, f32[256]{0:T(256)S(1)}, f32[1536]{0:T(1024)S(1)}, f32[256,1536]{1,0:T(8,128)S(1)}) fusion(f32[256]{0:T(256)S(1)} %fusion.154, bf16[1,512,1536]{2,1,0:T(8,128)(2,1)S(1)} %copy-done.2, f32[1536]{0:T(1024)S(1)} %copy-done.5, f32[256,1536]{1,0:T(8,128)S(1)} %fusion.77, f32[256]{0:T(256)S(1)} %fusion.156, ...), kind=kOutput, calls=%fused_computation.69 | convolution fusion | flops 618131968 | bytes 9069568 | tf_op jit(solution)/shard_map/dot_general | solution.py:117
  99.7 2.5 %collective-permute-start.9 = (f32[2304]{0:T(1024)S(1)}, f32[2304]{0:T(1024)S(1)}, u32[]{:S(2)}, u32[]{:S(2)}) collective-permute-start(f32[2304]{0:T(1024)S(1)} %pad_maximum_fusion), channel_id=1, source_target_pairs={{0,4},{2,6},{4,0},{6,2},{8,12},{10,14},{12,8},{14,10},{16,20},{18,... | collective-permute-start | bytes 27656 | tf_op jit(solution)/shard_map/ppermute | solution.py:37
  102.5 1.5 %collective-permute-done.9 = f32[2304]{0:T(1024)S(1)} collective-permute-done((f32[2304]{0:T(1024)S(1)}, f32[2304]{0:T(1024)S(1)}, u32[]{:S(2)}, u32[]{:S(2)}) %collective-permute-start.9) | collective-permute-done | bytes 9248 | tf_op jit(solution)/shard_map/ppermute | solution.py:37
  104.0 1.5 %collective-permute-done.10 = f32[2304]{0:T(1024)S(1)} collective-permute-done((f32[2304]{0:T(1024)S(1)}, f32[2304]{0:T(1024)S(1)}, u32[]{:S(2)}, u32[]{:S(2)}) %collective-permute-start.10) | collective-permute-done | bytes 9248 | tf_op jit(solution)/shard_map/ppermute | solution.py:37
  105.5 3.0 %collective-permute-start.12 = (f32[2304]{0:T(1024)S(1)}, f32[2304]{0:T(1024)S(1)}, u32[]{:S(2)}, u32[]{:S(2)}) collective-permute-start(f32[2304]{0:T(1024)S(1)} %add_add_fusion.5), channel_id=1, source_target_pairs={{0,16},{2,18},{4,20},{6,22},{8,24},{10,26},{12,28},{14,30},{16,0},... | collective-permute-start | bytes 27656 | tf_op jit(solution)/shard_map/ppermute | solution.py:37
  108.6 1.4 %collective-permute-start.11 = (f32[2304]{0:T(1024)S(1)}, f32[2304]{0:T(1024)S(1)}, u32[]{:S(2)}, u32[]{:S(2)}) collective-permute-start(f32[2304]{0:T(1024)S(1)} %add_add_fusion.5), channel_id=1, source_target_pairs={{0,8},{2,10},{4,12},{6,14},{8,0},{10,2},{12,4},{14,6},{16,24},{18,... | collective-permute-start | bytes 27656 | tf_op jit(solution)/shard_map/ppermute | solution.py:37
  111.0 1.2 %collective-permute-done.11 = f32[2304]{0:T(1024)S(1)} collective-permute-done((f32[2304]{0:T(1024)S(1)}, f32[2304]{0:T(1024)S(1)}, u32[]{:S(2)}, u32[]{:S(2)}) %collective-permute-start.11) | collective-permute-done | bytes 9248 | tf_op jit(solution)/shard_map/ppermute | solution.py:37
  112.3 1.5 %collective-permute-start.14 = (f32[2304]{0:T(1024)S(1)}, f32[2304]{0:T(1024)S(1)}, u32[]{:S(2)}, u32[]{:S(2)}) collective-permute-start(f32[2304]{0:T(1024)S(1)} %add_add_fusion.4), channel_id=1, source_target_pairs={{0,1},{1,0},{2,3},{3,2},{4,5},{5,4},{6,7},{7,6},{8,9},{9,8},{10,11... | collective-permute-start | bytes 27656 | tf_op jit(solution)/shard_map/ppermute | solution.py:37
  113.8 1.2 %maximum_bitcast_fusion.1 = bf16[1,512,1536]{2,1,0:T(8,128)(2,1)} fusion(bf16[256,1536]{1,0:T(8,128)(2,1)S(1)} %get-tuple-element.23, bf16[256,1536]{1,0:T(8,128)(2,1)S(1)} %get-tuple-element.22), kind=kLoop, calls=%fused_computation.103 | loop fusion | flops 3145728 | bytes 3145728 | tf_op jit(solution)/shard_map/broadcast_in_dim | solution.py:129
  (65 shorter events, 9.1 us)
Async XLA Ops:
  0.6 48.7 %copy-start = (bf16[768,1536]{1,0:T(8,128)(2,1)S(1)}, bf16[768,1536]{1,0:T(8,128)(2,1)}, u32[]{:S(2)}) copy-start(bf16[768,1536]{1,0:T(8,128)(2,1)} %param.13) | copy-start | bytes 7077892
  0.6 2.0 %copy-start.1 = (bf16[1,512,1536]{2,1,0:T(8,128)(2,1)S(1)}, bf16[1,512,1536]{2,1,0:T(8,128)(2,1)}, u32[]{:S(2)}) copy-start(bf16[1,512,1536]{2,1,0:T(8,128)(2,1)} %param.7) | copy-start | bytes 4718596
  2.7 5.1 %copy-start.3 = (bf16[3,1536,768]{2,1,0:T(8,128)(2,1)S(1)}, bf16[3,1536,768]{2,1,0:T(8,128)(2,1)}, u32[]{:S(2)}) copy-start(bf16[3,1536,768]{2,1,0:T(8,128)(2,1)} %param.11) | copy-start | bytes 21233668
  2.7 5.1 %copy-start.5 = (f32[1536]{0:T(1024)S(1)}, f32[1536]{0:T(1024)}, u32[]{:S(2)}) copy-start(f32[1536]{0:T(1024)} %param.10) | copy-start | bytes 18436
  6.5 19.5 %collective-permute-start.3 = (bf16[256,768]{1,0:T(8,128)(2,1)}, bf16[256,768]{1,0:T(8,128)(2,1)S(1)}, u32[]{:S(2)}, u32[]{:S(2)}) collective-permute-start(bf16[256,768]{1,0:T(8,128)(2,1)} %fusion.109), channel_id=1, source_target_pairs={{4,0},{6,2},{8,4},{10,6},{12,8},{14,10},{16,12},{18,14},{20,16},{2... | collective-permute-start | bytes 1179656 | tf_op jit(solution)/shard_map/ppermute | solution.py:19
  9.8 28.1 %collective-permute-start.2 = (bf16[256,768]{1,0:T(8,128)(2,1)}, bf16[256,768]{1,0:T(8,128)(2,1)}, u32[]{:S(2)}, u32[]{:S(2)}) collective-permute-start(bf16[256,768]{1,0:T(8,128)(2,1)} %fusion.103), channel_id=1, source_target_pairs={{0,4},{2,6},{4,8},{6,10},{8,12},{10,14},{12,16},{14,18},{16,20},{1... | collective-permute-start | bytes 1179656 | tf_op jit(solution)/shard_map/ppermute | solution.py:19
  18.1 7.6 %copy-start.7 = (s32[1,4]{1,0:T(1,128)S(1)}, s32[1,4]{1,0:T(1,128)}, u32[]{:S(2)}) copy-start(s32[1,4]{1,0:T(1,128)} %param.9) | copy-start | bytes 52
  18.1 28.1 %collective-permute-start = (bf16[256,768]{1,0:T(8,128)(2,1)}, bf16[256,768]{1,0:T(8,128)(2,1)S(1)}, u32[]{:S(2)}, u32[]{:S(2)}) collective-permute-start(bf16[256,768]{1,0:T(8,128)(2,1)} %fusion.100), channel_id=1, source_target_pairs={{0,4},{2,6},{4,8},{6,10},{8,12},{10,14},{12,16},{14,18},{16,20},{1... | collective-permute-start | bytes 1179656 | tf_op jit(solution)/shard_map/ppermute | solution.py:19
  24.3 21.9 %collective-permute-start.1 = (bf16[256,768]{1,0:T(8,128)(2,1)}, bf16[256,768]{1,0:T(8,128)(2,1)}, u32[]{:S(2)}, u32[]{:S(2)}) collective-permute-start(bf16[256,768]{1,0:T(8,128)(2,1)} %fusion.106), channel_id=1, source_target_pairs={{4,0},{6,2},{8,4},{10,6},{12,8},{14,10},{16,12},{18,14},{20,16},{2... | collective-permute-start | bytes 1179656 | tf_op jit(solution)/shard_map/ppermute | solution.py:19
  37.9 8.3 %copy-start.2 = (bf16[1,512,1536]{2,1,0:T(8,128)(2,1)S(1)}, bf16[1,512,1536]{2,1,0:T(8,128)(2,1)}, u32[]{:S(2)}) copy-start(bf16[1,512,1536]{2,1,0:T(8,128)(2,1)} %param.7) | copy-start | bytes 4718596
  46.2 3.1 %copy-start.6 = (f32[768]{0:T(1024)S(1)}, f32[768]{0:T(1024)}, u32[]{:S(2)}) copy-start(f32[768]{0:T(1024)} %param.12) | copy-start | bytes 9220
  49.3 1.4 %copy-start.4 = (bf16[1,512,1536]{2,1,0:T(8,128)(2,1)S(1)}, bf16[1,512,1536]{2,1,0:T(8,128)(2,1)}, u32[]{:S(2)}) copy-start(bf16[1,512,1536]{2,1,0:T(8,128)(2,1)} %param.8) | copy-start | bytes 4718596
  51.9 16.1 %slice-start = ((s8[7077888]{0:T(1024)(128)(4,1)}), s8[4194304]{0:T(1024)(128)(4,1)S(1)}, s32[]{:S(2)}) async-start(s8[7077888]{0:T(1024)(128)(4,1)} %bitcast.209), calls=%async_computation | async-start | bytes 8388608
  52.9 15.1 %slice-start.1 = ((s8[7077888]{0:T(1024)(128)(4,1)}), s8[2883584]{0:T(1024)(128)(4,1)S(1)}, s32[]{:S(2)}) async-start(s8[7077888]{0:T(1024)(128)(4,1)} %bitcast.209), calls=%async_computation.1 | async-start | bytes 5767168
  54.8 42.4 %collective-permute-start.5 = (bf16[256,768]{1,0:T(8,128)(2,1)S(1)}, bf16[256,768]{1,0:T(8,128)(2,1)S(1)}, u32[]{:S(2)}, u32[]{:S(2)}) collective-permute-start(bf16[256,768]{1,0:T(8,128)(2,1)S(1)} %get-tuple-element.24), channel_id=1, source_target_pairs={{4,0},{6,2},{8,4},{10,6},{12,8},{14,10},{16,12},{18,14},{20,16},{2... | collective-permute-start | bytes 1179656 | tf_op jit(solution)/shard_map/ppermute | solution.py:19
  56.1 40.3 %collective-permute-start.4 = (bf16[256,768]{1,0:T(8,128)(2,1)S(1)}, bf16[256,768]{1,0:T(8,128)(2,1)S(1)}, u32[]{:S(2)}, u32[]{:S(2)}) collective-permute-start(bf16[256,768]{1,0:T(8,128)(2,1)S(1)} %get-tuple-element.24), channel_id=1, source_target_pairs={{0,4},{2,6},{4,8},{6,10},{8,12},{10,14},{12,16},{14,18},{16,20},{1... | collective-permute-start | bytes 1179656 | tf_op jit(solution)/shard_map/ppermute | solution.py:19
  61.0 33.6 %collective-permute-start.7 = (bf16[256,768]{1,0:T(8,128)(2,1)S(1)}, bf16[256,768]{1,0:T(8,128)(2,1)S(1)}, u32[]{:S(2)}, u32[]{:S(2)}) collective-permute-start(bf16[256,768]{1,0:T(8,128)(2,1)S(1)} %get-tuple-element.25), channel_id=1, source_target_pairs={{4,0},{6,2},{8,4},{10,6},{12,8},{14,10},{16,12},{18,14},{20,16},{2... | collective-permute-start | bytes 1179656 | tf_op jit(solution)/shard_map/ppermute | solution.py:19
  62.5 31.3 %collective-permute-start.6 = (bf16[256,768]{1,0:T(8,128)(2,1)S(1)}, bf16[256,768]{1,0:T(8,128)(2,1)S(1)}, u32[]{:S(2)}, u32[]{:S(2)}) collective-permute-start(bf16[256,768]{1,0:T(8,128)(2,1)S(1)} %get-tuple-element.25), channel_id=1, source_target_pairs={{0,4},{2,6},{4,8},{6,10},{8,12},{10,14},{12,16},{14,18},{16,20},{1... | collective-permute-start | bytes 1179656 | tf_op jit(solution)/shard_map/ppermute | solution.py:19
  99.7 4.2 %collective-permute-start.9 = (f32[2304]{0:T(1024)S(1)}, f32[2304]{0:T(1024)S(1)}, u32[]{:S(2)}, u32[]{:S(2)}) collective-permute-start(f32[2304]{0:T(1024)S(1)} %pad_maximum_fusion), channel_id=1, source_target_pairs={{0,4},{2,6},{4,0},{6,2},{8,12},{10,14},{12,8},{14,10},{16,20},{18,... | collective-permute-start | bytes 27656 | tf_op jit(solution)/shard_map/ppermute | solution.py:37
  102.3 3.2 %collective-permute-start.10 = (f32[2304]{0:T(1024)S(1)}, f32[2304]{0:T(1024)S(1)}, u32[]{:S(2)}, u32[]{:S(2)}) collective-permute-start(f32[2304]{0:T(1024)S(1)} %pad_maximum_fusion), channel_id=1, source_target_pairs={{0,6},{2,4},{4,2},{6,0},{8,14},{10,12},{12,10},{14,8},{16,22},{18,... | collective-permute-start | bytes 27656 | tf_op jit(solution)/shard_map/ppermute | solution.py:37
  102.3 3.2 %collective-permute-start.8 = (f32[2304]{0:T(1024)S(1)}, f32[2304]{0:T(1024)S(1)}, u32[]{:S(2)}, u32[]{:S(2)}) collective-permute-start(f32[2304]{0:T(1024)S(1)} %pad_maximum_fusion), channel_id=1, source_target_pairs={{0,2},{2,0},{4,6},{6,4},{8,10},{10,8},{12,14},{14,12},{16,18},{18,... | collective-permute-start | bytes 27656 | tf_op jit(solution)/shard_map/ppermute | solution.py:37
  105.5 5.6 %collective-permute-start.13 = (f32[2304]{0:T(1024)S(1)}, f32[2304]{0:T(1024)S(1)}, u32[]{:S(2)}, u32[]{:S(2)}) collective-permute-start(f32[2304]{0:T(1024)S(1)} %add_add_fusion.5), channel_id=1, source_target_pairs={{0,24},{2,26},{4,28},{6,30},{8,16},{10,18},{12,20},{14,22},{16,8},... | collective-permute-start | bytes 27656 | tf_op jit(solution)/shard_map/ppermute | solution.py:37
  105.5 5.5 %collective-permute-start.12 = (f32[2304]{0:T(1024)S(1)}, f32[2304]{0:T(1024)S(1)}, u32[]{:S(2)}, u32[]{:S(2)}) collective-permute-start(f32[2304]{0:T(1024)S(1)} %add_add_fusion.5), channel_id=1, source_target_pairs={{0,16},{2,18},{4,20},{6,22},{8,24},{10,26},{12,28},{14,30},{16,0},... | collective-permute-start | bytes 27656 | tf_op jit(solution)/shard_map/ppermute | solution.py:37
  108.6 3.7 %collective-permute-start.11 = (f32[2304]{0:T(1024)S(1)}, f32[2304]{0:T(1024)S(1)}, u32[]{:S(2)}, u32[]{:S(2)}) collective-permute-start(f32[2304]{0:T(1024)S(1)} %add_add_fusion.5), channel_id=1, source_target_pairs={{0,8},{2,10},{4,12},{6,14},{8,0},{10,2},{12,4},{14,6},{16,24},{18,... | collective-permute-start | bytes 27656 | tf_op jit(solution)/shard_map/ppermute | solution.py:37
  112.3 3.7 %collective-permute-start.14 = (f32[2304]{0:T(1024)S(1)}, f32[2304]{0:T(1024)S(1)}, u32[]{:S(2)}, u32[]{:S(2)}) collective-permute-start(f32[2304]{0:T(1024)S(1)} %add_add_fusion.4), channel_id=1, source_target_pairs={{0,1},{1,0},{2,3},{3,2},{4,5},{5,4},{6,7},{7,6},{8,9},{9,8},{10,11... | collective-permute-start | bytes 27656 | tf_op jit(solution)/shard_map/ppermute | solution.py:37

commit v3 on v2

--- a/solution.py
+++ b/solution.py
@@ -6,8 +6,11 @@
 from jax.sharding import PartitionSpec as P
 
 SPAN = 2
-CHUNKS = 2
+CHUNKS = (1, 1)
+AXES = ("seq", "batch")
 RADIX = 4
+EARLY = True
+LATE_OUTPUT = True
 
 
 epsilon = 1e-06
@@ -41,7 +44,7 @@
 
 
 def reduce_all(x):
-    axes = ("seq", "batch")
+    axes = AXES
     sizes = [lax.axis_size(a) for a in axes]
     if any(s & (s - 1) for s in sizes):
         return lax.psum(x, axes)
@@ -65,14 +68,17 @@
     tap_before = tap_weights[0]
     tap_center = tap_weights[1]
     tap_after = tap_weights[2]
-    rows = shard_rows // CHUNKS
+    unit = shard_rows // sum(CHUNKS)
     first_row = lax.axis_index("seq") * shard_rows
 
     chunks = []
-    for c in range(CHUNKS):
-        signal = activations[0, c * rows:(c + 1) * rows]
-        upstream = cotangent[0, c * rows:(c + 1) * rows]
-        positions = first_row + c * rows + jnp.arange(rows, dtype=jnp.int32)
+    start = 0
+    for share in CHUNKS:
+        rows = share * unit
+        signal = activations[0, start:start + rows]
+        upstream = cotangent[0, start:start + rows]
+        positions = first_row + start + jnp.arange(rows, dtype=jnp.int32)
+        start += rows
         owners = contig_owner(lengths, positions)
         before_valid = (
             (positions >= tap_reach) & (contig_owner(lengths, positions - tap_reach) == owners)
@@ -82,7 +88,7 @@
             & (contig_owner(lengths, positions + tap_reach) == owners)
         ).astype(jnp.float32)[:, None]
         normed, input_vjp = jax.vjp(norm_activate, signal.astype(jnp.float32), gain_input)
-        hidden = normed.astype(jnp.bfloat16)
+        hidden = lax.optimization_barrier(normed.astype(jnp.bfloat16))
         sent_before = jnp.dot(hidden, tap_before, preferred_element_type=jnp.float32)
         sent_after = jnp.dot(hidden, tap_after, preferred_element_type=jnp.float32)
         chunks.append(dict(
@@ -94,6 +100,8 @@
     for ch in chunks:
         combined = jnp.dot(ch["hidden"], tap_center, preferred_element_type=jnp.float32)
         grad_middle = jnp.dot(ch["upstream"], point_weights.T, preferred_element_type=jnp.float32)
+        if EARLY:
+            combined, grad_middle = lax.optimization_barrier((combined, grad_middle))
         combined = combined + ch["before_valid"] * ch["product_before"].astype(jnp.float32)
         combined = combined + ch["after_valid"] * ch["product_after"].astype(jnp.float32)
         middle_f, middle_vjp = jax.vjp(norm_activate, combined, gain_middle)
@@ -103,6 +111,14 @@
         ch["grad_combined"] = grad_combined
         ch["combined_before"] = shifted(grad_combined, "seq", SPAN)
         ch["combined_after"] = shifted(grad_combined, "seq", -SPAN)
+    if LATE_OUTPUT:
+        last = chunks[-1]
+        middles = [ch["middle"] for ch in chunks]
+        middles, last["combined_before"], last["combined_after"] = lax.optimization_barrier(
+            (middles, last["combined_before"], last["combined_after"])
+        )
+        for ch, middle in zip(chunks, middles):
+            ch["middle"] = middle
     outputs, grads = [], []
     input_terms, middle_terms = None, None
     for ch in chunks:

time: 118 us -> 115 us (0.975)
  waiting for transfers between devices: 45 us -> 29.3 us
  other arithmetic: 7.31 us -> 19.3 us
    ppermute x8, waiting for transfers between devices: 39.7 us -> 23.1 us  [shifted(): return lax.ppermute(x, axis, pairs)]
    reduce_sum x1 -> x3, other arithmetic: 1.92 us -> 4.96 us  [norm_activate(): mean_square = jnp.mean(values * values, axis=-1, keepdims=True)]
    dot_general x2, matrix products: 5.84 us -> 3.07 us  [body(): sent_after = jnp.dot(hidden, tap_after, preferred_element_type=jnp.float32)]
    dot_general x2, matrix products: 1.62 us -> 3.28 us  [body(): jnp.dot(ch['grad_combined'], tap_center.T, preferred_element_type=jnp.flo...]
    dot_general x2, matrix products: 4.02 us -> 5.58 us  [body(): jnp.dot(hidden, tap_before, preferred_element_type=jnp.float32)]
    convert_element_type x1 -> x2, other arithmetic: 0.35 us -> 1.77 us  [body(): grad_combined = grad_combined_f.astype(jnp.bfloat16)]
    convert_element_type x0 -> x1, other arithmetic: none -> 1.4 us  [body(): hidden = lax.optimization_barrier(normed.astype(jnp.bfloat16))]
    ppermute x7, starting transfers between devices: 8.72 us -> 10.1 us  [group_sum(): parts.append(lax.ppermute(x, axis, pairs))]
  transfers between devices with their start and end apart: 15 -> 15, of which waited for: 8 -> 7; matrix products, arithmetic and copies ran while one was open for 16% -> 29% of each run, Pallas kernels for 0% -> 0%
where the time goes in v3:
time: 115 us
  starting transfers between devices  34.9 us (30%)
  waiting for transfers between devices  29.3 us (25%)
  matrix products  28.7 us (25%)
  other arithmetic  19.3 us (17%)
  local copies, waits for them, and re-layouts  1.36 us (1%)
    ppermute x8, starting transfers between devices, shifted(): return lax.ppermute(x, axis, pairs)  24.9 us
    ppermute x8, waiting for transfers between devices, shifted(): return lax.ppermute(x, axis, pairs)  23.1 us
    ppermute x7, starting transfers between devices, group_sum(): parts.append(lax.ppermute(x, axis, pairs))  10.1 us
    ppermute x7, waiting for transfers between devices, group_sum(): parts.append(lax.ppermute(x, axis, pairs))  6.18 us
    dot_general x2, matrix products, body(): jnp.dot(ch['hidden'], tap_center, preferred_element_type=jnp.float32)  5.95 us
    dot_general x2, matrix products, body(): jnp.dot(hidden, tap_before, preferred_element_type=jnp.float32)  5.58 us
    reduce_sum x3, other arithmetic, norm_activate(): mean_square = jnp.mean(values * values, axis=-1, keepdims=True)  4.96 us
    dot_general x2, matrix products, body(): jnp.dot(ch['combined_after'], tap_before.T, preferred_element_type=jnp.fl...  4.17 us
  transfers between devices with their start and end apart: 15, of which 7 were waited for; matrix products, arithmetic and copies ran while one was open for 29% of the time, Pallas kernels for 0%

profile of v3, /device:TPU:0, one launch (start us, length us, event | category | flops | bytes accessed | tf_op | source)
XLA Modules:
  0.0 114.7 jit_solution(13086757259114722347)
XLA Ops:
  0.7 1.9 %fusion.60 = (f32[256]{0:T(256)S(1)}, f32[256]{0:T(256)S(1)}) fusion(bf16[1,512,1536]{2,1,0:T(8,128)(2,1)} %param.7), kind=kLoop, calls=%fused_computation.80 | loop fusion | flops 2358784 | bytes 1574912 | tf_op jit(solution)/shard_map/jvp()/reduce_sum | solution.py:26
  3.1 1.4 %fusion.38 = (bf16[256,1536]{1,0:T(8,128)(2,1)S(1)}, bf16[256,1536]{1,0:T(8,128)(2,1)S(1)}) fusion(f32[256]{0:T(256)S(1)} %fusion.116, f32[1536]{0:T(1024)S(1)} %copy-done.11, bf16[1,512,1536]{2,1,0:T(8,128)(2,1)S(1)} %copy-done.1, f32[256]{0:T(256)S(1)} %fusion.114), kind=kLoop, calls=%fused_computation.58 | loop fusion | flops 9437184 | bytes 3153920 | tf_op jit(solution)/shard_map/convert_element_type | solution.py:91
  4.5 4.0 %fusion.81 = bf16[256,768]{1,0:T(8,128)(2,1)} fusion(bf16[256,1536]{1,0:T(8,128)(2,1)S(1)} %get-tuple-element.46, bf16[3,1536,768]{2,1,0:T(8,128)(2,1)} %param.11), kind=kOutput, calls=%fused_computation.97 | convolution fusion | flops 604176384 | bytes 3538944 | tf_op jit(solution)/shard_map/dot_general | solution.py:92
  8.6 5.6 %collective-permute-start.2 = (bf16[256,768]{1,0:T(8,128)(2,1)}, bf16[256,768]{1,0:T(8,128)(2,1)}, u32[]{:S(2)}, u32[]{:S(2)}) collective-permute-start(bf16[256,768]{1,0:T(8,128)(2,1)} %fusion.81), channel_id=1, source_target_pairs={{0,4},{2,6},{4,8},{6,10},{8,12},{10,14},{12,16},{14,18},{16,20},{1... | collective-permute-start | bytes 1179656 | tf_op jit(solution)/shard_map/ppermute | solution.py:22
  14.2 1.5 %fusion.87 = bf16[256,768]{1,0:T(8,128)(2,1)} fusion(bf16[256,1536]{1,0:T(8,128)(2,1)S(1)} %get-tuple-element.46, bf16[3,1536,768]{2,1,0:T(8,128)(2,1)S(1)} %copy-done.3), kind=kOutput, calls=%fused_computation.99 | convolution fusion | flops 604176384 | bytes 3538944 | tf_op jit(solution)/shard_map/dot_general | solution.py:93
  15.7 1.3 %collective-permute-start.3 = (bf16[256,768]{1,0:T(8,128)(2,1)}, bf16[256,768]{1,0:T(8,128)(2,1)}, u32[]{:S(2)}, u32[]{:S(2)}) collective-permute-start(bf16[256,768]{1,0:T(8,128)(2,1)} %fusion.87), channel_id=1, source_target_pairs={{4,0},{6,2},{8,4},{10,6},{12,8},{14,10},{16,12},{18,14},{20,16},{2... | collective-permute-start | bytes 1179656 | tf_op jit(solution)/shard_map/ppermute | solution.py:22
  17.0 1.5 %fusion.78 = bf16[256,768]{1,0:T(8,128)(2,1)} fusion(bf16[256,1536]{1,0:T(8,128)(2,1)S(1)} %get-tuple-element.47, bf16[3,1536,768]{2,1,0:T(8,128)(2,1)S(1)} %copy-done.3), kind=kOutput, calls=%fused_computation.96 | convolution fusion | flops 604176384 | bytes 3538944 | tf_op jit(solution)/shard_map/dot_general | solution.py:92
  18.5 4.6 %collective-permute-start = (bf16[256,768]{1,0:T(8,128)(2,1)}, bf16[256,768]{1,0:T(8,128)(2,1)S(1)}, u32[]{:S(2)}, u32[]{:S(2)}) collective-permute-start(bf16[256,768]{1,0:T(8,128)(2,1)} %fusion.78), channel_id=1, source_target_pairs={{0,4},{2,6},{4,8},{6,10},{8,12},{10,14},{12,16},{14,18},{16,20},{1... | collective-permute-start | bytes 1179656 | tf_op jit(solution)/shard_map/ppermute | solution.py:22
  23.1 1.6 %fusion.84 = bf16[256,768]{1,0:T(8,128)(2,1)} fusion(bf16[256,1536]{1,0:T(8,128)(2,1)S(1)} %get-tuple-element.47, bf16[3,1536,768]{2,1,0:T(8,128)(2,1)S(1)} %copy-done.3), kind=kOutput, calls=%fused_computation.98 | convolution fusion | flops 604176384 | bytes 3538944 | tf_op jit(solution)/shard_map/dot_general | solution.py:93
  24.7 1.3 %collective-permute-start.1 = (bf16[256,768]{1,0:T(8,128)(2,1)}, bf16[256,768]{1,0:T(8,128)(2,1)}, u32[]{:S(2)}, u32[]{:S(2)}) collective-permute-start(bf16[256,768]{1,0:T(8,128)(2,1)} %fusion.84), channel_id=1, source_target_pairs={{4,0},{6,2},{8,4},{10,6},{12,8},{14,10},{16,12},{18,14},{20,16},{2... | collective-permute-start | bytes 1179656 | tf_op jit(solution)/shard_map/ppermute | solution.py:22
  29.3 3.4 %fusion.22 = f32[256,768]{1,0:T(8,128)} fusion(bf16[256,1536]{1,0:T(8,128)(2,1)S(1)} %get-tuple-element.46, bf16[3,1536,768]{2,1,0:T(8,128)(2,1)} %param.11), kind=kOutput, calls=%fused_computation.38 | convolution fusion | flops 603979776 | bytes 3932160 | tf_op jit(solution)/shard_map/dot_general | solution.py:101
  32.7 2.6 %fusion.24 = f32[256,768]{1,0:T(8,128)S(1)} fusion(bf16[256,1536]{1,0:T(8,128)(2,1)S(1)} %copy-done.8, bf16[3,1536,768]{2,1,0:T(8,128)(2,1)} %param.11), kind=kOutput, calls=%fused_computation.40 | convolution fusion | flops 603979776 | bytes 3932160 | tf_op jit(solution)/shard_map/dot_general | solution.py:101
  35.3 1.7 %fusion.104 = f32[256,768]{1,0:T(8,128)} fusion(bf16[768,1536]{1,0:T(8,128)(2,1)S(1)} %copy-done, bf16[1,512,1536]{2,1,0:T(8,128)(2,1)S(1)} %copy-done.4), kind=kOutput, calls=%fused_computation.120 | convolution fusion | flops 603979776 | bytes 3932160 | tf_op jit(solution)/shard_map/dot_general | solution.py:102
  37.0 1.7 %fusion.106 = f32[256,768]{1,0:T(8,128)} fusion(bf16[768,1536]{1,0:T(8,128)(2,1)S(1)} %copy-done, bf16[1,512,1536]{2,1,0:T(8,128)(2,1)S(1)} %copy-done.4), kind=kOutput, calls=%fused_computation.122 | convolution fusion | flops 603979776 | bytes 3932160 | tf_op jit(solution)/shard_map/dot_general | solution.py:102
  38.7 1.3 %reduce-window.8 = s32[4,1]{0,1:T(1,128)} reduce-window(s32[4,1]{0,1:T(1,128)} %bitcast.94, s32[]{:T(128)} %constant.60.clone.1), window={size=4x1 pad=3_0x0_0}, to_apply=%region_1.2 | reduce-window | flops 12 | bytes 36 | tf_op jit(solution)/shard_map/reduce-window.3
  41.0 1.7 %multiply_reduce_fusion.4 = (f32[256]{0:T(256)S(1)}, f32[256,768]{1,0:T(8,128)S(1)}) fusion(bf16[256,768]{1,0:T(8,128)(2,1)} %collective-permute-done.3, f32[256]{0:T(256)S(1)} %get-tuple-element.56, f32[256,768]{1,0:T(8,128)} %fusion.22, bf16[256,768]{1,0:T(8,128)(2,1)} %collective-permute-done.2, f32[256]{0:T(256)S(1)} %get-tuple-element.55), kind=kLoop, calls=%fused_computation.129 | loop fusion | flops 1572608 | bytes 2362368 | tf_op jit(solution)/shard_map/jvp()/reduce_sum | solution.py:26
  42.7 4.7 %collective-permute-done = bf16[256,768]{1,0:T(8,128)(2,1)S(1)} collective-permute-done((bf16[256,768]{1,0:T(8,128)(2,1)}, bf16[256,768]{1,0:T(8,128)(2,1)S(1)}, u32[]{:S(2)}, u32[]{:S(2)}) %collective-permute-start) | collective-permute-done | bytes 393248 | tf_op jit(solution)/shard_map/ppermute | solution.py:22
  47.4 1.4 %multiply_reduce_fusion.5 = (f32[256]{0:T(256)S(1)}, f32[256,768]{1,0:T(8,128)S(1)}) fusion(bf16[256,768]{1,0:T(8,128)(2,1)} %collective-permute-done.1, f32[256]{0:T(256)S(1)} %get-tuple-element.58, f32[256,768]{1,0:T(8,128)S(1)} %fusion.24, bf16[256,768]{1,0:T(8,128)(2,1)S(1)} %collective-permute-done, f32[256]{0:T(256)S(1)} %get-tuple-element.57), kind=kLoop, calls=%fused_computation.132 | loop fusion | flops 1572608 | bytes 2362368 | tf_op jit(solution)/shard_map/jvp()/reduce_sum | solution.py:26
  51.7 4.3 %collective-permute-start.4 = (bf16[256,768]{1,0:T(8,128)(2,1)S(1)}, bf16[256,768]{1,0:T(8,128)(2,1)S(1)}, u32[]{:S(2)}, u32[]{:S(2)}) collective-permute-start(bf16[256,768]{1,0:T(8,128)(2,1)S(1)} %get-tuple-element.50), channel_id=1, source_target_pairs={{0,4},{2,6},{4,8},{6,10},{8,12},{10,14},{12,16},{14,18},{16,20},{1... | collective-permute-start | bytes 1179656 | tf_op jit(solution)/shard_map/ppermute | solution.py:22
  56.0 1.3 %collective-permute-start.5 = (bf16[256,768]{1,0:T(8,128)(2,1)S(1)}, bf16[256,768]{1,0:T(8,128)(2,1)S(1)}, u32[]{:S(2)}, u32[]{:S(2)}) collective-permute-start(bf16[256,768]{1,0:T(8,128)(2,1)S(1)} %get-tuple-element.50), channel_id=1, source_target_pairs={{4,0},{6,2},{8,4},{10,6},{12,8},{14,10},{16,12},{18,14},{20,16},{2... | collective-permute-start | bytes 1179656 | tf_op jit(solution)/shard_map/ppermute | solution.py:22
  57.3 2.5 %fusion.20 = f32[256,1536]{1,0:T(8,128)S(1)} fusion(bf16[256,768]{1,0:T(8,128)(2,1)S(1)} %get-tuple-element.48, bf16[3,1536,768]{2,1,0:T(8,128)(2,1)} %param.11), kind=kOutput, calls=%fused_computation.36 | convolution fusion | flops 603979776 | bytes 4325376 | tf_op jit(solution)/shard_map/dot_general | solution.py:129
  59.8 5.1 %collective-permute-start.6 = (bf16[256,768]{1,0:T(8,128)(2,1)S(1)}, bf16[256,768]{1,0:T(8,128)(2,1)S(1)}, u32[]{:S(2)}, u32[]{:S(2)}) collective-permute-start(bf16[256,768]{1,0:T(8,128)(2,1)S(1)} %get-tuple-element.48), channel_id=1, source_target_pairs={{0,4},{2,6},{4,8},{6,10},{8,12},{10,14},{12,16},{14,18},{16,20},{1... | collective-permute-start | bytes 1179656 | tf_op jit(solution)/shard_map/ppermute | solution.py:22
  64.9 1.5 %collective-permute-start.7 = (bf16[256,768]{1,0:T(8,128)(2,1)S(1)}, bf16[256,768]{1,0:T(8,128)(2,1)S(1)}, u32[]{:S(2)}, u32[]{:S(2)}) collective-permute-start(bf16[256,768]{1,0:T(8,128)(2,1)S(1)} %get-tuple-element.48), channel_id=1, source_target_pairs={{4,0},{6,2},{8,4},{10,6},{12,8},{14,10},{16,12},{18,14},{20,16},{2... | collective-permute-start | bytes 1179656 | tf_op jit(solution)/shard_map/ppermute | solution.py:22
  67.2 15.2 %collective-permute-done.4 = bf16[256,768]{1,0:T(8,128)(2,1)S(1)} collective-permute-done((bf16[256,768]{1,0:T(8,128)(2,1)S(1)}, bf16[256,768]{1,0:T(8,128)(2,1)S(1)}, u32[]{:S(2)}, u32[]{:S(2)}) %collective-permute-start.4) | collective-permute-done | bytes 393248 | tf_op jit(solution)/shard_map/ppermute | solution.py:22
  83.8 1.7 %fusion.53 = f32[256,1536]{1,0:T(8,128)S(1)} fusion(f32[256,1536]{1,0:T(8,128)S(1)} %fusion.1, bf16[256,768]{1,0:T(8,128)(2,1)S(1)} %collective-permute-done.5, bf16[3,1536,768]{2,1,0:T(8,128)(2,1)S(1)} %bitcast.92, f32[256]{0:T(256)S(1)} %get-tuple-element.56, f32[256]{0:T(256)S(1)} %fusion.116, f32[1536]{0:T(1024)S(1)} %copy-done.11, ...), kind=kOutput, calls=%fused_computation.73 | convolution fusion | flops 613416960 | bytes 6694912 | tf_op jit(solution)/shard_map/dot_general | solution.py:133
  85.5 3.3 %collective-permute-done.6 = bf16[256,768]{1,0:T(8,128)(2,1)S(1)} collective-permute-done((bf16[256,768]{1,0:T(8,128)(2,1)S(1)}, bf16[256,768]{1,0:T(8,128)(2,1)S(1)}, u32[]{:S(2)}, u32[]{:S(2)}) %collective-permute-start.6) | collective-permute-done | bytes 393248 | tf_op jit(solution)/shard_map/ppermute | solution.py:22
  89.6 2.5 %fusion.47 = (f32[1536]{0:T(1024)S(1)}, f32[256]{0:T(256)S(1)}, f32[256]{0:T(256)S(1)}, f32[1536]{0:T(1024)S(1)}, f32[256,1536]{1,0:T(8,128)S(1)}) fusion(f32[256]{0:T(256)S(1)} %fusion.114, bf16[1,512,1536]{2,1,0:T(8,128)(2,1)S(1)} %copy-done.2, f32[1536]{0:T(1024)S(1)} %copy-done.11, f32[256,1536]{1,0:T(8,128)S(1)} %fusion.53, f32[256]{0:T(256)S(1)} %fusion.116, ...), kind=kOutput, calls=%fused_computation.67 | convolution fusion | flops 618131968 | bytes 9069568 | tf_op jit(solution)/shard_map/dot_general | solution.py:133
  92.3 2.5 %collective-permute-start.8 = (f32[2304]{0:T(1024)S(1)}, f32[2304]{0:T(1024)S(1)}, u32[]{:S(2)}, u32[]{:S(2)}) collective-permute-start(f32[2304]{0:T(1024)S(1)} %pad_maximum_fusion), channel_id=1, source_target_pairs={{0,2},{2,0},{4,6},{6,4},{8,10},{10,8},{12,14},{14,12},{16,18},{18,... | collective-permute-start | bytes 27656 | tf_op jit(solution)/shard_map/ppermute | solution.py:40
  98.5 3.3 %collective-permute-start.11 = (f32[2304]{0:T(1024)S(1)}, f32[2304]{0:T(1024)S(1)}, u32[]{:S(2)}, u32[]{:S(2)}) collective-permute-start(f32[2304]{0:T(1024)S(1)} %add_add_fusion.5), channel_id=1, source_target_pairs={{0,8},{2,10},{4,12},{6,14},{8,0},{10,2},{12,4},{14,6},{16,24},{18,... | collective-permute-start | bytes 27656 | tf_op jit(solution)/shard_map/ppermute | solution.py:40
  101.7 2.6 %collective-permute-start.12 = (f32[2304]{0:T(1024)S(1)}, f32[2304]{0:T(1024)S(1)}, u32[]{:S(2)}, u32[]{:S(2)}) collective-permute-start(f32[2304]{0:T(1024)S(1)} %add_add_fusion.5), channel_id=1, source_target_pairs={{0,16},{2,18},{4,20},{6,22},{8,24},{10,26},{12,28},{14,30},{16,0},... | collective-permute-start | bytes 27656 | tf_op jit(solution)/shard_map/ppermute | solution.py:40
  106.3 3.5 %collective-permute-done.13 = f32[2304]{0:T(1024)S(1)} collective-permute-done((f32[2304]{0:T(1024)S(1)}, f32[2304]{0:T(1024)S(1)}, u32[]{:S(2)}, u32[]{:S(2)}) %collective-permute-start.13) | collective-permute-done | bytes 9248 | tf_op jit(solution)/shard_map/ppermute | solution.py:40
  109.8 1.5 %collective-permute-start.14 = (f32[2304]{0:T(1024)S(1)}, f32[2304]{0:T(1024)S(1)}, u32[]{:S(2)}, u32[]{:S(2)}) collective-permute-start(f32[2304]{0:T(1024)S(1)} %add_add_fusion.4), channel_id=1, source_target_pairs={{0,1},{1,0},{2,3},{3,2},{4,5},{5,4},{6,7},{7,6},{8,9},{9,8},{10,11... | collective-permute-start | bytes 27656 | tf_op jit(solution)/shard_map/ppermute | solution.py:40
  (86 shorter events, 20.0 us)
Async XLA Ops:
  0.6 34.7 %copy-start = (bf16[768,1536]{1,0:T(8,128)(2,1)S(1)}, bf16[768,1536]{1,0:T(8,128)(2,1)}, u32[]{:S(2)}) copy-start(bf16[768,1536]{1,0:T(8,128)(2,1)} %param.13) | copy-start | bytes 7077892
  0.6 2.5 %copy-start.1 = (bf16[1,512,1536]{2,1,0:T(8,128)(2,1)S(1)}, bf16[1,512,1536]{2,1,0:T(8,128)(2,1)}, u32[]{:S(2)}) copy-start(bf16[1,512,1536]{2,1,0:T(8,128)(2,1)} %param.7) | copy-start | bytes 4718596
  0.7 2.5 %copy-start.11 = (f32[1536]{0:T(1024)S(1)}, f32[1536]{0:T(1024)}, u32[]{:S(2)}) copy-start(f32[1536]{0:T(1024)} %param.10) | copy-start | bytes 18436
  2.6 0.5 copy-start.14
  3.1 11.1 %copy-start.3 = (bf16[3,1536,768]{2,1,0:T(8,128)(2,1)S(1)}, bf16[3,1536,768]{2,1,0:T(8,128)(2,1)}, u32[]{:S(2)}) copy-start(bf16[3,1536,768]{2,1,0:T(8,128)(2,1)} %param.11) | copy-start | bytes 21233668
  4.5 18.6 %copy-start.7 = (bf16[256,1536]{1,0:T(8,128)(2,1)}, bf16[256,1536]{1,0:T(8,128)(2,1)S(1)}, u32[]{:S(2)}) copy-start(bf16[256,1536]{1,0:T(8,128)(2,1)S(1)} %get-tuple-element.47) | copy-start | bytes 2359300
  8.6 32.3 %collective-permute-start.2 = (bf16[256,768]{1,0:T(8,128)(2,1)}, bf16[256,768]{1,0:T(8,128)(2,1)}, u32[]{:S(2)}, u32[]{:S(2)}) collective-permute-start(bf16[256,768]{1,0:T(8,128)(2,1)} %fusion.81), channel_id=1, source_target_pairs={{0,4},{2,6},{4,8},{6,10},{8,12},{10,14},{12,16},{14,18},{16,20},{1... | collective-permute-start | bytes 1179656 | tf_op jit(solution)/shard_map/ppermute | solution.py:22
  15.7 25.2 %collective-permute-start.3 = (bf16[256,768]{1,0:T(8,128)(2,1)}, bf16[256,768]{1,0:T(8,128)(2,1)}, u32[]{:S(2)}, u32[]{:S(2)}) collective-permute-start(bf16[256,768]{1,0:T(8,128)(2,1)} %fusion.87), channel_id=1, source_target_pairs={{4,0},{6,2},{8,4},{10,6},{12,8},{14,10},{16,12},{18,14},{20,16},{2... | collective-permute-start | bytes 1179656 | tf_op jit(solution)/shard_map/ppermute | solution.py:22
  18.5 28.9 %collective-permute-start = (bf16[256,768]{1,0:T(8,128)(2,1)}, bf16[256,768]{1,0:T(8,128)(2,1)S(1)}, u32[]{:S(2)}, u32[]{:S(2)}) collective-permute-start(bf16[256,768]{1,0:T(8,128)(2,1)} %fusion.78), channel_id=1, source_target_pairs={{0,4},{2,6},{4,8},{6,10},{8,12},{10,14},{12,16},{14,18},{16,20},{1... | collective-permute-start | bytes 1179656 | tf_op jit(solution)/shard_map/ppermute | solution.py:22
  24.7 22.7 %collective-permute-start.1 = (bf16[256,768]{1,0:T(8,128)(2,1)}, bf16[256,768]{1,0:T(8,128)(2,1)}, u32[]{:S(2)}, u32[]{:S(2)}) collective-permute-start(bf16[256,768]{1,0:T(8,128)(2,1)} %fusion.84), channel_id=1, source_target_pairs={{4,0},{6,2},{8,4},{10,6},{12,8},{14,10},{16,12},{18,14},{20,16},{2... | collective-permute-start | bytes 1179656 | tf_op jit(solution)/shard_map/ppermute | solution.py:22
  29.3 3.4 %copy-start.8 = (bf16[256,1536]{1,0:T(8,128)(2,1)S(1)}, bf16[256,1536]{1,0:T(8,128)(2,1)}, u32[]{:S(2)}) copy-start(bf16[256,1536]{1,0:T(8,128)(2,1)} %copy-done.7) | copy-start | bytes 2359300
  32.7 2.6 %copy-start.4 = (bf16[1,512,1536]{2,1,0:T(8,128)(2,1)S(1)}, bf16[1,512,1536]{2,1,0:T(8,128)(2,1)}, u32[]{:S(2)}) copy-start(bf16[1,512,1536]{2,1,0:T(8,128)(2,1)} %param.8) | copy-start | bytes 4718596
  42.7 6.1 %copy-start.6 = (f32[256,768]{1,0:T(8,128)S(1)}, f32[256,768]{1,0:T(8,128)}, u32[]{:S(2)}) copy-start(f32[256,768]{1,0:T(8,128)} %fusion.106) | copy-start | bytes 2359300
  42.7 6.1 %copy-start.10 = (f32[768]{0:T(1024)S(1)}, f32[768]{0:T(1024)}, u32[]{:S(2)}) copy-start(f32[768]{0:T(1024)} %param.12) | copy-start | bytes 9220
  48.7 1.1 copy-start.9
  48.8 17.6 %slice-start = ((s8[7077888]{0:T(1024)(128)(4,1)}), s8[4194304]{0:T(1024)(128)(4,1)S(1)}, s32[]{:S(2)}) async-start(s8[7077888]{0:T(1024)(128)(4,1)} %bitcast.91), calls=%async_computation | async-start | bytes 8388608
  49.9 16.5 %slice-start.1 = ((s8[7077888]{0:T(1024)(128)(4,1)}), s8[2883584]{0:T(1024)(128)(4,1)S(1)}, s32[]{:S(2)}) async-start(s8[7077888]{0:T(1024)(128)(4,1)} %bitcast.91), calls=%async_computation.1 | async-start | bytes 5767168
  51.7 30.7 %collective-permute-start.4 = (bf16[256,768]{1,0:T(8,128)(2,1)S(1)}, bf16[256,768]{1,0:T(8,128)(2,1)S(1)}, u32[]{:S(2)}, u32[]{:S(2)}) collective-permute-start(bf16[256,768]{1,0:T(8,128)(2,1)S(1)} %get-tuple-element.50), channel_id=1, source_target_pairs={{0,4},{2,6},{4,8},{6,10},{8,12},{10,14},{12,16},{14,18},{16,20},{1... | collective-permute-start | bytes 1179656 | tf_op jit(solution)/shard_map/ppermute | solution.py:22
  56.0 26.4 %collective-permute-start.5 = (bf16[256,768]{1,0:T(8,128)(2,1)S(1)}, bf16[256,768]{1,0:T(8,128)(2,1)S(1)}, u32[]{:S(2)}, u32[]{:S(2)}) collective-permute-start(bf16[256,768]{1,0:T(8,128)(2,1)S(1)} %get-tuple-element.50), channel_id=1, source_target_pairs={{4,0},{6,2},{8,4},{10,6},{12,8},{14,10},{16,12},{18,14},{20,16},{2... | collective-permute-start | bytes 1179656 | tf_op jit(solution)/shard_map/ppermute | solution.py:22
  59.8 29.0 %collective-permute-start.6 = (bf16[256,768]{1,0:T(8,128)(2,1)S(1)}, bf16[256,768]{1,0:T(8,128)(2,1)S(1)}, u32[]{:S(2)}, u32[]{:S(2)}) collective-permute-start(bf16[256,768]{1,0:T(8,128)(2,1)S(1)} %get-tuple-element.48), channel_id=1, source_target_pairs={{0,4},{2,6},{4,8},{6,10},{8,12},{10,14},{12,16},{14,18},{16,20},{1... | collective-permute-start | bytes 1179656 | tf_op jit(solution)/shard_map/ppermute | solution.py:22
  64.9 24.7 %collective-permute-start.7 = (bf16[256,768]{1,0:T(8,128)(2,1)S(1)}, bf16[256,768]{1,0:T(8,128)(2,1)S(1)}, u32[]{:S(2)}, u32[]{:S(2)}) collective-permute-start(bf16[256,768]{1,0:T(8,128)(2,1)S(1)} %get-tuple-element.48), channel_id=1, source_target_pairs={{4,0},{6,2},{8,4},{10,6},{12,8},{14,10},{16,12},{18,14},{20,16},{2... | collective-permute-start | bytes 1179656 | tf_op jit(solution)/shard_map/ppermute | solution.py:22
  82.4 1.4 %copy-start.2 = (bf16[1,512,1536]{2,1,0:T(8,128)(2,1)S(1)}, bf16[1,512,1536]{2,1,0:T(8,128)(2,1)}, u32[]{:S(2)}) copy-start(bf16[1,512,1536]{2,1,0:T(8,128)(2,1)} %param.7) | copy-start | bytes 4718596
  92.1 3.5 %copy-start.13 = (f32[256]{0:T(256)S(1)}, f32[256]{0:T(256)}, u32[]{:S(2)}) copy-start(f32[256]{0:T(256)} %copy-done.12) | copy-start | bytes 3076
  92.1 3.5 %copy-start.15 = (f32[256]{0:T(256)S(1)}, f32[256]{0:T(256)}, u32[]{:S(2)}) copy-start(f32[256]{0:T(256)} %copy-done.14) | copy-start | bytes 3076
  92.1 3.5 %copy-start.5 = (bf16[1,512,1536]{2,1,0:T(8,128)(2,1)S(1)}, bf16[1,512,1536]{2,1,0:T(8,128)(2,1)}, u32[]{:S(2)}) copy-start(bf16[1,512,1536]{2,1,0:T(8,128)(2,1)} %param.8) | copy-start | bytes 4718596
  92.1 5.3 %collective-permute-start.10 = (f32[2304]{0:T(1024)S(1)}, f32[2304]{0:T(1024)S(1)}, u32[]{:S(2)}, u32[]{:S(2)}) collective-permute-start(f32[2304]{0:T(1024)S(1)} %pad_maximum_fusion), channel_id=1, source_target_pairs={{0,6},{2,4},{4,2},{6,0},{8,14},{10,12},{12,10},{14,8},{16,22},{18,... | collective-permute-start | bytes 27656 | tf_op jit(solution)/shard_map/ppermute | solution.py:40
  92.3 5.2 %collective-permute-start.8 = (f32[2304]{0:T(1024)S(1)}, f32[2304]{0:T(1024)S(1)}, u32[]{:S(2)}, u32[]{:S(2)}) collective-permute-start(f32[2304]{0:T(1024)S(1)} %pad_maximum_fusion), channel_id=1, source_target_pairs={{0,2},{2,0},{4,6},{6,4},{8,10},{10,8},{12,14},{14,12},{16,18},{18,... | collective-permute-start | bytes 27656 | tf_op jit(solution)/shard_map/ppermute | solution.py:40
  94.8 3.7 %collective-permute-start.9 = (f32[2304]{0:T(1024)S(1)}, f32[2304]{0:T(1024)S(1)}, u32[]{:S(2)}, u32[]{:S(2)}) collective-permute-start(f32[2304]{0:T(1024)S(1)} %pad_maximum_fusion), channel_id=1, source_target_pairs={{0,4},{2,6},{4,0},{6,2},{8,12},{10,14},{12,8},{14,10},{16,20},{18,... | collective-permute-start | bytes 27656 | tf_op jit(solution)/shard_map/ppermute | solution.py:40
  98.5 7.1 %collective-permute-start.11 = (f32[2304]{0:T(1024)S(1)}, f32[2304]{0:T(1024)S(1)}, u32[]{:S(2)}, u32[]{:S(2)}) collective-permute-start(f32[2304]{0:T(1024)S(1)} %add_add_fusion.5), channel_id=1, source_target_pairs={{0,8},{2,10},{4,12},{6,14},{8,0},{10,2},{12,4},{14,6},{16,24},{18,... | collective-permute-start | bytes 27656 | tf_op jit(solution)/shard_map/ppermute | solution.py:40
  101.7 4.6 %collective-permute-start.12 = (f32[2304]{0:T(1024)S(1)}, f32[2304]{0:T(1024)S(1)}, u32[]{:S(2)}, u32[]{:S(2)}) collective-permute-start(f32[2304]{0:T(1024)S(1)} %add_add_fusion.5), channel_id=1, source_target_pairs={{0,16},{2,18},{4,20},{6,22},{8,24},{10,26},{12,28},{14,30},{16,0},... | collective-permute-start | bytes 27656 | tf_op jit(solution)/shard_map/ppermute | solution.py:40
  104.3 5.5 %collective-permute-start.13 = (f32[2304]{0:T(1024)S(1)}, f32[2304]{0:T(1024)S(1)}, u32[]{:S(2)}, u32[]{:S(2)}) collective-permute-start(f32[2304]{0:T(1024)S(1)} %add_add_fusion.5), channel_id=1, source_target_pairs={{0,24},{2,26},{4,28},{6,30},{8,16},{10,18},{12,20},{14,22},{16,8},... | collective-permute-start | bytes 27656 | tf_op jit(solution)/shard_map/ppermute | solution.py:40
  109.8 3.7 %collective-permute-start.14 = (f32[2304]{0:T(1024)S(1)}, f32[2304]{0:T(1024)S(1)}, u32[]{:S(2)}, u32[]{:S(2)}) collective-permute-start(f32[2304]{0:T(1024)S(1)} %add_add_fusion.4), channel_id=1, source_target_pairs={{0,1},{1,0},{2,3},{3,2},{4,5},{5,4},{6,7},{7,6},{8,9},{9,8},{10,11... | collective-permute-start | bytes 27656 | tf_op jit(solution)/shard_map/ppermute | solution.py:40
  (1 other events, 0.5 us)

commit v4 on v3

--- a/solution.py
+++ b/solution.py
@@ -8,7 +8,7 @@
 SPAN = 2
 CHUNKS = (1, 1)
 AXES = ("seq", "batch")
-RADIX = 4
+STAGES = (2, 4, 4)
 EARLY = True
 LATE_OUTPUT = True
 
@@ -44,16 +44,21 @@
 
 
 def reduce_all(x):
-    axes = AXES
-    sizes = [lax.axis_size(a) for a in axes]
-    if any(s & (s - 1) for s in sizes):
+    axes = ("seq", "batch")
+    size = lax.axis_size(axes)
+    if size & (size - 1):
         return lax.psum(x, axes)
-    for axis, size in zip(axes, sizes):
-        stride = 1
-        while stride < size:
-            radix = min(RADIX, size // stride)
-            x = group_sum(x, axis, stride, radix)
-            stride *= radix
+    stride = 1
+    for radix in STAGES:
+        if stride >= size:
+            break
+        radix = min(radix, size // stride)
+        x = group_sum(x, axes, stride, radix)
+        stride *= radix
+    while stride < size:
+        radix = min(4, size // stride)
+        x = group_sum(x, axes, stride, radix)
+        stride *= radix
     return x
 
 

time: 115 us -> 115 us (level)
  no operation moved by 1% of the time
where the time goes in v4:
time: 115 us; the launch traced here: 114 us
  starting transfers between devices  34.6 us (30%)
  waiting for transfers between devices  29.1 us (25%)
  matrix products  28.7 us (25%)
  other arithmetic  19.3 us (17%)
  local copies, waits for them, and re-layouts  1.38 us (1%)
    ppermute x8, starting transfers between devices, shifted(): return lax.ppermute(x, axis, pairs)  24.9 us
    ppermute x8, waiting for transfers between devices, shifted(): return lax.ppermute(x, axis, pairs)  23.1 us
    ppermute x7, starting transfers between devices, group_sum(): parts.append(lax.ppermute(x, axis, pairs))  9.76 us
    dot_general x2, matrix products, body(): jnp.dot(ch['hidden'], tap_center, preferred_element_type=jnp.float32)  5.95 us
    ppermute x7, waiting for transfers between devices, group_sum(): parts.append(lax.ppermute(x, axis, pairs))  5.93 us
    dot_general x2, matrix products, body(): jnp.dot(hidden, tap_before, preferred_element_type=jnp.float32)  5.58 us
    reduce_sum x3, other arithmetic, norm_activate(): mean_square = jnp.mean(values * values, axis=-1, keepdims=True)  4.96 us
    dot_general x2, matrix products, body(): jnp.dot(ch['combined_after'], tap_before.T, preferred_element_type=jnp.fl...  4.15 us
  transfers between devices with their start and end apart: 15, of which 7 were waited for; matrix products, arithmetic and copies ran while one was open for 29% of the time, Pallas kernels for 0%

profile of v4, /device:TPU:0, one launch (start us, length us, event | category | flops | bytes accessed | tf_op | source)
XLA Modules:
  0.0 114.2 jit_solution(5073557271203290404)
XLA Ops:
  0.7 1.9 %fusion.60 = (f32[256]{0:T(256)S(1)}, f32[256]{0:T(256)S(1)}) fusion(bf16[1,512,1536]{2,1,0:T(8,128)(2,1)} %param.7), kind=kLoop, calls=%fused_computation.80 | loop fusion | flops 2358784 | bytes 1574912 | tf_op jit(solution)/shard_map/jvp()/reduce_sum | solution.py:26
  3.1 1.4 %fusion.38 = (bf16[256,1536]{1,0:T(8,128)(2,1)S(1)}, bf16[256,1536]{1,0:T(8,128)(2,1)S(1)}) fusion(f32[256]{0:T(256)S(1)} %fusion.116, f32[1536]{0:T(1024)S(1)} %copy-done.11, bf16[1,512,1536]{2,1,0:T(8,128)(2,1)S(1)} %copy-done.1, f32[256]{0:T(256)S(1)} %fusion.114), kind=kLoop, calls=%fused_computation.58 | loop fusion | flops 9437184 | bytes 3153920 | tf_op jit(solution)/shard_map/convert_element_type | solution.py:96
  4.5 4.0 %fusion.81 = bf16[256,768]{1,0:T(8,128)(2,1)} fusion(bf16[256,1536]{1,0:T(8,128)(2,1)S(1)} %get-tuple-element.46, bf16[3,1536,768]{2,1,0:T(8,128)(2,1)} %param.11), kind=kOutput, calls=%fused_computation.97 | convolution fusion | flops 604176384 | bytes 3538944 | tf_op jit(solution)/shard_map/dot_general | solution.py:97
  8.6 5.6 %collective-permute-start.2 = (bf16[256,768]{1,0:T(8,128)(2,1)}, bf16[256,768]{1,0:T(8,128)(2,1)}, u32[]{:S(2)}, u32[]{:S(2)}) collective-permute-start(bf16[256,768]{1,0:T(8,128)(2,1)} %fusion.81), channel_id=1, source_target_pairs={{0,4},{2,6},{4,8},{6,10},{8,12},{10,14},{12,16},{14,18},{16,20},{1... | collective-permute-start | bytes 1179656 | tf_op jit(solution)/shard_map/ppermute | solution.py:22
  14.2 1.5 %fusion.87 = bf16[256,768]{1,0:T(8,128)(2,1)} fusion(bf16[256,1536]{1,0:T(8,128)(2,1)S(1)} %get-tuple-element.46, bf16[3,1536,768]{2,1,0:T(8,128)(2,1)S(1)} %copy-done.3), kind=kOutput, calls=%fused_computation.99 | convolution fusion | flops 604176384 | bytes 3538944 | tf_op jit(solution)/shard_map/dot_general | solution.py:98
  15.7 1.3 %collective-permute-start.3 = (bf16[256,768]{1,0:T(8,128)(2,1)}, bf16[256,768]{1,0:T(8,128)(2,1)}, u32[]{:S(2)}, u32[]{:S(2)}) collective-permute-start(bf16[256,768]{1,0:T(8,128)(2,1)} %fusion.87), channel_id=1, source_target_pairs={{4,0},{6,2},{8,4},{10,6},{12,8},{14,10},{16,12},{18,14},{20,16},{2... | collective-permute-start | bytes 1179656 | tf_op jit(solution)/shard_map/ppermute | solution.py:22
  17.0 1.5 %fusion.78 = bf16[256,768]{1,0:T(8,128)(2,1)} fusion(bf16[256,1536]{1,0:T(8,128)(2,1)S(1)} %get-tuple-element.47, bf16[3,1536,768]{2,1,0:T(8,128)(2,1)S(1)} %copy-done.3), kind=kOutput, calls=%fused_computation.96 | convolution fusion | flops 604176384 | bytes 3538944 | tf_op jit(solution)/shard_map/dot_general | solution.py:97
  18.5 4.6 %collective-permute-start = (bf16[256,768]{1,0:T(8,128)(2,1)}, bf16[256,768]{1,0:T(8,128)(2,1)S(1)}, u32[]{:S(2)}, u32[]{:S(2)}) collective-permute-start(bf16[256,768]{1,0:T(8,128)(2,1)} %fusion.78), channel_id=1, source_target_pairs={{0,4},{2,6},{4,8},{6,10},{8,12},{10,14},{12,16},{14,18},{16,20},{1... | collective-permute-start | bytes 1179656 | tf_op jit(solution)/shard_map/ppermute | solution.py:22
  23.1 1.6 %fusion.84 = bf16[256,768]{1,0:T(8,128)(2,1)} fusion(bf16[256,1536]{1,0:T(8,128)(2,1)S(1)} %get-tuple-element.47, bf16[3,1536,768]{2,1,0:T(8,128)(2,1)S(1)} %copy-done.3), kind=kOutput, calls=%fused_computation.98 | convolution fusion | flops 604176384 | bytes 3538944 | tf_op jit(solution)/shard_map/dot_general | solution.py:98
  29.3 3.4 %fusion.22 = f32[256,768]{1,0:T(8,128)} fusion(bf16[256,1536]{1,0:T(8,128)(2,1)S(1)} %get-tuple-element.46, bf16[3,1536,768]{2,1,0:T(8,128)(2,1)} %param.11), kind=kOutput, calls=%fused_computation.38 | convolution fusion | flops 603979776 | bytes 3932160 | tf_op jit(solution)/shard_map/dot_general | solution.py:106
  32.7 2.6 %fusion.24 = f32[256,768]{1,0:T(8,128)S(1)} fusion(bf16[256,1536]{1,0:T(8,128)(2,1)S(1)} %copy-done.8, bf16[3,1536,768]{2,1,0:T(8,128)(2,1)} %param.11), kind=kOutput, calls=%fused_computation.40 | convolution fusion | flops 603979776 | bytes 3932160 | tf_op jit(solution)/shard_map/dot_general | solution.py:106
  35.3 1.7 %fusion.104 = f32[256,768]{1,0:T(8,128)} fusion(bf16[768,1536]{1,0:T(8,128)(2,1)S(1)} %copy-done, bf16[1,512,1536]{2,1,0:T(8,128)(2,1)S(1)} %copy-done.4), kind=kOutput, calls=%fused_computation.120 | convolution fusion | flops 603979776 | bytes 3932160 | tf_op jit(solution)/shard_map/dot_general | solution.py:107
  37.0 1.7 %fusion.106 = f32[256,768]{1,0:T(8,128)} fusion(bf16[768,1536]{1,0:T(8,128)(2,1)S(1)} %copy-done, bf16[1,512,1536]{2,1,0:T(8,128)(2,1)S(1)} %copy-done.4), kind=kOutput, calls=%fused_computation.122 | convolution fusion | flops 603979776 | bytes 3932160 | tf_op jit(solution)/shard_map/dot_general | solution.py:107
  38.7 1.3 %reduce-window.8 = s32[4,1]{0,1:T(1,128)} reduce-window(s32[4,1]{0,1:T(1,128)} %bitcast.94, s32[]{:T(128)} %constant.60.clone.1), window={size=4x1 pad=3_0x0_0}, to_apply=%region_1.2 | reduce-window | flops 12 | bytes 36 | tf_op jit(solution)/shard_map/reduce-window.3
  41.0 1.7 %multiply_reduce_fusion.4 = (f32[256]{0:T(256)S(1)}, f32[256,768]{1,0:T(8,128)S(1)}) fusion(bf16[256,768]{1,0:T(8,128)(2,1)} %collective-permute-done.3, f32[256]{0:T(256)S(1)} %get-tuple-element.56, f32[256,768]{1,0:T(8,128)} %fusion.22, bf16[256,768]{1,0:T(8,128)(2,1)} %collective-permute-done.2, f32[256]{0:T(256)S(1)} %get-tuple-element.55), kind=kLoop, calls=%fused_computation.129 | loop fusion | flops 1572608 | bytes 2362368 | tf_op jit(solution)/shard_map/jvp()/reduce_sum | solution.py:26
  42.7 4.7 %collective-permute-done = bf16[256,768]{1,0:T(8,128)(2,1)S(1)} collective-permute-done((bf16[256,768]{1,0:T(8,128)(2,1)}, bf16[256,768]{1,0:T(8,128)(2,1)S(1)}, u32[]{:S(2)}, u32[]{:S(2)}) %collective-permute-start) | collective-permute-done | bytes 393248 | tf_op jit(solution)/shard_map/ppermute | solution.py:22
  47.4 1.4 %multiply_reduce_fusion.5 = (f32[256]{0:T(256)S(1)}, f32[256,768]{1,0:T(8,128)S(1)}) fusion(bf16[256,768]{1,0:T(8,128)(2,1)} %collective-permute-done.1, f32[256]{0:T(256)S(1)} %get-tuple-element.58, f32[256,768]{1,0:T(8,128)S(1)} %fusion.24, bf16[256,768]{1,0:T(8,128)(2,1)S(1)} %collective-permute-done, f32[256]{0:T(256)S(1)} %get-tuple-element.57), kind=kLoop, calls=%fused_computation.132 | loop fusion | flops 1572608 | bytes 2362368 | tf_op jit(solution)/shard_map/jvp()/reduce_sum | solution.py:26
  51.7 4.3 %collective-permute-start.4 = (bf16[256,768]{1,0:T(8,128)(2,1)S(1)}, bf16[256,768]{1,0:T(8,128)(2,1)S(1)}, u32[]{:S(2)}, u32[]{:S(2)}) collective-permute-start(bf16[256,768]{1,0:T(8,128)(2,1)S(1)} %get-tuple-element.50), channel_id=1, source_target_pairs={{0,4},{2,6},{4,8},{6,10},{8,12},{10,14},{12,16},{14,18},{16,20},{1... | collective-permute-start | bytes 1179656 | tf_op jit(solution)/shard_map/ppermute | solution.py:22
  56.0 1.3 %collective-permute-start.5 = (bf16[256,768]{1,0:T(8,128)(2,1)S(1)}, bf16[256,768]{1,0:T(8,128)(2,1)S(1)}, u32[]{:S(2)}, u32[]{:S(2)}) collective-permute-start(bf16[256,768]{1,0:T(8,128)(2,1)S(1)} %get-tuple-element.50), channel_id=1, source_target_pairs={{4,0},{6,2},{8,4},{10,6},{12,8},{14,10},{16,12},{18,14},{20,16},{2... | collective-permute-start | bytes 1179656 | tf_op jit(solution)/shard_map/ppermute | solution.py:22
  57.3 2.5 %fusion.20 = f32[256,1536]{1,0:T(8,128)S(1)} fusion(bf16[256,768]{1,0:T(8,128)(2,1)S(1)} %get-tuple-element.48, bf16[3,1536,768]{2,1,0:T(8,128)(2,1)} %param.11), kind=kOutput, calls=%fused_computation.36 | convolution fusion | flops 603979776 | bytes 4325376 | tf_op jit(solution)/shard_map/dot_general | solution.py:134
  59.8 5.1 %collective-permute-start.6 = (bf16[256,768]{1,0:T(8,128)(2,1)S(1)}, bf16[256,768]{1,0:T(8,128)(2,1)S(1)}, u32[]{:S(2)}, u32[]{:S(2)}) collective-permute-start(bf16[256,768]{1,0:T(8,128)(2,1)S(1)} %get-tuple-element.48), channel_id=1, source_target_pairs={{0,4},{2,6},{4,8},{6,10},{8,12},{10,14},{12,16},{14,18},{16,20},{1... | collective-permute-start | bytes 1179656 | tf_op jit(solution)/shard_map/ppermute | solution.py:22
  64.8 1.5 %collective-permute-start.7 = (bf16[256,768]{1,0:T(8,128)(2,1)S(1)}, bf16[256,768]{1,0:T(8,128)(2,1)S(1)}, u32[]{:S(2)}, u32[]{:S(2)}) collective-permute-start(bf16[256,768]{1,0:T(8,128)(2,1)S(1)} %get-tuple-element.48), channel_id=1, source_target_pairs={{4,0},{6,2},{8,4},{10,6},{12,8},{14,10},{16,12},{18,14},{20,16},{2... | collective-permute-start | bytes 1179656 | tf_op jit(solution)/shard_map/ppermute | solution.py:22
  67.2 15.2 %collective-permute-done.4 = bf16[256,768]{1,0:T(8,128)(2,1)S(1)} collective-permute-done((bf16[256,768]{1,0:T(8,128)(2,1)S(1)}, bf16[256,768]{1,0:T(8,128)(2,1)S(1)}, u32[]{:S(2)}, u32[]{:S(2)}) %collective-permute-start.4) | collective-permute-done | bytes 393248 | tf_op jit(solution)/shard_map/ppermute | solution.py:22
  83.8 1.7 %fusion.53 = f32[256,1536]{1,0:T(8,128)S(1)} fusion(f32[256,1536]{1,0:T(8,128)S(1)} %fusion.1, bf16[256,768]{1,0:T(8,128)(2,1)S(1)} %collective-permute-done.5, bf16[3,1536,768]{2,1,0:T(8,128)(2,1)S(1)} %bitcast.92, f32[256]{0:T(256)S(1)} %get-tuple-element.56, f32[256]{0:T(256)S(1)} %fusion.116, f32[1536]{0:T(1024)S(1)} %copy-done.11, ...), kind=kOutput, calls=%fused_computation.73 | convolution fusion | flops 613416960 | bytes 6694912 | tf_op jit(solution)/shard_map/dot_general | solution.py:138
  85.4 3.3 %collective-permute-done.6 = bf16[256,768]{1,0:T(8,128)(2,1)S(1)} collective-permute-done((bf16[256,768]{1,0:T(8,128)(2,1)S(1)}, bf16[256,768]{1,0:T(8,128)(2,1)S(1)}, u32[]{:S(2)}, u32[]{:S(2)}) %collective-permute-start.6) | collective-permute-done | bytes 393248 | tf_op jit(solution)/shard_map/ppermute | solution.py:22
  89.6 2.5 %fusion.47 = (f32[1536]{0:T(1024)S(1)}, f32[256]{0:T(256)S(1)}, f32[256]{0:T(256)S(1)}, f32[1536]{0:T(1024)S(1)}, f32[256,1536]{1,0:T(8,128)S(1)}) fusion(f32[256]{0:T(256)S(1)} %fusion.114, bf16[1,512,1536]{2,1,0:T(8,128)(2,1)S(1)} %copy-done.2, f32[1536]{0:T(1024)S(1)} %copy-done.11, f32[256,1536]{1,0:T(8,128)S(1)} %fusion.53, f32[256]{0:T(256)S(1)} %fusion.116, ...), kind=kOutput, calls=%fused_computation.67 | convolution fusion | flops 618131968 | bytes 9069568 | tf_op jit(solution)/shard_map/dot_general | solution.py:138
  92.1 1.6 %collective-permute-start.8 = (f32[2304]{0:T(1024)S(1)}, f32[2304]{0:T(1024)S(1)}, u32[]{:S(2)}, u32[]{:S(2)}) collective-permute-start(f32[2304]{0:T(1024)S(1)} %pad_maximum_fusion), channel_id=1, source_target_pairs={{0,1},{1,0},{2,3},{3,2},{4,5},{5,4},{6,7},{7,6},{8,9},{9,8},{10,11... | collective-permute-start | bytes 27656 | tf_op jit(solution)/shard_map/ppermute | solution.py:40
  96.4 2.6 %collective-permute-start.10 = (f32[2304]{0:T(1024)S(1)}, f32[2304]{0:T(1024)S(1)}, u32[]{:S(2)}, u32[]{:S(2)}) collective-permute-start(f32[2304]{0:T(1024)S(1)} %fusion.118), channel_id=1, source_target_pairs={{0,4},{1,5},{2,6},{3,7},{4,0},{5,1},{6,2},{7,3},{8,12},{9,13},{10,... | collective-permute-start | bytes 27656 | tf_op jit(solution)/shard_map/ppermute | solution.py:40
  100.6 1.4 %collective-permute-done.11 = f32[2304]{0:T(1024)S(1)} collective-permute-done((f32[2304]{0:T(1024)S(1)}, f32[2304]{0:T(1024)S(1)}, u32[]{:S(2)}, u32[]{:S(2)}) %collective-permute-start.11) | collective-permute-done | bytes 9248 | tf_op jit(solution)/shard_map/ppermute | solution.py:40
  102.0 2.8 %collective-permute-start.12 = (f32[2304]{0:T(1024)S(1)}, f32[2304]{0:T(1024)S(1)}, u32[]{:S(2)}, u32[]{:S(2)}) collective-permute-start(f32[2304]{0:T(1024)S(1)} %add_add_fusion.5), channel_id=1, source_target_pairs={{0,8},{1,9},{2,10},{3,11},{4,12},{5,13},{6,14},{7,15},{8,0},{9,1},... | collective-permute-start | bytes 27656 | tf_op jit(solution)/shard_map/ppermute | solution.py:40
  104.9 2.6 %collective-permute-start.13 = (f32[2304]{0:T(1024)S(1)}, f32[2304]{0:T(1024)S(1)}, u32[]{:S(2)}, u32[]{:S(2)}) collective-permute-start(f32[2304]{0:T(1024)S(1)} %add_add_fusion.5), channel_id=1, source_target_pairs={{0,16},{1,17},{2,18},{3,19},{4,20},{5,21},{6,22},{7,23},{8,24},{9,... | collective-permute-start | bytes 27656 | tf_op jit(solution)/shard_map/ppermute | solution.py:40
  109.5 3.5 %collective-permute-done.14 = f32[2304]{0:T(1024)S(1)} collective-permute-done((f32[2304]{0:T(1024)S(1)}, f32[2304]{0:T(1024)S(1)}, u32[]{:S(2)}, u32[]{:S(2)}) %collective-permute-start.14) | collective-permute-done | bytes 9248 | tf_op jit(solution)/shard_map/ppermute | solution.py:40
  (86 shorter events, 19.5 us)
Async XLA Ops:
  0.6 34.7 %copy-start = (bf16[768,1536]{1,0:T(8,128)(2,1)S(1)}, bf16[768,1536]{1,0:T(8,128)(2,1)}, u32[]{:S(2)}) copy-start(bf16[768,1536]{1,0:T(8,128)(2,1)} %param.13) | copy-start | bytes 7077892
  0.6 2.5 %copy-start.1 = (bf16[1,512,1536]{2,1,0:T(8,128)(2,1)S(1)}, bf16[1,512,1536]{2,1,0:T(8,128)(2,1)}, u32[]{:S(2)}) copy-start(bf16[1,512,1536]{2,1,0:T(8,128)(2,1)} %param.7) | copy-start | bytes 4718596
  0.7 2.5 %copy-start.11 = (f32[1536]{0:T(1024)S(1)}, f32[1536]{0:T(1024)}, u32[]{:S(2)}) copy-start(f32[1536]{0:T(1024)} %param.10) | copy-start | bytes 18436
  2.6 0.5 copy-start.14
  3.1 11.1 %copy-start.3 = (bf16[3,1536,768]{2,1,0:T(8,128)(2,1)S(1)}, bf16[3,1536,768]{2,1,0:T(8,128)(2,1)}, u32[]{:S(2)}) copy-start(bf16[3,1536,768]{2,1,0:T(8,128)(2,1)} %param.11) | copy-start | bytes 21233668
  4.5 18.6 %copy-start.7 = (bf16[256,1536]{1,0:T(8,128)(2,1)}, bf16[256,1536]{1,0:T(8,128)(2,1)S(1)}, u32[]{:S(2)}) copy-start(bf16[256,1536]{1,0:T(8,128)(2,1)S(1)} %get-tuple-element.47) | copy-start | bytes 2359300
  8.6 32.3 %collective-permute-start.2 = (bf16[256,768]{1,0:T(8,128)(2,1)}, bf16[256,768]{1,0:T(8,128)(2,1)}, u32[]{:S(2)}, u32[]{:S(2)}) collective-permute-start(bf16[256,768]{1,0:T(8,128)(2,1)} %fusion.81), channel_id=1, source_target_pairs={{0,4},{2,6},{4,8},{6,10},{8,12},{10,14},{12,16},{14,18},{16,20},{1... | collective-permute-start | bytes 1179656 | tf_op jit(solution)/shard_map/ppermute | solution.py:22
  15.7 25.2 %collective-permute-start.3 = (bf16[256,768]{1,0:T(8,128)(2,1)}, bf16[256,768]{1,0:T(8,128)(2,1)}, u32[]{:S(2)}, u32[]{:S(2)}) collective-permute-start(bf16[256,768]{1,0:T(8,128)(2,1)} %fusion.87), channel_id=1, source_target_pairs={{4,0},{6,2},{8,4},{10,6},{12,8},{14,10},{16,12},{18,14},{20,16},{2... | collective-permute-start | bytes 1179656 | tf_op jit(solution)/shard_map/ppermute | solution.py:22
  18.5 28.9 %collective-permute-start = (bf16[256,768]{1,0:T(8,128)(2,1)}, bf16[256,768]{1,0:T(8,128)(2,1)S(1)}, u32[]{:S(2)}, u32[]{:S(2)}) collective-permute-start(bf16[256,768]{1,0:T(8,128)(2,1)} %fusion.78), channel_id=1, source_target_pairs={{0,4},{2,6},{4,8},{6,10},{8,12},{10,14},{12,16},{14,18},{16,20},{1... | collective-permute-start | bytes 1179656 | tf_op jit(solution)/shard_map/ppermute | solution.py:22
  24.7 22.7 %collective-permute-start.1 = (bf16[256,768]{1,0:T(8,128)(2,1)}, bf16[256,768]{1,0:T(8,128)(2,1)}, u32[]{:S(2)}, u32[]{:S(2)}) collective-permute-start(bf16[256,768]{1,0:T(8,128)(2,1)} %fusion.84), channel_id=1, source_target_pairs={{4,0},{6,2},{8,4},{10,6},{12,8},{14,10},{16,12},{18,14},{20,16},{2... | collective-permute-start | bytes 1179656 | tf_op jit(solution)/shard_map/ppermute | solution.py:22
  29.3 3.4 %copy-start.8 = (bf16[256,1536]{1,0:T(8,128)(2,1)S(1)}, bf16[256,1536]{1,0:T(8,128)(2,1)}, u32[]{:S(2)}) copy-start(bf16[256,1536]{1,0:T(8,128)(2,1)} %copy-done.7) | copy-start | bytes 2359300
  32.7 2.6 %copy-start.4 = (bf16[1,512,1536]{2,1,0:T(8,128)(2,1)S(1)}, bf16[1,512,1536]{2,1,0:T(8,128)(2,1)}, u32[]{:S(2)}) copy-start(bf16[1,512,1536]{2,1,0:T(8,128)(2,1)} %param.8) | copy-start | bytes 4718596
  42.7 6.1 %copy-start.6 = (f32[256,768]{1,0:T(8,128)S(1)}, f32[256,768]{1,0:T(8,128)}, u32[]{:S(2)}) copy-start(f32[256,768]{1,0:T(8,128)} %fusion.106) | copy-start | bytes 2359300
  42.7 6.1 %copy-start.10 = (f32[768]{0:T(1024)S(1)}, f32[768]{0:T(1024)}, u32[]{:S(2)}) copy-start(f32[768]{0:T(1024)} %param.12) | copy-start | bytes 9220
  48.7 1.1 copy-start.9
  48.8 17.6 %slice-start = ((s8[7077888]{0:T(1024)(128)(4,1)}), s8[4194304]{0:T(1024)(128)(4,1)S(1)}, s32[]{:S(2)}) async-start(s8[7077888]{0:T(1024)(128)(4,1)} %bitcast.91), calls=%async_computation | async-start | bytes 8388608
  49.9 16.5 %slice-start.1 = ((s8[7077888]{0:T(1024)(128)(4,1)}), s8[2883584]{0:T(1024)(128)(4,1)S(1)}, s32[]{:S(2)}) async-start(s8[7077888]{0:T(1024)(128)(4,1)} %bitcast.91), calls=%async_computation.1 | async-start | bytes 5767168
  51.7 30.7 %collective-permute-start.4 = (bf16[256,768]{1,0:T(8,128)(2,1)S(1)}, bf16[256,768]{1,0:T(8,128)(2,1)S(1)}, u32[]{:S(2)}, u32[]{:S(2)}) collective-permute-start(bf16[256,768]{1,0:T(8,128)(2,1)S(1)} %get-tuple-element.50), channel_id=1, source_target_pairs={{0,4},{2,6},{4,8},{6,10},{8,12},{10,14},{12,16},{14,18},{16,20},{1... | collective-permute-start | bytes 1179656 | tf_op jit(solution)/shard_map/ppermute | solution.py:22
  56.0 26.4 %collective-permute-start.5 = (bf16[256,768]{1,0:T(8,128)(2,1)S(1)}, bf16[256,768]{1,0:T(8,128)(2,1)S(1)}, u32[]{:S(2)}, u32[]{:S(2)}) collective-permute-start(bf16[256,768]{1,0:T(8,128)(2,1)S(1)} %get-tuple-element.50), channel_id=1, source_target_pairs={{4,0},{6,2},{8,4},{10,6},{12,8},{14,10},{16,12},{18,14},{20,16},{2... | collective-permute-start | bytes 1179656 | tf_op jit(solution)/shard_map/ppermute | solution.py:22
  59.8 29.0 %collective-permute-start.6 = (bf16[256,768]{1,0:T(8,128)(2,1)S(1)}, bf16[256,768]{1,0:T(8,128)(2,1)S(1)}, u32[]{:S(2)}, u32[]{:S(2)}) collective-permute-start(bf16[256,768]{1,0:T(8,128)(2,1)S(1)} %get-tuple-element.48), channel_id=1, source_target_pairs={{0,4},{2,6},{4,8},{6,10},{8,12},{10,14},{12,16},{14,18},{16,20},{1... | collective-permute-start | bytes 1179656 | tf_op jit(solution)/shard_map/ppermute | solution.py:22
  64.8 24.7 %collective-permute-start.7 = (bf16[256,768]{1,0:T(8,128)(2,1)S(1)}, bf16[256,768]{1,0:T(8,128)(2,1)S(1)}, u32[]{:S(2)}, u32[]{:S(2)}) collective-permute-start(bf16[256,768]{1,0:T(8,128)(2,1)S(1)} %get-tuple-element.48), channel_id=1, source_target_pairs={{4,0},{6,2},{8,4},{10,6},{12,8},{14,10},{16,12},{18,14},{20,16},{2... | collective-permute-start | bytes 1179656 | tf_op jit(solution)/shard_map/ppermute | solution.py:22
  82.4 1.4 %copy-start.2 = (bf16[1,512,1536]{2,1,0:T(8,128)(2,1)S(1)}, bf16[1,512,1536]{2,1,0:T(8,128)(2,1)}, u32[]{:S(2)}) copy-start(bf16[1,512,1536]{2,1,0:T(8,128)(2,1)} %param.7) | copy-start | bytes 4718596
  92.1 2.4 %copy-start.13 = (f32[256]{0:T(256)S(1)}, f32[256]{0:T(256)}, u32[]{:S(2)}) copy-start(f32[256]{0:T(256)} %copy-done.12) | copy-start | bytes 3076
  92.1 2.4 %copy-start.15 = (f32[256]{0:T(256)S(1)}, f32[256]{0:T(256)}, u32[]{:S(2)}) copy-start(f32[256]{0:T(256)} %copy-done.14) | copy-start | bytes 3076
  92.1 2.4 %copy-start.5 = (bf16[1,512,1536]{2,1,0:T(8,128)(2,1)S(1)}, bf16[1,512,1536]{2,1,0:T(8,128)(2,1)}, u32[]{:S(2)}) copy-start(bf16[1,512,1536]{2,1,0:T(8,128)(2,1)} %param.8) | copy-start | bytes 4718596
  92.1 4.2 %collective-permute-start.8 = (f32[2304]{0:T(1024)S(1)}, f32[2304]{0:T(1024)S(1)}, u32[]{:S(2)}, u32[]{:S(2)}) collective-permute-start(f32[2304]{0:T(1024)S(1)} %pad_maximum_fusion), channel_id=1, source_target_pairs={{0,1},{1,0},{2,3},{3,2},{4,5},{5,4},{6,7},{7,6},{8,9},{9,8},{10,11... | collective-permute-start | bytes 27656 | tf_op jit(solution)/shard_map/ppermute | solution.py:40
  96.4 4.2 %collective-permute-start.10 = (f32[2304]{0:T(1024)S(1)}, f32[2304]{0:T(1024)S(1)}, u32[]{:S(2)}, u32[]{:S(2)}) collective-permute-start(f32[2304]{0:T(1024)S(1)} %fusion.118), channel_id=1, source_target_pairs={{0,4},{1,5},{2,6},{3,7},{4,0},{5,1},{6,2},{7,3},{8,12},{9,13},{10,... | collective-permute-start | bytes 27656 | tf_op jit(solution)/shard_map/ppermute | solution.py:40
  98.9 3.1 %collective-permute-start.11 = (f32[2304]{0:T(1024)S(1)}, f32[2304]{0:T(1024)S(1)}, u32[]{:S(2)}, u32[]{:S(2)}) collective-permute-start(f32[2304]{0:T(1024)S(1)} %fusion.118), channel_id=1, source_target_pairs={{0,6},{1,7},{2,4},{3,5},{4,2},{5,3},{6,0},{7,1},{8,14},{9,15},{10,... | collective-permute-start | bytes 27656 | tf_op jit(solution)/shard_map/ppermute | solution.py:40
  98.9 3.1 %collective-permute-start.9 = (f32[2304]{0:T(1024)S(1)}, f32[2304]{0:T(1024)S(1)}, u32[]{:S(2)}, u32[]{:S(2)}) collective-permute-start(f32[2304]{0:T(1024)S(1)} %fusion.118), channel_id=1, source_target_pairs={{0,2},{1,3},{2,0},{3,1},{4,6},{5,7},{6,4},{7,5},{8,10},{9,11},{10,... | collective-permute-start | bytes 27656 | tf_op jit(solution)/shard_map/ppermute | solution.py:40
  102.0 6.7 %collective-permute-start.12 = (f32[2304]{0:T(1024)S(1)}, f32[2304]{0:T(1024)S(1)}, u32[]{:S(2)}, u32[]{:S(2)}) collective-permute-start(f32[2304]{0:T(1024)S(1)} %add_add_fusion.5), channel_id=1, source_target_pairs={{0,8},{1,9},{2,10},{3,11},{4,12},{5,13},{6,14},{7,15},{8,0},{9,1},... | collective-permute-start | bytes 27656 | tf_op jit(solution)/shard_map/ppermute | solution.py:40
  104.9 4.6 %collective-permute-start.13 = (f32[2304]{0:T(1024)S(1)}, f32[2304]{0:T(1024)S(1)}, u32[]{:S(2)}, u32[]{:S(2)}) collective-permute-start(f32[2304]{0:T(1024)S(1)} %add_add_fusion.5), channel_id=1, source_target_pairs={{0,16},{1,17},{2,18},{3,19},{4,20},{5,21},{6,22},{7,23},{8,24},{9,... | collective-permute-start | bytes 27656 | tf_op jit(solution)/shard_map/ppermute | solution.py:40
  107.5 5.5 %collective-permute-start.14 = (f32[2304]{0:T(1024)S(1)}, f32[2304]{0:T(1024)S(1)}, u32[]{:S(2)}, u32[]{:S(2)}) collective-permute-start(f32[2304]{0:T(1024)S(1)} %add_add_fusion.5), channel_id=1, source_target_pairs={{0,24},{1,25},{2,26},{3,27},{4,28},{5,29},{6,30},{7,31},{8,16},{9,... | collective-permute-start | bytes 27656 | tf_op jit(solution)/shard_map/ppermute | solution.py:40
  (1 other events, 0.5 us)

commit v5 on v4

--- a/solution.py
+++ b/solution.py
@@ -48,17 +48,18 @@
     size = lax.axis_size(axes)
     if size & (size - 1):
         return lax.psum(x, axes)
-    stride = 1
+    stride, stages = 1, []
     for radix in STAGES:
-        if stride >= size:
-            break
-        radix = min(radix, size // stride)
-        x = group_sum(x, axes, stride, radix)
-        stride *= radix
+        if stride < size:
+            radix = min(radix, size // stride)
+            stages.append((stride, radix))
+            stride *= radix
     while stride < size:
         radix = min(4, size // stride)
+        stages.append((stride, radix))
+        stride *= radix
+    for stride, radix in reversed(stages):
         x = group_sum(x, axes, stride, radix)
-        stride *= radix
     return x
 
 

time: 115 us -> 113 us (0.983)
  waiting for transfers between devices: 29.1 us -> 26.1 us
  starting transfers between devices: 34.6 us -> 35.8 us
    ppermute x7, waiting for transfers between devices: 5.93 us -> 2.99 us  [group_sum(): parts.append(lax.ppermute(x, axis, pairs))]
where the time goes in v5:
time: 113 us; the launch traced here: 112 us
  starting transfers between devices  35.8 us (32%)
  matrix products  28.7 us (25%)
  waiting for transfers between devices  26.1 us (23%)
  other arithmetic  19.3 us (17%)
  local copies, waits for them, and re-layouts  1.36 us (1%)
    ppermute x8, starting transfers between devices, shifted(): return lax.ppermute(x, axis, pairs)  24.9 us
    ppermute x8, waiting for transfers between devices, shifted(): return lax.ppermute(x, axis, pairs)  23.1 us
    ppermute x7, starting transfers between devices, group_sum(): parts.append(lax.ppermute(x, axis, pairs))  10.9 us
    dot_general x2, matrix products, body(): jnp.dot(ch['hidden'], tap_center, preferred_element_type=jnp.float32)  5.95 us
    dot_general x2, matrix products, body(): jnp.dot(hidden, tap_before, preferred_element_type=jnp.float32)  5.58 us
    reduce_sum x3, other arithmetic, norm_activate(): mean_square = jnp.mean(values * values, axis=-1, keepdims=True)  4.96 us
    dot_general x2, matrix products, body(): jnp.dot(ch['combined_after'], tap_before.T, preferred_element_type=jnp.fl...  4.17 us
    dot_general x2, matrix products, body(): jnp.dot(ch['upstream'], point_weights.T, preferred_element_type=jnp.float32)  3.42 us
  transfers between devices with their start and end apart: 15, of which 7 were waited for; matrix products, arithmetic and copies ran while one was open for 29% of the time, Pallas kernels for 0%

profile of v5, /device:TPU:0, one launch (start us, length us, event | category | flops | bytes accessed | tf_op | source)
XLA Modules:
  0.0 112.4 jit_solution(6937716850852618049)
XLA Ops:
  0.7 1.9 %fusion.60 = (f32[256]{0:T(256)S(1)}, f32[256]{0:T(256)S(1)}) fusion(bf16[1,512,1536]{2,1,0:T(8,128)(2,1)} %param.7), kind=kLoop, calls=%fused_computation.80 | loop fusion | flops 2358784 | bytes 1574912 | tf_op jit(solution)/shard_map/jvp()/reduce_sum | solution.py:26
  3.1 1.4 %fusion.38 = (bf16[256,1536]{1,0:T(8,128)(2,1)S(1)}, bf16[256,1536]{1,0:T(8,128)(2,1)S(1)}) fusion(f32[256]{0:T(256)S(1)} %fusion.116, f32[1536]{0:T(1024)S(1)} %copy-done.11, bf16[1,512,1536]{2,1,0:T(8,128)(2,1)S(1)} %copy-done.1, f32[256]{0:T(256)S(1)} %fusion.114), kind=kLoop, calls=%fused_computation.58 | loop fusion | flops 9437184 | bytes 3153920 | tf_op jit(solution)/shard_map/convert_element_type | solution.py:97
  4.5 4.0 %fusion.81 = bf16[256,768]{1,0:T(8,128)(2,1)} fusion(bf16[256,1536]{1,0:T(8,128)(2,1)S(1)} %get-tuple-element.46, bf16[3,1536,768]{2,1,0:T(8,128)(2,1)} %param.11), kind=kOutput, calls=%fused_computation.97 | convolution fusion | flops 604176384 | bytes 3538944 | tf_op jit(solution)/shard_map/dot_general | solution.py:98
  8.6 5.6 %collective-permute-start.2 = (bf16[256,768]{1,0:T(8,128)(2,1)}, bf16[256,768]{1,0:T(8,128)(2,1)}, u32[]{:S(2)}, u32[]{:S(2)}) collective-permute-start(bf16[256,768]{1,0:T(8,128)(2,1)} %fusion.81), channel_id=1, source_target_pairs={{0,4},{2,6},{4,8},{6,10},{8,12},{10,14},{12,16},{14,18},{16,20},{1... | collective-permute-start | bytes 1179656 | tf_op jit(solution)/shard_map/ppermute | solution.py:22
  14.2 1.5 %fusion.87 = bf16[256,768]{1,0:T(8,128)(2,1)} fusion(bf16[256,1536]{1,0:T(8,128)(2,1)S(1)} %get-tuple-element.46, bf16[3,1536,768]{2,1,0:T(8,128)(2,1)S(1)} %copy-done.3), kind=kOutput, calls=%fused_computation.99 | convolution fusion | flops 604176384 | bytes 3538944 | tf_op jit(solution)/shard_map/dot_general | solution.py:99
  15.7 1.3 %collective-permute-start.3 = (bf16[256,768]{1,0:T(8,128)(2,1)}, bf16[256,768]{1,0:T(8,128)(2,1)}, u32[]{:S(2)}, u32[]{:S(2)}) collective-permute-start(bf16[256,768]{1,0:T(8,128)(2,1)} %fusion.87), channel_id=1, source_target_pairs={{4,0},{6,2},{8,4},{10,6},{12,8},{14,10},{16,12},{18,14},{20,16},{2... | collective-permute-start | bytes 1179656 | tf_op jit(solution)/shard_map/ppermute | solution.py:22
  17.0 1.5 %fusion.78 = bf16[256,768]{1,0:T(8,128)(2,1)} fusion(bf16[256,1536]{1,0:T(8,128)(2,1)S(1)} %get-tuple-element.47, bf16[3,1536,768]{2,1,0:T(8,128)(2,1)S(1)} %copy-done.3), kind=kOutput, calls=%fused_computation.96 | convolution fusion | flops 604176384 | bytes 3538944 | tf_op jit(solution)/shard_map/dot_general | solution.py:98
  18.5 4.6 %collective-permute-start = (bf16[256,768]{1,0:T(8,128)(2,1)}, bf16[256,768]{1,0:T(8,128)(2,1)S(1)}, u32[]{:S(2)}, u32[]{:S(2)}) collective-permute-start(bf16[256,768]{1,0:T(8,128)(2,1)} %fusion.78), channel_id=1, source_target_pairs={{0,4},{2,6},{4,8},{6,10},{8,12},{10,14},{12,16},{14,18},{16,20},{1... | collective-permute-start | bytes 1179656 | tf_op jit(solution)/shard_map/ppermute | solution.py:22
  23.1 1.6 %fusion.84 = bf16[256,768]{1,0:T(8,128)(2,1)} fusion(bf16[256,1536]{1,0:T(8,128)(2,1)S(1)} %get-tuple-element.47, bf16[3,1536,768]{2,1,0:T(8,128)(2,1)S(1)} %copy-done.3), kind=kOutput, calls=%fused_computation.98 | convolution fusion | flops 604176384 | bytes 3538944 | tf_op jit(solution)/shard_map/dot_general | solution.py:99
  24.7 1.3 %collective-permute-start.1 = (bf16[256,768]{1,0:T(8,128)(2,1)}, bf16[256,768]{1,0:T(8,128)(2,1)}, u32[]{:S(2)}, u32[]{:S(2)}) collective-permute-start(bf16[256,768]{1,0:T(8,128)(2,1)} %fusion.84), channel_id=1, source_target_pairs={{4,0},{6,2},{8,4},{10,6},{12,8},{14,10},{16,12},{18,14},{20,16},{2... | collective-permute-start | bytes 1179656 | tf_op jit(solution)/shard_map/ppermute | solution.py:22
  29.3 3.4 %fusion.22 = f32[256,768]{1,0:T(8,128)} fusion(bf16[256,1536]{1,0:T(8,128)(2,1)S(1)} %get-tuple-element.46, bf16[3,1536,768]{2,1,0:T(8,128)(2,1)} %param.11), kind=kOutput, calls=%fused_computation.38 | convolution fusion | flops 603979776 | bytes 3932160 | tf_op jit(solution)/shard_map/dot_general | solution.py:107
  32.7 2.6 %fusion.24 = f32[256,768]{1,0:T(8,128)S(1)} fusion(bf16[256,1536]{1,0:T(8,128)(2,1)S(1)} %copy-done.8, bf16[3,1536,768]{2,1,0:T(8,128)(2,1)} %param.11), kind=kOutput, calls=%fused_computation.40 | convolution fusion | flops 603979776 | bytes 3932160 | tf_op jit(solution)/shard_map/dot_general | solution.py:107
  35.3 1.7 %fusion.104 = f32[256,768]{1,0:T(8,128)} fusion(bf16[768,1536]{1,0:T(8,128)(2,1)S(1)} %copy-done, bf16[1,512,1536]{2,1,0:T(8,128)(2,1)S(1)} %copy-done.4), kind=kOutput, calls=%fused_computation.120 | convolution fusion | flops 603979776 | bytes 3932160 | tf_op jit(solution)/shard_map/dot_general | solution.py:108
  37.0 1.7 %fusion.106 = f32[256,768]{1,0:T(8,128)} fusion(bf16[768,1536]{1,0:T(8,128)(2,1)S(1)} %copy-done, bf16[1,512,1536]{2,1,0:T(8,128)(2,1)S(1)} %copy-done.4), kind=kOutput, calls=%fused_computation.122 | convolution fusion | flops 603979776 | bytes 3932160 | tf_op jit(solution)/shard_map/dot_general | solution.py:108
  38.7 1.3 %reduce-window.8 = s32[4,1]{0,1:T(1,128)} reduce-window(s32[4,1]{0,1:T(1,128)} %bitcast.94, s32[]{:T(128)} %constant.60.clone.1), window={size=4x1 pad=3_0x0_0}, to_apply=%region_1.2 | reduce-window | flops 12 | bytes 36 | tf_op jit(solution)/shard_map/reduce-window.3
  41.0 1.7 %multiply_reduce_fusion.4 = (f32[256]{0:T(256)S(1)}, f32[256,768]{1,0:T(8,128)S(1)}) fusion(bf16[256,768]{1,0:T(8,128)(2,1)} %collective-permute-done.3, f32[256]{0:T(256)S(1)} %get-tuple-element.56, f32[256,768]{1,0:T(8,128)} %fusion.22, bf16[256,768]{1,0:T(8,128)(2,1)} %collective-permute-done.2, f32[256]{0:T(256)S(1)} %get-tuple-element.55), kind=kLoop, calls=%fused_computation.129 | loop fusion | flops 1572608 | bytes 2362368 | tf_op jit(solution)/shard_map/jvp()/reduce_sum | solution.py:26
  42.7 4.7 %collective-permute-done = bf16[256,768]{1,0:T(8,128)(2,1)S(1)} collective-permute-done((bf16[256,768]{1,0:T(8,128)(2,1)}, bf16[256,768]{1,0:T(8,128)(2,1)S(1)}, u32[]{:S(2)}, u32[]{:S(2)}) %collective-permute-start) | collective-permute-done | bytes 393248 | tf_op jit(solution)/shard_map/ppermute | solution.py:22
  47.4 1.4 %multiply_reduce_fusion.5 = (f32[256]{0:T(256)S(1)}, f32[256,768]{1,0:T(8,128)S(1)}) fusion(bf16[256,768]{1,0:T(8,128)(2,1)} %collective-permute-done.1, f32[256]{0:T(256)S(1)} %get-tuple-element.58, f32[256,768]{1,0:T(8,128)S(1)} %fusion.24, bf16[256,768]{1,0:T(8,128)(2,1)S(1)} %collective-permute-done, f32[256]{0:T(256)S(1)} %get-tuple-element.57), kind=kLoop, calls=%fused_computation.132 | loop fusion | flops 1572608 | bytes 2362368 | tf_op jit(solution)/shard_map/jvp()/reduce_sum | solution.py:26
  49.9 1.3 %fusion.103 = (bf16[256,768]{1,0:T(8,128)(2,1)S(1)}, bf16[256,768]{1,0:T(8,128)(2,1)S(1)}, f32[256]{0:T(256)S(1)}, f32[768]{0:T(1024)S(1)}, f32[256,768]{1,0:T(8,128)S(1)}) fusion(f32[256,768]{1,0:T(8,128)S(1)} %get-tuple-element.43, f32[256,768]{1,0:T(8,128)S(1)} %get-tuple-element.38, f32[256]{0:T(256)S(1)} %multiply_multiply_fusion.12, ...), kind=kLoop, calls=%fused_computation.119 | loop fusion | flops 8453120 | bytes 4728832 | tf_op jit(solution)/shard_map/convert_element_type | solution.py:116
  51.7 4.3 %collective-permute-start.4 = (bf16[256,768]{1,0:T(8,128)(2,1)S(1)}, bf16[256,768]{1,0:T(8,128)(2,1)S(1)}, u32[]{:S(2)}, u32[]{:S(2)}) collective-permute-start(bf16[256,768]{1,0:T(8,128)(2,1)S(1)} %get-tuple-element.50), channel_id=1, source_target_pairs={{0,4},{2,6},{4,8},{6,10},{8,12},{10,14},{12,16},{14,18},{16,20},{1... | collective-permute-start | bytes 1179656 | tf_op jit(solution)/shard_map/ppermute | solution.py:22
  56.0 1.3 %collective-permute-start.5 = (bf16[256,768]{1,0:T(8,128)(2,1)S(1)}, bf16[256,768]{1,0:T(8,128)(2,1)S(1)}, u32[]{:S(2)}, u32[]{:S(2)}) collective-permute-start(bf16[256,768]{1,0:T(8,128)(2,1)S(1)} %get-tuple-element.50), channel_id=1, source_target_pairs={{4,0},{6,2},{8,4},{10,6},{12,8},{14,10},{16,12},{18,14},{20,16},{2... | collective-permute-start | bytes 1179656 | tf_op jit(solution)/shard_map/ppermute | solution.py:22
  57.3 2.5 %fusion.20 = f32[256,1536]{1,0:T(8,128)S(1)} fusion(bf16[256,768]{1,0:T(8,128)(2,1)S(1)} %get-tuple-element.48, bf16[3,1536,768]{2,1,0:T(8,128)(2,1)} %param.11), kind=kOutput, calls=%fused_computation.36 | convolution fusion | flops 603979776 | bytes 4325376 | tf_op jit(solution)/shard_map/dot_general | solution.py:135
  59.8 5.1 %collective-permute-start.6 = (bf16[256,768]{1,0:T(8,128)(2,1)S(1)}, bf16[256,768]{1,0:T(8,128)(2,1)S(1)}, u32[]{:S(2)}, u32[]{:S(2)}) collective-permute-start(bf16[256,768]{1,0:T(8,128)(2,1)S(1)} %get-tuple-element.48), channel_id=1, source_target_pairs={{0,4},{2,6},{4,8},{6,10},{8,12},{10,14},{12,16},{14,18},{16,20},{1... | collective-permute-start | bytes 1179656 | tf_op jit(solution)/shard_map/ppermute | solution.py:22
  64.9 1.5 %collective-permute-start.7 = (bf16[256,768]{1,0:T(8,128)(2,1)S(1)}, bf16[256,768]{1,0:T(8,128)(2,1)S(1)}, u32[]{:S(2)}, u32[]{:S(2)}) collective-permute-start(bf16[256,768]{1,0:T(8,128)(2,1)S(1)} %get-tuple-element.48), channel_id=1, source_target_pairs={{4,0},{6,2},{8,4},{10,6},{12,8},{14,10},{16,12},{18,14},{20,16},{2... | collective-permute-start | bytes 1179656 | tf_op jit(solution)/shard_map/ppermute | solution.py:22
  67.2 15.2 %collective-permute-done.4 = bf16[256,768]{1,0:T(8,128)(2,1)S(1)} collective-permute-done((bf16[256,768]{1,0:T(8,128)(2,1)S(1)}, bf16[256,768]{1,0:T(8,128)(2,1)S(1)}, u32[]{:S(2)}, u32[]{:S(2)}) %collective-permute-start.4) | collective-permute-done | bytes 393248 | tf_op jit(solution)/shard_map/ppermute | solution.py:22
  83.8 1.7 %fusion.53 = f32[256,1536]{1,0:T(8,128)S(1)} fusion(f32[256,1536]{1,0:T(8,128)S(1)} %fusion.1, bf16[256,768]{1,0:T(8,128)(2,1)S(1)} %collective-permute-done.5, bf16[3,1536,768]{2,1,0:T(8,128)(2,1)S(1)} %bitcast.92, f32[256]{0:T(256)S(1)} %get-tuple-element.56, f32[256]{0:T(256)S(1)} %fusion.116, f32[1536]{0:T(1024)S(1)} %copy-done.11, ...), kind=kOutput, calls=%fused_computation.73 | convolution fusion | flops 613416960 | bytes 6694912 | tf_op jit(solution)/shard_map/dot_general | solution.py:139
  85.5 3.3 %collective-permute-done.6 = bf16[256,768]{1,0:T(8,128)(2,1)S(1)} collective-permute-done((bf16[256,768]{1,0:T(8,128)(2,1)S(1)}, bf16[256,768]{1,0:T(8,128)(2,1)S(1)}, u32[]{:S(2)}, u32[]{:S(2)}) %collective-permute-start.6) | collective-permute-done | bytes 393248 | tf_op jit(solution)/shard_map/ppermute | solution.py:22
  89.6 2.5 %fusion.47 = (f32[1536]{0:T(1024)S(1)}, f32[256]{0:T(256)S(1)}, f32[256]{0:T(256)S(1)}, f32[1536]{0:T(1024)S(1)}, f32[256,1536]{1,0:T(8,128)S(1)}) fusion(f32[256]{0:T(256)S(1)} %fusion.114, bf16[1,512,1536]{2,1,0:T(8,128)(2,1)S(1)} %copy-done.2, f32[1536]{0:T(1024)S(1)} %copy-done.11, f32[256,1536]{1,0:T(8,128)S(1)} %fusion.53, f32[256]{0:T(256)S(1)} %fusion.116, ...), kind=kOutput, calls=%fused_computation.67 | convolution fusion | flops 618131968 | bytes 9069568 | tf_op jit(solution)/shard_map/dot_general | solution.py:139
  92.1 6.8 %collective-permute-start.10 = (f32[2304]{0:T(1024)S(1)}, f32[2304]{0:T(1024)S(1)}, u32[]{:S(2)}, u32[]{:S(2)}) collective-permute-start(f32[2304]{0:T(1024)S(1)} %pad_maximum_fusion), channel_id=1, source_target_pairs={{0,24},{1,25},{2,26},{3,27},{4,28},{5,29},{6,30},{7,31},{8,16},{9,... | collective-permute-start | bytes 27656 | tf_op jit(solution)/shard_map/ppermute | solution.py:40
  103.7 1.8 %collective-permute-start.13 = (f32[2304]{0:T(1024)S(1)}, f32[2304]{0:T(1024)S(1)}, u32[]{:S(2)}, u32[]{:S(2)}) collective-permute-start(f32[2304]{0:T(1024)S(1)} %add_add_fusion.5), channel_id=1, source_target_pairs={{0,6},{1,7},{2,4},{3,5},{4,2},{5,3},{6,0},{7,1},{8,14},{9,15},{10,... | collective-permute-start | bytes 27656 | tf_op jit(solution)/shard_map/ppermute | solution.py:40
  105.5 1.2 %maximum_bitcast_fusion.1 = bf16[1,512,1536]{2,1,0:T(8,128)(2,1)} fusion(bf16[256,1536]{1,0:T(8,128)(2,1)S(1)} %get-tuple-element.45, bf16[256,1536]{1,0:T(8,128)(2,1)S(1)} %get-tuple-element.44), kind=kLoop, calls=%fused_computation.83 | loop fusion | flops 3145728 | bytes 3145728 | tf_op jit(solution)/shard_map/broadcast_in_dim | solution.py:151
  107.4 1.6 %collective-permute-start.14 = (f32[2304]{0:T(1024)S(1)}, f32[2304]{0:T(1024)S(1)}, u32[]{:S(2)}, u32[]{:S(2)}) collective-permute-start(f32[2304]{0:T(1024)S(1)} %add_add_fusion.4), channel_id=1, source_target_pairs={{0,1},{1,0},{2,3},{3,2},{4,5},{5,4},{6,7},{7,6},{8,9},{9,8},{10,11... | collective-permute-start | bytes 27656 | tf_op jit(solution)/shard_map/ppermute | solution.py:40
  (86 shorter events, 18.3 us)
Async XLA Ops:
  0.6 34.7 %copy-start = (bf16[768,1536]{1,0:T(8,128)(2,1)S(1)}, bf16[768,1536]{1,0:T(8,128)(2,1)}, u32[]{:S(2)}) copy-start(bf16[768,1536]{1,0:T(8,128)(2,1)} %param.13) | copy-start | bytes 7077892
  0.6 2.5 %copy-start.1 = (bf16[1,512,1536]{2,1,0:T(8,128)(2,1)S(1)}, bf16[1,512,1536]{2,1,0:T(8,128)(2,1)}, u32[]{:S(2)}) copy-start(bf16[1,512,1536]{2,1,0:T(8,128)(2,1)} %param.7) | copy-start | bytes 4718596
  0.7 2.5 %copy-start.11 = (f32[1536]{0:T(1024)S(1)}, f32[1536]{0:T(1024)}, u32[]{:S(2)}) copy-start(f32[1536]{0:T(1024)} %param.10) | copy-start | bytes 18436
  2.6 0.5 copy-start.14
  3.1 11.1 %copy-start.3 = (bf16[3,1536,768]{2,1,0:T(8,128)(2,1)S(1)}, bf16[3,1536,768]{2,1,0:T(8,128)(2,1)}, u32[]{:S(2)}) copy-start(bf16[3,1536,768]{2,1,0:T(8,128)(2,1)} %param.11) | copy-start | bytes 21233668
  4.5 18.6 %copy-start.7 = (bf16[256,1536]{1,0:T(8,128)(2,1)}, bf16[256,1536]{1,0:T(8,128)(2,1)S(1)}, u32[]{:S(2)}) copy-start(bf16[256,1536]{1,0:T(8,128)(2,1)S(1)} %get-tuple-element.47) | copy-start | bytes 2359300
  8.6 32.3 %collective-permute-start.2 = (bf16[256,768]{1,0:T(8,128)(2,1)}, bf16[256,768]{1,0:T(8,128)(2,1)}, u32[]{:S(2)}, u32[]{:S(2)}) collective-permute-start(bf16[256,768]{1,0:T(8,128)(2,1)} %fusion.81), channel_id=1, source_target_pairs={{0,4},{2,6},{4,8},{6,10},{8,12},{10,14},{12,16},{14,18},{16,20},{1... | collective-permute-start | bytes 1179656 | tf_op jit(solution)/shard_map/ppermute | solution.py:22
  15.7 25.2 %collective-permute-start.3 = (bf16[256,768]{1,0:T(8,128)(2,1)}, bf16[256,768]{1,0:T(8,128)(2,1)}, u32[]{:S(2)}, u32[]{:S(2)}) collective-permute-start(bf16[256,768]{1,0:T(8,128)(2,1)} %fusion.87), channel_id=1, source_target_pairs={{4,0},{6,2},{8,4},{10,6},{12,8},{14,10},{16,12},{18,14},{20,16},{2... | collective-permute-start | bytes 1179656 | tf_op jit(solution)/shard_map/ppermute | solution.py:22
  18.5 28.9 %collective-permute-start = (bf16[256,768]{1,0:T(8,128)(2,1)}, bf16[256,768]{1,0:T(8,128)(2,1)S(1)}, u32[]{:S(2)}, u32[]{:S(2)}) collective-permute-start(bf16[256,768]{1,0:T(8,128)(2,1)} %fusion.78), channel_id=1, source_target_pairs={{0,4},{2,6},{4,8},{6,10},{8,12},{10,14},{12,16},{14,18},{16,20},{1... | collective-permute-start | bytes 1179656 | tf_op jit(solution)/shard_map/ppermute | solution.py:22
  24.7 22.7 %collective-permute-start.1 = (bf16[256,768]{1,0:T(8,128)(2,1)}, bf16[256,768]{1,0:T(8,128)(2,1)}, u32[]{:S(2)}, u32[]{:S(2)}) collective-permute-start(bf16[256,768]{1,0:T(8,128)(2,1)} %fusion.84), channel_id=1, source_target_pairs={{4,0},{6,2},{8,4},{10,6},{12,8},{14,10},{16,12},{18,14},{20,16},{2... | collective-permute-start | bytes 1179656 | tf_op jit(solution)/shard_map/ppermute | solution.py:22
  29.3 3.4 %copy-start.8 = (bf16[256,1536]{1,0:T(8,128)(2,1)S(1)}, bf16[256,1536]{1,0:T(8,128)(2,1)}, u32[]{:S(2)}) copy-start(bf16[256,1536]{1,0:T(8,128)(2,1)} %copy-done.7) | copy-start | bytes 2359300
  32.7 2.6 %copy-start.4 = (bf16[1,512,1536]{2,1,0:T(8,128)(2,1)S(1)}, bf16[1,512,1536]{2,1,0:T(8,128)(2,1)}, u32[]{:S(2)}) copy-start(bf16[1,512,1536]{2,1,0:T(8,128)(2,1)} %param.8) | copy-start | bytes 4718596
  42.7 6.1 %copy-start.6 = (f32[256,768]{1,0:T(8,128)S(1)}, f32[256,768]{1,0:T(8,128)}, u32[]{:S(2)}) copy-start(f32[256,768]{1,0:T(8,128)} %fusion.106) | copy-start | bytes 2359300
  42.7 6.1 %copy-start.10 = (f32[768]{0:T(1024)S(1)}, f32[768]{0:T(1024)}, u32[]{:S(2)}) copy-start(f32[768]{0:T(1024)} %param.12) | copy-start | bytes 9220
  48.7 1.1 %copy-start.9 = (f32[256,768]{1,0:T(8,128)S(1)}, f32[256,768]{1,0:T(8,128)}, u32[]{:S(2)}) copy-start(f32[256,768]{1,0:T(8,128)} %fusion.104) | copy-start | bytes 2359300
  48.8 17.6 %slice-start = ((s8[7077888]{0:T(1024)(128)(4,1)}), s8[4194304]{0:T(1024)(128)(4,1)S(1)}, s32[]{:S(2)}) async-start(s8[7077888]{0:T(1024)(128)(4,1)} %bitcast.91), calls=%async_computation | async-start | bytes 8388608
  49.9 16.5 %slice-start.1 = ((s8[7077888]{0:T(1024)(128)(4,1)}), s8[2883584]{0:T(1024)(128)(4,1)S(1)}, s32[]{:S(2)}) async-start(s8[7077888]{0:T(1024)(128)(4,1)} %bitcast.91), calls=%async_computation.1 | async-start | bytes 5767168
  51.7 30.7 %collective-permute-start.4 = (bf16[256,768]{1,0:T(8,128)(2,1)S(1)}, bf16[256,768]{1,0:T(8,128)(2,1)S(1)}, u32[]{:S(2)}, u32[]{:S(2)}) collective-permute-start(bf16[256,768]{1,0:T(8,128)(2,1)S(1)} %get-tuple-element.50), channel_id=1, source_target_pairs={{0,4},{2,6},{4,8},{6,10},{8,12},{10,14},{12,16},{14,18},{16,20},{1... | collective-permute-start | bytes 1179656 | tf_op jit(solution)/shard_map/ppermute | solution.py:22
  56.0 26.4 %collective-permute-start.5 = (bf16[256,768]{1,0:T(8,128)(2,1)S(1)}, bf16[256,768]{1,0:T(8,128)(2,1)S(1)}, u32[]{:S(2)}, u32[]{:S(2)}) collective-permute-start(bf16[256,768]{1,0:T(8,128)(2,1)S(1)} %get-tuple-element.50), channel_id=1, source_target_pairs={{4,0},{6,2},{8,4},{10,6},{12,8},{14,10},{16,12},{18,14},{20,16},{2... | collective-permute-start | bytes 1179656 | tf_op jit(solution)/shard_map/ppermute | solution.py:22
  59.8 29.0 %collective-permute-start.6 = (bf16[256,768]{1,0:T(8,128)(2,1)S(1)}, bf16[256,768]{1,0:T(8,128)(2,1)S(1)}, u32[]{:S(2)}, u32[]{:S(2)}) collective-permute-start(bf16[256,768]{1,0:T(8,128)(2,1)S(1)} %get-tuple-element.48), channel_id=1, source_target_pairs={{0,4},{2,6},{4,8},{6,10},{8,12},{10,14},{12,16},{14,18},{16,20},{1... | collective-permute-start | bytes 1179656 | tf_op jit(solution)/shard_map/ppermute | solution.py:22
  64.9 24.7 %collective-permute-start.7 = (bf16[256,768]{1,0:T(8,128)(2,1)S(1)}, bf16[256,768]{1,0:T(8,128)(2,1)S(1)}, u32[]{:S(2)}, u32[]{:S(2)}) collective-permute-start(bf16[256,768]{1,0:T(8,128)(2,1)S(1)} %get-tuple-element.48), channel_id=1, source_target_pairs={{4,0},{6,2},{8,4},{10,6},{12,8},{14,10},{16,12},{18,14},{20,16},{2... | collective-permute-start | bytes 1179656 | tf_op jit(solution)/shard_map/ppermute | solution.py:22
  82.4 1.4 %copy-start.2 = (bf16[1,512,1536]{2,1,0:T(8,128)(2,1)S(1)}, bf16[1,512,1536]{2,1,0:T(8,128)(2,1)}, u32[]{:S(2)}) copy-start(bf16[1,512,1536]{2,1,0:T(8,128)(2,1)} %param.7) | copy-start | bytes 4718596
  92.1 8.2 %copy-start.13 = (f32[256]{0:T(256)S(1)}, f32[256]{0:T(256)}, u32[]{:S(2)}) copy-start(f32[256]{0:T(256)} %copy-done.12) | copy-start | bytes 3076
  92.1 8.2 %copy-start.15 = (f32[256]{0:T(256)S(1)}, f32[256]{0:T(256)}, u32[]{:S(2)}) copy-start(f32[256]{0:T(256)} %copy-done.14) | copy-start | bytes 3076
  92.1 8.2 %copy-start.5 = (bf16[1,512,1536]{2,1,0:T(8,128)(2,1)S(1)}, bf16[1,512,1536]{2,1,0:T(8,128)(2,1)}, u32[]{:S(2)}) copy-start(bf16[1,512,1536]{2,1,0:T(8,128)(2,1)} %param.8) | copy-start | bytes 4718596
  92.1 10.0 %collective-permute-start.10 = (f32[2304]{0:T(1024)S(1)}, f32[2304]{0:T(1024)S(1)}, u32[]{:S(2)}, u32[]{:S(2)}) collective-permute-start(f32[2304]{0:T(1024)S(1)} %pad_maximum_fusion), channel_id=1, source_target_pairs={{0,24},{1,25},{2,26},{3,27},{4,28},{5,29},{6,30},{7,31},{8,16},{9,... | collective-permute-start | bytes 27656 | tf_op jit(solution)/shard_map/ppermute | solution.py:40
  98.9 3.7 %collective-permute-start.8 = (f32[2304]{0:T(1024)S(1)}, f32[2304]{0:T(1024)S(1)}, u32[]{:S(2)}, u32[]{:S(2)}) collective-permute-start(f32[2304]{0:T(1024)S(1)} %pad_maximum_fusion), channel_id=1, source_target_pairs={{0,8},{1,9},{2,10},{3,11},{4,12},{5,13},{6,14},{7,15},{8,0},{9,1},... | collective-permute-start | bytes 27656 | tf_op jit(solution)/shard_map/ppermute | solution.py:40
  98.9 4.7 %collective-permute-start.9 = (f32[2304]{0:T(1024)S(1)}, f32[2304]{0:T(1024)S(1)}, u32[]{:S(2)}, u32[]{:S(2)}) collective-permute-start(f32[2304]{0:T(1024)S(1)} %pad_maximum_fusion), channel_id=1, source_target_pairs={{0,16},{1,17},{2,18},{3,19},{4,20},{5,21},{6,22},{7,23},{8,24},{9,... | collective-permute-start | bytes 27656 | tf_op jit(solution)/shard_map/ppermute | solution.py:40
  103.6 3.2 %collective-permute-start.11 = (f32[2304]{0:T(1024)S(1)}, f32[2304]{0:T(1024)S(1)}, u32[]{:S(2)}, u32[]{:S(2)}) collective-permute-start(f32[2304]{0:T(1024)S(1)} %add_add_fusion.5), channel_id=1, source_target_pairs={{0,2},{1,3},{2,0},{3,1},{4,6},{5,7},{6,4},{7,5},{8,10},{9,11},{10,... | collective-permute-start | bytes 27656 | tf_op jit(solution)/shard_map/ppermute | solution.py:40
  103.6 3.8 %collective-permute-start.12 = (f32[2304]{0:T(1024)S(1)}, f32[2304]{0:T(1024)S(1)}, u32[]{:S(2)}, u32[]{:S(2)}) collective-permute-start(f32[2304]{0:T(1024)S(1)} %add_add_fusion.5), channel_id=1, source_target_pairs={{0,4},{1,5},{2,6},{3,7},{4,0},{5,1},{6,2},{7,3},{8,12},{9,13},{10,... | collective-permute-start | bytes 27656 | tf_op jit(solution)/shard_map/ppermute | solution.py:40
  103.7 3.7 %collective-permute-start.13 = (f32[2304]{0:T(1024)S(1)}, f32[2304]{0:T(1024)S(1)}, u32[]{:S(2)}, u32[]{:S(2)}) collective-permute-start(f32[2304]{0:T(1024)S(1)} %add_add_fusion.5), channel_id=1, source_target_pairs={{0,6},{1,7},{2,4},{3,5},{4,2},{5,3},{6,0},{7,1},{8,14},{9,15},{10,... | collective-permute-start | bytes 27656 | tf_op jit(solution)/shard_map/ppermute | solution.py:40
  107.4 3.8 %collective-permute-start.14 = (f32[2304]{0:T(1024)S(1)}, f32[2304]{0:T(1024)S(1)}, u32[]{:S(2)}, u32[]{:S(2)}) collective-permute-start(f32[2304]{0:T(1024)S(1)} %add_add_fusion.4), channel_id=1, source_target_pairs={{0,1},{1,0},{2,3},{3,2},{4,5},{5,4},{6,7},{7,6},{8,9},{9,8},{10,11... | collective-permute-start | bytes 27656 | tf_op jit(solution)/shard_map/ppermute | solution.py:40
  (1 other events, 0.5 us)

commit v6 on v5

--- a/solution.py
+++ b/solution.py
@@ -8,7 +8,7 @@
 SPAN = 2
 CHUNKS = (1, 1)
 AXES = ("seq", "batch")
-STAGES = (2, 4, 4)
+STAGES = (2, 4, 2, 2)
 EARLY = True
 LATE_OUTPUT = True
 

time: 113 us -> 113 us (level)
    ppermute x7 -> x6, waiting for transfers between devices: 2.99 us -> 2.71 us  [group_sum(): parts.append(lax.ppermute(x, axis, pairs))]
    ppermute x7 -> x6, starting transfers between devices: 10.9 us -> 11 us  [group_sum(): parts.append(lax.ppermute(x, axis, pairs))]
  transfers between devices with their start and end apart: 15 -> 14, of which waited for: 7 -> 6; matrix products, arithmetic and copies ran while one was open for 29% -> 29% of each run, Pallas kernels for 0% -> 0%
where the time goes in v6:
time: 113 us; the launch traced here: 112 us
  starting transfers between devices  35.8 us (32%)
  matrix products  28.7 us (25%)
  waiting for transfers between devices  25.8 us (23%)
  other arithmetic  19.3 us (17%)
  local copies, waits for them, and re-layouts  1.37 us (1%)
    ppermute x8, starting transfers between devices, shifted(): return lax.ppermute(x, axis, pairs)  24.9 us
    ppermute x8, waiting for transfers between devices, shifted(): return lax.ppermute(x, axis, pairs)  23.1 us
    ppermute x6, starting transfers between devices, group_sum(): parts.append(lax.ppermute(x, axis, pairs))  11 us
    dot_general x2, matrix products, body(): jnp.dot(ch['hidden'], tap_center, preferred_element_type=jnp.float32)  5.95 us
    dot_general x2, matrix products, body(): jnp.dot(hidden, tap_before, preferred_element_type=jnp.float32)  5.58 us
    reduce_sum x3, other arithmetic, norm_activate(): mean_square = jnp.mean(values * values, axis=-1, keepdims=True)  4.96 us
    dot_general x2, matrix products, body(): jnp.dot(ch['combined_after'], tap_before.T, preferred_element_type=jnp.fl...  4.16 us
    dot_general x2, matrix products, body(): jnp.dot(ch['upstream'], point_weights.T, preferred_element_type=jnp.float32)  3.42 us
  transfers between devices with their start and end apart: 14, of which 6 were waited for; matrix products, arithmetic and copies ran while one was open for 29% of the time, Pallas kernels for 0%

profile of v6, /device:TPU:0, one launch (start us, length us, event | category | flops | bytes accessed | tf_op | source)
XLA Modules:
  0.0 112.1 jit_solution(6054210432018653145)
XLA Ops:
  0.7 1.9 %fusion.60 = (f32[256]{0:T(256)S(1)}, f32[256]{0:T(256)S(1)}) fusion(bf16[1,512,1536]{2,1,0:T(8,128)(2,1)} %param.7), kind=kLoop, calls=%fused_computation.80 | loop fusion | flops 2358784 | bytes 1574912 | tf_op jit(solution)/shard_map/jvp()/reduce_sum | solution.py:26
  3.1 1.4 %fusion.38 = (bf16[256,1536]{1,0:T(8,128)(2,1)S(1)}, bf16[256,1536]{1,0:T(8,128)(2,1)S(1)}) fusion(f32[256]{0:T(256)S(1)} %fusion.116, f32[1536]{0:T(1024)S(1)} %copy-done.11, bf16[1,512,1536]{2,1,0:T(8,128)(2,1)S(1)} %copy-done.1, f32[256]{0:T(256)S(1)} %fusion.114), kind=kLoop, calls=%fused_computation.58 | loop fusion | flops 9437184 | bytes 3153920 | tf_op jit(solution)/shard_map/convert_element_type | solution.py:97
  4.5 4.0 %fusion.81 = bf16[256,768]{1,0:T(8,128)(2,1)} fusion(bf16[256,1536]{1,0:T(8,128)(2,1)S(1)} %get-tuple-element.46, bf16[3,1536,768]{2,1,0:T(8,128)(2,1)} %param.11), kind=kOutput, calls=%fused_computation.97 | convolution fusion | flops 604176384 | bytes 3538944 | tf_op jit(solution)/shard_map/dot_general | solution.py:98
  8.6 5.6 %collective-permute-start.2 = (bf16[256,768]{1,0:T(8,128)(2,1)}, bf16[256,768]{1,0:T(8,128)(2,1)}, u32[]{:S(2)}, u32[]{:S(2)}) collective-permute-start(bf16[256,768]{1,0:T(8,128)(2,1)} %fusion.81), channel_id=1, source_target_pairs={{0,4},{2,6},{4,8},{6,10},{8,12},{10,14},{12,16},{14,18},{16,20},{1... | collective-permute-start | bytes 1179656 | tf_op jit(solution)/shard_map/ppermute | solution.py:22
  14.2 1.5 %fusion.87 = bf16[256,768]{1,0:T(8,128)(2,1)} fusion(bf16[256,1536]{1,0:T(8,128)(2,1)S(1)} %get-tuple-element.46, bf16[3,1536,768]{2,1,0:T(8,128)(2,1)S(1)} %copy-done.3), kind=kOutput, calls=%fused_computation.99 | convolution fusion | flops 604176384 | bytes 3538944 | tf_op jit(solution)/shard_map/dot_general | solution.py:99
  15.7 1.3 %collective-permute-start.3 = (bf16[256,768]{1,0:T(8,128)(2,1)}, bf16[256,768]{1,0:T(8,128)(2,1)}, u32[]{:S(2)}, u32[]{:S(2)}) collective-permute-start(bf16[256,768]{1,0:T(8,128)(2,1)} %fusion.87), channel_id=1, source_target_pairs={{4,0},{6,2},{8,4},{10,6},{12,8},{14,10},{16,12},{18,14},{20,16},{2... | collective-permute-start | bytes 1179656 | tf_op jit(solution)/shard_map/ppermute | solution.py:22
  17.0 1.5 %fusion.78 = bf16[256,768]{1,0:T(8,128)(2,1)} fusion(bf16[256,1536]{1,0:T(8,128)(2,1)S(1)} %get-tuple-element.47, bf16[3,1536,768]{2,1,0:T(8,128)(2,1)S(1)} %copy-done.3), kind=kOutput, calls=%fused_computation.96 | convolution fusion | flops 604176384 | bytes 3538944 | tf_op jit(solution)/shard_map/dot_general | solution.py:98
  18.5 4.6 %collective-permute-start = (bf16[256,768]{1,0:T(8,128)(2,1)}, bf16[256,768]{1,0:T(8,128)(2,1)S(1)}, u32[]{:S(2)}, u32[]{:S(2)}) collective-permute-start(bf16[256,768]{1,0:T(8,128)(2,1)} %fusion.78), channel_id=1, source_target_pairs={{0,4},{2,6},{4,8},{6,10},{8,12},{10,14},{12,16},{14,18},{16,20},{1... | collective-permute-start | bytes 1179656 | tf_op jit(solution)/shard_map/ppermute | solution.py:22
  23.1 1.6 %fusion.84 = bf16[256,768]{1,0:T(8,128)(2,1)} fusion(bf16[256,1536]{1,0:T(8,128)(2,1)S(1)} %get-tuple-element.47, bf16[3,1536,768]{2,1,0:T(8,128)(2,1)S(1)} %copy-done.3), kind=kOutput, calls=%fused_computation.98 | convolution fusion | flops 604176384 | bytes 3538944 | tf_op jit(solution)/shard_map/dot_general | solution.py:99
  24.7 1.3 %collective-permute-start.1 = (bf16[256,768]{1,0:T(8,128)(2,1)}, bf16[256,768]{1,0:T(8,128)(2,1)}, u32[]{:S(2)}, u32[]{:S(2)}) collective-permute-start(bf16[256,768]{1,0:T(8,128)(2,1)} %fusion.84), channel_id=1, source_target_pairs={{4,0},{6,2},{8,4},{10,6},{12,8},{14,10},{16,12},{18,14},{20,16},{2... | collective-permute-start | bytes 1179656 | tf_op jit(solution)/shard_map/ppermute | solution.py:22
  29.3 3.4 %fusion.22 = f32[256,768]{1,0:T(8,128)} fusion(bf16[256,1536]{1,0:T(8,128)(2,1)S(1)} %get-tuple-element.46, bf16[3,1536,768]{2,1,0:T(8,128)(2,1)} %param.11), kind=kOutput, calls=%fused_computation.38 | convolution fusion | flops 603979776 | bytes 3932160 | tf_op jit(solution)/shard_map/dot_general | solution.py:107
  32.7 2.6 %fusion.24 = f32[256,768]{1,0:T(8,128)S(1)} fusion(bf16[256,1536]{1,0:T(8,128)(2,1)S(1)} %copy-done.8, bf16[3,1536,768]{2,1,0:T(8,128)(2,1)} %param.11), kind=kOutput, calls=%fused_computation.40 | convolution fusion | flops 603979776 | bytes 3932160 | tf_op jit(solution)/shard_map/dot_general | solution.py:107
  35.3 1.7 %fusion.104 = f32[256,768]{1,0:T(8,128)} fusion(bf16[768,1536]{1,0:T(8,128)(2,1)S(1)} %copy-done, bf16[1,512,1536]{2,1,0:T(8,128)(2,1)S(1)} %copy-done.4), kind=kOutput, calls=%fused_computation.120 | convolution fusion | flops 603979776 | bytes 3932160 | tf_op jit(solution)/shard_map/dot_general | solution.py:108
  37.0 1.7 %fusion.106 = f32[256,768]{1,0:T(8,128)} fusion(bf16[768,1536]{1,0:T(8,128)(2,1)S(1)} %copy-done, bf16[1,512,1536]{2,1,0:T(8,128)(2,1)S(1)} %copy-done.4), kind=kOutput, calls=%fused_computation.122 | convolution fusion | flops 603979776 | bytes 3932160 | tf_op jit(solution)/shard_map/dot_general | solution.py:108
  38.7 1.3 %reduce-window.8 = s32[4,1]{0,1:T(1,128)} reduce-window(s32[4,1]{0,1:T(1,128)} %bitcast.94, s32[]{:T(128)} %constant.60.clone.1), window={size=4x1 pad=3_0x0_0}, to_apply=%region_1.2 | reduce-window | flops 12 | bytes 36 | tf_op jit(solution)/shard_map/reduce-window.3
  41.0 1.7 %multiply_reduce_fusion.4 = (f32[256]{0:T(256)S(1)}, f32[256,768]{1,0:T(8,128)S(1)}) fusion(bf16[256,768]{1,0:T(8,128)(2,1)} %collective-permute-done.3, f32[256]{0:T(256)S(1)} %get-tuple-element.56, f32[256,768]{1,0:T(8,128)} %fusion.22, bf16[256,768]{1,0:T(8,128)(2,1)} %collective-permute-done.2, f32[256]{0:T(256)S(1)} %get-tuple-element.55), kind=kLoop, calls=%fused_computation.129 | loop fusion | flops 1572608 | bytes 2362368 | tf_op jit(solution)/shard_map/jvp()/reduce_sum | solution.py:26
  42.7 4.7 %collective-permute-done = bf16[256,768]{1,0:T(8,128)(2,1)S(1)} collective-permute-done((bf16[256,768]{1,0:T(8,128)(2,1)}, bf16[256,768]{1,0:T(8,128)(2,1)S(1)}, u32[]{:S(2)}, u32[]{:S(2)}) %collective-permute-start) | collective-permute-done | bytes 393248 | tf_op jit(solution)/shard_map/ppermute | solution.py:22
  47.4 1.4 %multiply_reduce_fusion.5 = (f32[256]{0:T(256)S(1)}, f32[256,768]{1,0:T(8,128)S(1)}) fusion(bf16[256,768]{1,0:T(8,128)(2,1)} %collective-permute-done.1, f32[256]{0:T(256)S(1)} %get-tuple-element.58, f32[256,768]{1,0:T(8,128)S(1)} %fusion.24, bf16[256,768]{1,0:T(8,128)(2,1)S(1)} %collective-permute-done, f32[256]{0:T(256)S(1)} %get-tuple-element.57), kind=kLoop, calls=%fused_computation.132 | loop fusion | flops 1572608 | bytes 2362368 | tf_op jit(solution)/shard_map/jvp()/reduce_sum | solution.py:26
  49.9 1.2 %fusion.103 = (bf16[256,768]{1,0:T(8,128)(2,1)S(1)}, bf16[256,768]{1,0:T(8,128)(2,1)S(1)}, f32[256]{0:T(256)S(1)}, f32[768]{0:T(1024)S(1)}, f32[256,768]{1,0:T(8,128)S(1)}) fusion(f32[256,768]{1,0:T(8,128)S(1)} %get-tuple-element.43, f32[256,768]{1,0:T(8,128)S(1)} %get-tuple-element.38, f32[256]{0:T(256)S(1)} %multiply_multiply_fusion.12, ...), kind=kLoop, calls=%fused_computation.119 | loop fusion | flops 8453120 | bytes 4728832 | tf_op jit(solution)/shard_map/convert_element_type | solution.py:116
  51.7 4.3 %collective-permute-start.4 = (bf16[256,768]{1,0:T(8,128)(2,1)S(1)}, bf16[256,768]{1,0:T(8,128)(2,1)S(1)}, u32[]{:S(2)}, u32[]{:S(2)}) collective-permute-start(bf16[256,768]{1,0:T(8,128)(2,1)S(1)} %get-tuple-element.50), channel_id=1, source_target_pairs={{0,4},{2,6},{4,8},{6,10},{8,12},{10,14},{12,16},{14,18},{16,20},{1... | collective-permute-start | bytes 1179656 | tf_op jit(solution)/shard_map/ppermute | solution.py:22
  56.0 1.3 %collective-permute-start.5 = (bf16[256,768]{1,0:T(8,128)(2,1)S(1)}, bf16[256,768]{1,0:T(8,128)(2,1)S(1)}, u32[]{:S(2)}, u32[]{:S(2)}) collective-permute-start(bf16[256,768]{1,0:T(8,128)(2,1)S(1)} %get-tuple-element.50), channel_id=1, source_target_pairs={{4,0},{6,2},{8,4},{10,6},{12,8},{14,10},{16,12},{18,14},{20,16},{2... | collective-permute-start | bytes 1179656 | tf_op jit(solution)/shard_map/ppermute | solution.py:22
  57.3 2.5 %fusion.20 = f32[256,1536]{1,0:T(8,128)S(1)} fusion(bf16[256,768]{1,0:T(8,128)(2,1)S(1)} %get-tuple-element.48, bf16[3,1536,768]{2,1,0:T(8,128)(2,1)} %param.11), kind=kOutput, calls=%fused_computation.36 | convolution fusion | flops 603979776 | bytes 4325376 | tf_op jit(solution)/shard_map/dot_general | solution.py:135
  59.8 5.1 %collective-permute-start.6 = (bf16[256,768]{1,0:T(8,128)(2,1)S(1)}, bf16[256,768]{1,0:T(8,128)(2,1)S(1)}, u32[]{:S(2)}, u32[]{:S(2)}) collective-permute-start(bf16[256,768]{1,0:T(8,128)(2,1)S(1)} %get-tuple-element.48), channel_id=1, source_target_pairs={{0,4},{2,6},{4,8},{6,10},{8,12},{10,14},{12,16},{14,18},{16,20},{1... | collective-permute-start | bytes 1179656 | tf_op jit(solution)/shard_map/ppermute | solution.py:22
  64.9 1.5 %collective-permute-start.7 = (bf16[256,768]{1,0:T(8,128)(2,1)S(1)}, bf16[256,768]{1,0:T(8,128)(2,1)S(1)}, u32[]{:S(2)}, u32[]{:S(2)}) collective-permute-start(bf16[256,768]{1,0:T(8,128)(2,1)S(1)} %get-tuple-element.48), channel_id=1, source_target_pairs={{4,0},{6,2},{8,4},{10,6},{12,8},{14,10},{16,12},{18,14},{20,16},{2... | collective-permute-start | bytes 1179656 | tf_op jit(solution)/shard_map/ppermute | solution.py:22
  67.2 15.2 %collective-permute-done.4 = bf16[256,768]{1,0:T(8,128)(2,1)S(1)} collective-permute-done((bf16[256,768]{1,0:T(8,128)(2,1)S(1)}, bf16[256,768]{1,0:T(8,128)(2,1)S(1)}, u32[]{:S(2)}, u32[]{:S(2)}) %collective-permute-start.4) | collective-permute-done | bytes 393248 | tf_op jit(solution)/shard_map/ppermute | solution.py:22
  83.8 1.7 %fusion.53 = f32[256,1536]{1,0:T(8,128)S(1)} fusion(f32[256,1536]{1,0:T(8,128)S(1)} %fusion.1, bf16[256,768]{1,0:T(8,128)(2,1)S(1)} %collective-permute-done.5, bf16[3,1536,768]{2,1,0:T(8,128)(2,1)S(1)} %bitcast.92, f32[256]{0:T(256)S(1)} %get-tuple-element.56, f32[256]{0:T(256)S(1)} %fusion.116, f32[1536]{0:T(1024)S(1)} %copy-done.11, ...), kind=kOutput, calls=%fused_computation.73 | convolution fusion | flops 613416960 | bytes 6694912 | tf_op jit(solution)/shard_map/dot_general | solution.py:139
  85.5 3.3 %collective-permute-done.6 = bf16[256,768]{1,0:T(8,128)(2,1)S(1)} collective-permute-done((bf16[256,768]{1,0:T(8,128)(2,1)S(1)}, bf16[256,768]{1,0:T(8,128)(2,1)S(1)}, u32[]{:S(2)}, u32[]{:S(2)}) %collective-permute-start.6) | collective-permute-done | bytes 393248 | tf_op jit(solution)/shard_map/ppermute | solution.py:22
  89.6 2.5 %fusion.47 = (f32[1536]{0:T(1024)S(1)}, f32[256]{0:T(256)S(1)}, f32[256]{0:T(256)S(1)}, f32[1536]{0:T(1024)S(1)}, f32[256,1536]{1,0:T(8,128)S(1)}) fusion(f32[256]{0:T(256)S(1)} %fusion.114, bf16[1,512,1536]{2,1,0:T(8,128)(2,1)S(1)} %copy-done.2, f32[1536]{0:T(1024)S(1)} %copy-done.11, f32[256,1536]{1,0:T(8,128)S(1)} %fusion.53, f32[256]{0:T(256)S(1)} %fusion.116, ...), kind=kOutput, calls=%fused_computation.67 | convolution fusion | flops 618131968 | bytes 9069568 | tf_op jit(solution)/shard_map/dot_general | solution.py:139
  92.1 5.7 %collective-permute-start.8 = (f32[2304]{0:T(1024)S(1)}, f32[2304]{0:T(1024)S(1)}, u32[]{:S(2)}, u32[]{:S(2)}) collective-permute-start(f32[2304]{0:T(1024)S(1)} %pad_maximum_fusion), channel_id=1, source_target_pairs={{0,16},{1,17},{2,18},{3,19},{4,20},{5,21},{6,22},{7,23},{8,24},{9,... | collective-permute-start | bytes 27656 | tf_op jit(solution)/shard_map/ppermute | solution.py:40
  99.6 1.8 %collective-permute-start.9 = (f32[2304]{0:T(1024)S(1)}, f32[2304]{0:T(1024)S(1)}, u32[]{:S(2)}, u32[]{:S(2)}) collective-permute-start(f32[2304]{0:T(1024)S(1)} %fusion.118), channel_id=1, source_target_pairs={{0,8},{1,9},{2,10},{3,11},{4,12},{5,13},{6,14},{7,15},{8,0},{9,1},... | collective-permute-start | bytes 27656 | tf_op jit(solution)/shard_map/ppermute | solution.py:40
  103.7 1.6 %collective-permute-start.12 = (f32[2304]{0:T(1024)S(1)}, f32[2304]{0:T(1024)S(1)}, u32[]{:S(2)}, u32[]{:S(2)}) collective-permute-start(f32[2304]{0:T(1024)S(1)} %add.233), channel_id=1, source_target_pairs={{0,6},{1,7},{2,4},{3,5},{4,2},{5,3},{6,0},{7,1},{8,14},{9,15},{10,... | collective-permute-start | bytes 27656 | tf_op jit(solution)/shard_map/ppermute | solution.py:40
  107.1 1.6 %collective-permute-start.13 = (f32[2304]{0:T(1024)S(1)}, f32[2304]{0:T(1024)S(1)}, u32[]{:S(2)}, u32[]{:S(2)}) collective-permute-start(f32[2304]{0:T(1024)S(1)} %add_add_fusion.4), channel_id=1, source_target_pairs={{0,1},{1,0},{2,3},{3,2},{4,5},{5,4},{6,7},{7,6},{8,9},{9,8},{10,11... | collective-permute-start | bytes 27656 | tf_op jit(solution)/shard_map/ppermute | solution.py:40
  (85 shorter events, 18.7 us)
Async XLA Ops:
  0.6 34.7 %copy-start = (bf16[768,1536]{1,0:T(8,128)(2,1)S(1)}, bf16[768,1536]{1,0:T(8,128)(2,1)}, u32[]{:S(2)}) copy-start(bf16[768,1536]{1,0:T(8,128)(2,1)} %param.13) | copy-start | bytes 7077892
  0.6 2.5 %copy-start.1 = (bf16[1,512,1536]{2,1,0:T(8,128)(2,1)S(1)}, bf16[1,512,1536]{2,1,0:T(8,128)(2,1)}, u32[]{:S(2)}) copy-start(bf16[1,512,1536]{2,1,0:T(8,128)(2,1)} %param.7) | copy-start | bytes 4718596
  0.7 2.5 %copy-start.11 = (f32[1536]{0:T(1024)S(1)}, f32[1536]{0:T(1024)}, u32[]{:S(2)}) copy-start(f32[1536]{0:T(1024)} %param.10) | copy-start | bytes 18436
  2.6 0.5 copy-start.12
  2.6 0.5 copy-start.14
  3.1 11.1 %copy-start.3 = (bf16[3,1536,768]{2,1,0:T(8,128)(2,1)S(1)}, bf16[3,1536,768]{2,1,0:T(8,128)(2,1)}, u32[]{:S(2)}) copy-start(bf16[3,1536,768]{2,1,0:T(8,128)(2,1)} %param.11) | copy-start | bytes 21233668
  4.5 18.6 %copy-start.7 = (bf16[256,1536]{1,0:T(8,128)(2,1)}, bf16[256,1536]{1,0:T(8,128)(2,1)S(1)}, u32[]{:S(2)}) copy-start(bf16[256,1536]{1,0:T(8,128)(2,1)S(1)} %get-tuple-element.47) | copy-start | bytes 2359300
  8.6 32.3 %collective-permute-start.2 = (bf16[256,768]{1,0:T(8,128)(2,1)}, bf16[256,768]{1,0:T(8,128)(2,1)}, u32[]{:S(2)}, u32[]{:S(2)}) collective-permute-start(bf16[256,768]{1,0:T(8,128)(2,1)} %fusion.81), channel_id=1, source_target_pairs={{0,4},{2,6},{4,8},{6,10},{8,12},{10,14},{12,16},{14,18},{16,20},{1... | collective-permute-start | bytes 1179656 | tf_op jit(solution)/shard_map/ppermute | solution.py:22
  15.7 25.2 %collective-permute-start.3 = (bf16[256,768]{1,0:T(8,128)(2,1)}, bf16[256,768]{1,0:T(8,128)(2,1)}, u32[]{:S(2)}, u32[]{:S(2)}) collective-permute-start(bf16[256,768]{1,0:T(8,128)(2,1)} %fusion.87), channel_id=1, source_target_pairs={{4,0},{6,2},{8,4},{10,6},{12,8},{14,10},{16,12},{18,14},{20,16},{2... | collective-permute-start | bytes 1179656 | tf_op jit(solution)/shard_map/ppermute | solution.py:22
  18.5 28.9 %collective-permute-start = (bf16[256,768]{1,0:T(8,128)(2,1)}, bf16[256,768]{1,0:T(8,128)(2,1)S(1)}, u32[]{:S(2)}, u32[]{:S(2)}) collective-permute-start(bf16[256,768]{1,0:T(8,128)(2,1)} %fusion.78), channel_id=1, source_target_pairs={{0,4},{2,6},{4,8},{6,10},{8,12},{10,14},{12,16},{14,18},{16,20},{1... | collective-permute-start | bytes 1179656 | tf_op jit(solution)/shard_map/ppermute | solution.py:22
  24.7 22.7 %collective-permute-start.1 = (bf16[256,768]{1,0:T(8,128)(2,1)}, bf16[256,768]{1,0:T(8,128)(2,1)}, u32[]{:S(2)}, u32[]{:S(2)}) collective-permute-start(bf16[256,768]{1,0:T(8,128)(2,1)} %fusion.84), channel_id=1, source_target_pairs={{4,0},{6,2},{8,4},{10,6},{12,8},{14,10},{16,12},{18,14},{20,16},{2... | collective-permute-start | bytes 1179656 | tf_op jit(solution)/shard_map/ppermute | solution.py:22
  29.3 3.4 %copy-start.8 = (bf16[256,1536]{1,0:T(8,128)(2,1)S(1)}, bf16[256,1536]{1,0:T(8,128)(2,1)}, u32[]{:S(2)}) copy-start(bf16[256,1536]{1,0:T(8,128)(2,1)} %copy-done.7) | copy-start | bytes 2359300
  32.7 2.6 %copy-start.4 = (bf16[1,512,1536]{2,1,0:T(8,128)(2,1)S(1)}, bf16[1,512,1536]{2,1,0:T(8,128)(2,1)}, u32[]{:S(2)}) copy-start(bf16[1,512,1536]{2,1,0:T(8,128)(2,1)} %param.8) | copy-start | bytes 4718596
  42.7 6.1 %copy-start.6 = (f32[256,768]{1,0:T(8,128)S(1)}, f32[256,768]{1,0:T(8,128)}, u32[]{:S(2)}) copy-start(f32[256,768]{1,0:T(8,128)} %fusion.106) | copy-start | bytes 2359300
  42.7 6.1 %copy-start.10 = (f32[768]{0:T(1024)S(1)}, f32[768]{0:T(1024)}, u32[]{:S(2)}) copy-start(f32[768]{0:T(1024)} %param.12) | copy-start | bytes 9220
  48.7 1.1 %copy-start.9 = (f32[256,768]{1,0:T(8,128)S(1)}, f32[256,768]{1,0:T(8,128)}, u32[]{:S(2)}) copy-start(f32[256,768]{1,0:T(8,128)} %fusion.104) | copy-start | bytes 2359300
  48.8 17.6 %slice-start = ((s8[7077888]{0:T(1024)(128)(4,1)}), s8[4194304]{0:T(1024)(128)(4,1)S(1)}, s32[]{:S(2)}) async-start(s8[7077888]{0:T(1024)(128)(4,1)} %bitcast.91), calls=%async_computation | async-start | bytes 8388608
  49.9 16.5 %slice-start.1 = ((s8[7077888]{0:T(1024)(128)(4,1)}), s8[2883584]{0:T(1024)(128)(4,1)S(1)}, s32[]{:S(2)}) async-start(s8[7077888]{0:T(1024)(128)(4,1)} %bitcast.91), calls=%async_computation.1 | async-start | bytes 5767168
  51.7 30.7 %collective-permute-start.4 = (bf16[256,768]{1,0:T(8,128)(2,1)S(1)}, bf16[256,768]{1,0:T(8,128)(2,1)S(1)}, u32[]{:S(2)}, u32[]{:S(2)}) collective-permute-start(bf16[256,768]{1,0:T(8,128)(2,1)S(1)} %get-tuple-element.50), channel_id=1, source_target_pairs={{0,4},{2,6},{4,8},{6,10},{8,12},{10,14},{12,16},{14,18},{16,20},{1... | collective-permute-start | bytes 1179656 | tf_op jit(solution)/shard_map/ppermute | solution.py:22
  56.0 26.4 %collective-permute-start.5 = (bf16[256,768]{1,0:T(8,128)(2,1)S(1)}, bf16[256,768]{1,0:T(8,128)(2,1)S(1)}, u32[]{:S(2)}, u32[]{:S(2)}) collective-permute-start(bf16[256,768]{1,0:T(8,128)(2,1)S(1)} %get-tuple-element.50), channel_id=1, source_target_pairs={{4,0},{6,2},{8,4},{10,6},{12,8},{14,10},{16,12},{18,14},{20,16},{2... | collective-permute-start | bytes 1179656 | tf_op jit(solution)/shard_map/ppermute | solution.py:22
  59.8 29.0 %collective-permute-start.6 = (bf16[256,768]{1,0:T(8,128)(2,1)S(1)}, bf16[256,768]{1,0:T(8,128)(2,1)S(1)}, u32[]{:S(2)}, u32[]{:S(2)}) collective-permute-start(bf16[256,768]{1,0:T(8,128)(2,1)S(1)} %get-tuple-element.48), channel_id=1, source_target_pairs={{0,4},{2,6},{4,8},{6,10},{8,12},{10,14},{12,16},{14,18},{16,20},{1... | collective-permute-start | bytes 1179656 | tf_op jit(solution)/shard_map/ppermute | solution.py:22
  64.9 24.7 %collective-permute-start.7 = (bf16[256,768]{1,0:T(8,128)(2,1)S(1)}, bf16[256,768]{1,0:T(8,128)(2,1)S(1)}, u32[]{:S(2)}, u32[]{:S(2)}) collective-permute-start(bf16[256,768]{1,0:T(8,128)(2,1)S(1)} %get-tuple-element.48), channel_id=1, source_target_pairs={{4,0},{6,2},{8,4},{10,6},{12,8},{14,10},{16,12},{18,14},{20,16},{2... | collective-permute-start | bytes 1179656 | tf_op jit(solution)/shard_map/ppermute | solution.py:22
  82.4 1.4 %copy-start.2 = (bf16[1,512,1536]{2,1,0:T(8,128)(2,1)S(1)}, bf16[1,512,1536]{2,1,0:T(8,128)(2,1)}, u32[]{:S(2)}) copy-start(bf16[1,512,1536]{2,1,0:T(8,128)(2,1)} %param.7) | copy-start | bytes 4718596
  89.5 8.3 %copy-start.13 = (f32[256]{0:T(256)S(1)}, f32[256]{0:T(256)}, u32[]{:S(2)}) copy-start(f32[256]{0:T(256)} %copy-done.12) | copy-start | bytes 3076
  89.6 8.3 %copy-start.15 = (f32[256]{0:T(256)S(1)}, f32[256]{0:T(256)}, u32[]{:S(2)}) copy-start(f32[256]{0:T(256)} %copy-done.14) | copy-start | bytes 3076
  89.6 8.3 %copy-start.5 = (bf16[1,512,1536]{2,1,0:T(8,128)(2,1)S(1)}, bf16[1,512,1536]{2,1,0:T(8,128)(2,1)}, u32[]{:S(2)}) copy-start(bf16[1,512,1536]{2,1,0:T(8,128)(2,1)} %param.8) | copy-start | bytes 4718596
  92.1 7.5 %collective-permute-start.8 = (f32[2304]{0:T(1024)S(1)}, f32[2304]{0:T(1024)S(1)}, u32[]{:S(2)}, u32[]{:S(2)}) collective-permute-start(f32[2304]{0:T(1024)S(1)} %pad_maximum_fusion), channel_id=1, source_target_pairs={{0,16},{1,17},{2,18},{3,19},{4,20},{5,21},{6,22},{7,23},{8,24},{9,... | collective-permute-start | bytes 27656 | tf_op jit(solution)/shard_map/ppermute | solution.py:40
  99.6 3.8 %collective-permute-start.9 = (f32[2304]{0:T(1024)S(1)}, f32[2304]{0:T(1024)S(1)}, u32[]{:S(2)}, u32[]{:S(2)}) collective-permute-start(f32[2304]{0:T(1024)S(1)} %fusion.118), channel_id=1, source_target_pairs={{0,8},{1,9},{2,10},{3,11},{4,12},{5,13},{6,14},{7,15},{8,0},{9,1},... | collective-permute-start | bytes 27656 | tf_op jit(solution)/shard_map/ppermute | solution.py:40
  103.4 3.1 %collective-permute-start.10 = (f32[2304]{0:T(1024)S(1)}, f32[2304]{0:T(1024)S(1)}, u32[]{:S(2)}, u32[]{:S(2)}) collective-permute-start(f32[2304]{0:T(1024)S(1)} %add.233), channel_id=1, source_target_pairs={{0,2},{1,3},{2,0},{3,1},{4,6},{5,7},{6,4},{7,5},{8,10},{9,11},{10,... | collective-permute-start | bytes 27656 | tf_op jit(solution)/shard_map/ppermute | solution.py:40
  103.4 3.7 %collective-permute-start.11 = (f32[2304]{0:T(1024)S(1)}, f32[2304]{0:T(1024)S(1)}, u32[]{:S(2)}, u32[]{:S(2)}) collective-permute-start(f32[2304]{0:T(1024)S(1)} %add.233), channel_id=1, source_target_pairs={{0,4},{1,5},{2,6},{3,7},{4,0},{5,1},{6,2},{7,3},{8,12},{9,13},{10,... | collective-permute-start | bytes 27656 | tf_op jit(solution)/shard_map/ppermute | solution.py:40
  103.7 3.4 %collective-permute-start.12 = (f32[2304]{0:T(1024)S(1)}, f32[2304]{0:T(1024)S(1)}, u32[]{:S(2)}, u32[]{:S(2)}) collective-permute-start(f32[2304]{0:T(1024)S(1)} %add.233), channel_id=1, source_target_pairs={{0,6},{1,7},{2,4},{3,5},{4,2},{5,3},{6,0},{7,1},{8,14},{9,15},{10,... | collective-permute-start | bytes 27656 | tf_op jit(solution)/shard_map/ppermute | solution.py:40
  107.1 3.8 %collective-permute-start.13 = (f32[2304]{0:T(1024)S(1)}, f32[2304]{0:T(1024)S(1)}, u32[]{:S(2)}, u32[]{:S(2)}) collective-permute-start(f32[2304]{0:T(1024)S(1)} %add_add_fusion.4), channel_id=1, source_target_pairs={{0,1},{1,0},{2,3},{3,2},{4,5},{5,4},{6,7},{7,6},{8,9},{9,8},{10,11... | collective-permute-start | bytes 27656 | tf_op jit(solution)/shard_map/ppermute | solution.py:40

commit v7 on v6

--- a/solution.py
+++ b/solution.py
@@ -3,6 +3,7 @@
 import jax
 import jax.numpy as jnp
 from jax import lax
+from jax.experimental import pallas as pl
 from jax.sharding import PartitionSpec as P
 
 SPAN = 2
@@ -11,6 +12,7 @@
 STAGES = (2, 4, 2, 2)
 EARLY = True
 LATE_OUTPUT = True
+BLOCK = 128
 
 
 epsilon = 1e-06
@@ -25,6 +27,46 @@
 def norm_activate(values, scales):
     mean_square = jnp.mean(values * values, axis=-1, keepdims=True)
     return jax.nn.gelu(values * lax.rsqrt(mean_square + epsilon) * scales, approximate=True)
+
+
+def middle_kernel(center_ref, before_ref, after_ref, bv_ref, av_ref, grad_ref, gain_ref,
+                  middle_ref, gc_ref, terms_ref):
+    values = (center_ref[...] + bv_ref[...] * before_ref[...].astype(jnp.float32)
+              + av_ref[...] * after_ref[...].astype(jnp.float32))
+    width = values.shape[-1]
+    scale = lax.rsqrt(jnp.sum(values * values, axis=-1, keepdims=True) / width + epsilon)
+    gain = gain_ref[...]
+    unit = values * scale
+    z = unit * gain
+    k = math.sqrt(2.0 / math.pi)
+    t = jnp.tanh(k * (z + 0.044715 * z * z * z))
+    middle_ref[...] = (0.5 * z * (1.0 + t)).astype(middle_ref.dtype)
+    slope = 0.5 * (1.0 + t) + 0.5 * z * (1.0 - t * t) * k * (1.0 + 3.0 * 0.044715 * z * z)
+    gz = grad_ref[...] * slope
+    terms = jnp.sum(gz * unit, axis=0, keepdims=True)
+    terms_ref[...] = jnp.broadcast_to(terms, terms_ref.shape)
+    through = gz * gain
+    inner = jnp.sum(through * values, axis=-1, keepdims=True)
+    gc_ref[...] = (scale * through - values * (scale * scale * scale / width * inner)).astype(gc_ref.dtype)
+
+
+def middle_block(center, before, after, bv, av, grad, gain):
+    rows, width = center.shape
+    blocks = rows // BLOCK
+    row = pl.BlockSpec((BLOCK, width), lambda i: (i, 0))
+    col = pl.BlockSpec((BLOCK, 1), lambda i: (i, 0))
+    middle, gc, terms = pl.pallas_call(
+        middle_kernel,
+        grid=(blocks,),
+        in_specs=[row, row, row, col, col, row, pl.BlockSpec((1, width), lambda i: (0, 0))],
+        out_specs=[row, row, pl.BlockSpec((8, width), lambda i: (i, 0))],
+        out_shape=[
+            jax.ShapeDtypeStruct((rows, width), jnp.bfloat16),
+            jax.ShapeDtypeStruct((rows, width), jnp.bfloat16),
+            jax.ShapeDtypeStruct((blocks * 8, width), jnp.float32),
+        ],
+    )(center, before, after, bv, av, grad, gain.reshape(1, width))
+    return middle, gc, jnp.sum(terms.reshape(blocks, 8, width)[:, 0], axis=0)
 
 
 def contig_owner(lengths, positions):
@@ -108,12 +150,10 @@
         grad_middle = jnp.dot(ch["upstream"], point_weights.T, preferred_element_type=jnp.float32)
         if EARLY:
             combined, grad_middle = lax.optimization_barrier((combined, grad_middle))
-        combined = combined + ch["before_valid"] * ch["product_before"].astype(jnp.float32)
-        combined = combined + ch["after_valid"] * ch["product_after"].astype(jnp.float32)
-        middle_f, middle_vjp = jax.vjp(norm_activate, combined, gain_middle)
-        ch["middle"] = middle_f.astype(jnp.bfloat16)
-        grad_combined_f, ch["middle_terms"] = middle_vjp(grad_middle)
-        grad_combined = grad_combined_f.astype(jnp.bfloat16)
+        ch["middle"], grad_combined, ch["middle_terms"] = middle_block(
+            combined, ch["product_before"], ch["product_after"], ch["before_valid"],
+            ch["after_valid"], grad_middle, gain_middle,
+        )
         ch["grad_combined"] = grad_combined
         ch["combined_before"] = shifted(grad_combined, "seq", SPAN)
         ch["combined_after"] = shifted(grad_combined, "seq", -SPAN)

time: 113 us -> 112 us (level)
  waiting for transfers between devices: 25.8 us -> 15.4 us
  Pallas kernels: 0 us -> 6.91 us
  matrix products: 28.7 us -> 34.7 us
  other arithmetic: 19.3 us -> 17 us
  starting transfers between devices: 35.8 us -> 34.3 us
    ppermute x8, waiting for transfers between devices: 23.1 us -> 11.6 us  [shifted(): return lax.ppermute(x, axis, pairs)]
    pallas_call x0 -> x2, Pallas kernels: none -> 6.91 us  [middle_block(): pl.pallas_call(middle_kernel, grid=(blocks,), in_specs=[row, row, row, co...]
    reduce_sum x3 -> x1, other arithmetic: 4.96 us -> 1.9 us  [norm_activate(): mean_square = jnp.mean(values * values, axis=-1, keepdims=True)]
    dot_general x2, matrix products: 3.27 us -> 6.01 us  [body(): jnp.dot(ch['grad_combined'], tap_center.T, preferred_element_type=jnp.flo...]
    ppermute x6, starting transfers between devices: 11 us -> 8.54 us  [group_sum(): parts.append(lax.ppermute(x, axis, pairs))]
    dot_general x2, matrix products: 1.64 us -> 3.43 us  [body(): jnp.dot(ch['combined_before'], tap_after.T, preferred_element_type=jnp.fl...]
    convert_element_type x2, other arithmetic: 0.01 us -> 1.49 us  [body(): before_valid = ((positions >= tap_reach) & (contig_owner(lengths, positio...]
    dot_general x2, matrix products: 3.42 us -> 4.65 us  [body(): jnp.dot(ch['upstream'], point_weights.T, preferred_element_type=jnp.float32)]
  transfers between devices with their start and end apart: 14 -> 14, of which waited for: 6 -> 5; matrix products, arithmetic and copies ran while one was open for 29% -> 36% of each run, Pallas kernels for 0% -> 6%
where the time goes in v7:
time: 112 us
  matrix products  34.7 us (31%)
  starting transfers between devices  34.3 us (31%)
  other arithmetic  17 us (15%)
  waiting for transfers between devices  15.4 us (14%)
  Pallas kernels  6.91 us (6%)
  local copies, waits for them, and re-layouts  2.18 us (2%)
    ppermute x8, starting transfers between devices, shifted(): return lax.ppermute(x, axis, pairs)  25.8 us
    ppermute x8, waiting for transfers between devices, shifted(): return lax.ppermute(x, axis, pairs)  11.6 us
    ppermute x6, starting transfers between devices, group_sum(): parts.append(lax.ppermute(x, axis, pairs))  8.54 us
    dot_general x2, matrix products, body(): jnp.dot(ch['hidden'], tap_center, preferred_element_type=jnp.float32)  6.91 us
    pallas_call x2, Pallas kernels, middle_block(): pl.pallas_call(middle_kernel, grid=(blocks,), in_specs=[row, row, row, co...  6.91 us
    dot_general x2, matrix products, body(): jnp.dot(ch['grad_combined'], tap_center.T, preferred_element_type=jnp.flo...  6.01 us
    dot_general x2, matrix products, body(): jnp.dot(hidden, tap_before, preferred_element_type=jnp.float32)  5.62 us
    dot_general x2, matrix products, body(): jnp.dot(ch['upstream'], point_weights.T, preferred_element_type=jnp.float32)  4.65 us
  transfers between devices with their start and end apart: 14, of which 5 were waited for; matrix products, arithmetic and copies ran while one was open for 36% of the time, Pallas kernels for 6%

profile of v7, /device:TPU:0, one launch (start us, length us, event | category | flops | bytes accessed | tf_op | source)
XLA Modules:
  0.0 111.6 jit_solution(10392838425525041542)
XLA Ops:
  0.7 1.9 %fusion.56 = (f32[256]{0:T(256)S(1)}, f32[256]{0:T(256)S(1)}) fusion(bf16[1,512,1536]{2,1,0:T(8,128)(2,1)} %param.7), kind=kLoop, calls=%fused_computation.78 | loop fusion | flops 2358784 | bytes 1574912 | tf_op jit(solution)/shard_map/jvp()/reduce_sum | solution.py:28
  3.2 1.4 %fusion.34 = (bf16[256,1536]{1,0:T(8,128)(2,1)S(1)}, bf16[256,1536]{1,0:T(8,128)(2,1)S(1)}) fusion(f32[256]{0:T(256)S(1)} %fusion.109, f32[1536]{0:T(1024)S(1)} %copy-done.7, bf16[1,512,1536]{2,1,0:T(8,128)(2,1)S(1)} %copy-done.1, f32[256]{0:T(256)S(1)} %fusion.108), kind=kLoop, calls=%fused_computation.56 | loop fusion | flops 9437184 | bytes 3153920 | tf_op jit(solution)/shard_map/convert_element_type | solution.py:139
  4.6 4.1 %fusion.77 = bf16[256,768]{1,0:T(8,128)(2,1)} fusion(bf16[256,1536]{1,0:T(8,128)(2,1)S(1)} %get-tuple-element.56, bf16[3,1536,768]{2,1,0:T(8,128)(2,1)} %param.11), kind=kOutput, calls=%fused_computation.95 | convolution fusion | flops 604176384 | bytes 3538944 | tf_op jit(solution)/shard_map/dot_general | solution.py:140
  8.7 5.6 %collective-permute-start.2 = (bf16[256,768]{1,0:T(8,128)(2,1)}, bf16[256,768]{1,0:T(8,128)(2,1)}, u32[]{:S(2)}, u32[]{:S(2)}) collective-permute-start(bf16[256,768]{1,0:T(8,128)(2,1)} %fusion.77), channel_id=1, source_target_pairs={{0,4},{2,6},{4,8},{6,10},{8,12},{10,14},{12,16},{14,18},{16,20},{1... | collective-permute-start | bytes 1179656 | tf_op jit(solution)/shard_map/ppermute | solution.py:24
  14.3 1.5 %fusion.83 = bf16[256,768]{1,0:T(8,128)(2,1)} fusion(bf16[256,1536]{1,0:T(8,128)(2,1)S(1)} %get-tuple-element.56, bf16[3,1536,768]{2,1,0:T(8,128)(2,1)S(1)} %copy-done.13), kind=kOutput, calls=%fused_computation.97 | convolution fusion | flops 604176384 | bytes 3538944 | tf_op jit(solution)/shard_map/dot_general | solution.py:141
  15.8 1.3 %collective-permute-start.3 = (bf16[256,768]{1,0:T(8,128)(2,1)}, bf16[256,768]{1,0:T(8,128)(2,1)}, u32[]{:S(2)}, u32[]{:S(2)}) collective-permute-start(bf16[256,768]{1,0:T(8,128)(2,1)} %fusion.83), channel_id=1, source_target_pairs={{4,0},{6,2},{8,4},{10,6},{12,8},{14,10},{16,12},{18,14},{20,16},{2... | collective-permute-start | bytes 1179656 | tf_op jit(solution)/shard_map/ppermute | solution.py:24
  17.1 1.6 %fusion.74 = bf16[256,768]{1,0:T(8,128)(2,1)} fusion(bf16[256,1536]{1,0:T(8,128)(2,1)S(1)} %get-tuple-element.57, bf16[3,1536,768]{2,1,0:T(8,128)(2,1)S(1)} %copy-done.13), kind=kOutput, calls=%fused_computation.94 | convolution fusion | flops 604176384 | bytes 3538944 | tf_op jit(solution)/shard_map/dot_general | solution.py:140
  18.6 4.6 %collective-permute-start = (bf16[256,768]{1,0:T(8,128)(2,1)}, bf16[256,768]{1,0:T(8,128)(2,1)S(1)}, u32[]{:S(2)}, u32[]{:S(2)}) collective-permute-start(bf16[256,768]{1,0:T(8,128)(2,1)} %fusion.74), channel_id=1, source_target_pairs={{0,4},{2,6},{4,8},{6,10},{8,12},{10,14},{12,16},{14,18},{16,20},{1... | collective-permute-start | bytes 1179656 | tf_op jit(solution)/shard_map/ppermute | solution.py:24
  23.2 1.5 %fusion.80 = bf16[256,768]{1,0:T(8,128)(2,1)} fusion(bf16[256,1536]{1,0:T(8,128)(2,1)S(1)} %get-tuple-element.57, bf16[3,1536,768]{2,1,0:T(8,128)(2,1)S(1)} %copy-done.13), kind=kOutput, calls=%fused_computation.96 | convolution fusion | flops 604176384 | bytes 3538944 | tf_op jit(solution)/shard_map/dot_general | solution.py:141
  24.7 1.3 %collective-permute-start.1 = (bf16[256,768]{1,0:T(8,128)(2,1)}, bf16[256,768]{1,0:T(8,128)(2,1)}, u32[]{:S(2)}, u32[]{:S(2)}) collective-permute-start(bf16[256,768]{1,0:T(8,128)(2,1)} %fusion.80), channel_id=1, source_target_pairs={{4,0},{6,2},{8,4},{10,6},{12,8},{14,10},{16,12},{18,14},{20,16},{2... | collective-permute-start | bytes 1179656 | tf_op jit(solution)/shard_map/ppermute | solution.py:24
  29.5 3.6 %fusion.18.center_ref = f32[256,768]{1,0:T(8,128)} fusion(bf16[256,1536]{1,0:T(8,128)(2,1)} %copy-done.5, bf16[3,1536,768]{2,1,0:T(8,128)(2,1)} %param.11), kind=kOutput, calls=%fused_computation.36 | convolution fusion | flops 603979776 | bytes 3932160 | tf_op jit(solution)/shard_map/dot_general | solution.py:149
  33.1 3.3 %fusion.20.center_ref = f32[256,768]{1,0:T(8,128)} fusion(bf16[256,1536]{1,0:T(8,128)(2,1)S(1)} %get-tuple-element.57, bf16[3,1536,768]{2,1,0:T(8,128)(2,1)} %param.11), kind=kOutput, calls=%fused_computation.38 | convolution fusion | flops 603979776 | bytes 3932160 | tf_op jit(solution)/shard_map/dot_general | solution.py:149
  38.8 2.9 %fusion.86.grad_ref = f32[256,768]{1,0:T(8,128)} fusion(bf16[768,1536]{1,0:T(8,128)(2,1)S(1)} %copy-done, bf16[1,512,1536]{2,1,0:T(8,128)(2,1)} %param.8), kind=kOutput, calls=%fused_computation.98 | convolution fusion | flops 603979776 | bytes 3932160 | tf_op jit(solution)/shard_map/dot_general | solution.py:150
  43.1 1.7 %fusion.88.grad_ref = f32[256,768]{1,0:T(8,128)} fusion(bf16[768,1536]{1,0:T(8,128)(2,1)S(1)} %copy-done, bf16[1,512,1536]{2,1,0:T(8,128)(2,1)S(1)} %copy-done.3), kind=kOutput, calls=%fused_computation.100 | convolution fusion | flops 603979776 | bytes 3932160 | tf_op jit(solution)/shard_map/dot_general | solution.py:150
  44.8 3.5 %shard_map.103 = (bf16[256,768]{1,0:T(8,128)(2,1)}, bf16[256,768]{1,0:T(8,128)(2,1)}, f32[16,768]{1,0:T(8,128)}) custom-call(f32[256,768]{1,0:T(8,128)} %fusion.18.center_ref, bf16[256,768]{1,0:T(8,128)(2,1)} %collective-permute-done.2.before_ref, bf16[256,768]{1,0:T(8,128)(2,1)} %collective-permute-done.3.after_ref, f32[256,1]{1,0:T(8,128)} %fusion.101.bv_ref, ...), custom_call_target="tpu_custom_call" | custom-call | tf_op jit(solution)/shard_map/pallas_call | solution.py:58
  48.3 4.5 %collective-permute-start.4 = (bf16[256,768]{1,0:T(8,128)(2,1)}, bf16[256,768]{1,0:T(8,128)(2,1)S(1)}, u32[]{:S(2)}, u32[]{:S(2)}) collective-permute-start(bf16[256,768]{1,0:T(8,128)(2,1)} %get-tuple-element.24), channel_id=1, source_target_pairs={{0,4},{2,6},{4,8},{6,10},{8,12},{10,14},{12,16},{14,18},{16,20},{1... | collective-permute-start | bytes 1179656 | tf_op jit(solution)/shard_map/ppermute | solution.py:24
  52.8 1.3 %collective-permute-start.5 = (bf16[256,768]{1,0:T(8,128)(2,1)}, bf16[256,768]{1,0:T(8,128)(2,1)}, u32[]{:S(2)}, u32[]{:S(2)}) collective-permute-start(bf16[256,768]{1,0:T(8,128)(2,1)} %get-tuple-element.24), channel_id=1, source_target_pairs={{4,0},{6,2},{8,4},{10,6},{12,8},{14,10},{16,12},{18,14},{20,16},{2... | collective-permute-start | bytes 1179656 | tf_op jit(solution)/shard_map/ppermute | solution.py:24
  56.4 3.4 %shard_map.102 = (bf16[256,768]{1,0:T(8,128)(2,1)}, bf16[256,768]{1,0:T(8,128)(2,1)}, f32[16,768]{1,0:T(8,128)}) custom-call(f32[256,768]{1,0:T(8,128)} %fusion.20.center_ref, bf16[256,768]{1,0:T(8,128)(2,1)} %copy-done.6, bf16[256,768]{1,0:T(8,128)(2,1)} %collective-permute-done.1.after_ref, f32[256,1]{1,0:T(8,128)} %fusion.97.bv_ref, ...), custom_call_target="tpu_custom_call" | custom-call | tf_op jit(solution)/shard_map/pallas_call | solution.py:58
  59.9 1.3 %collective-permute-start.7 = (bf16[256,768]{1,0:T(8,128)(2,1)}, bf16[256,768]{1,0:T(8,128)(2,1)S(1)}, u32[]{:S(2)}, u32[]{:S(2)}) collective-permute-start(bf16[256,768]{1,0:T(8,128)(2,1)} %get-tuple-element.27), channel_id=1, source_target_pairs={{4,0},{6,2},{8,4},{10,6},{12,8},{14,10},{16,12},{18,14},{20,16},{2... | collective-permute-start | bytes 1179656 | tf_op jit(solution)/shard_map/ppermute | solution.py:24
  61.2 6.0 %collective-permute-start.6 = (bf16[256,768]{1,0:T(8,128)(2,1)}, bf16[256,768]{1,0:T(8,128)(2,1)S(1)}, u32[]{:S(2)}, u32[]{:S(2)}) collective-permute-start(bf16[256,768]{1,0:T(8,128)(2,1)} %get-tuple-element.27), channel_id=1, source_target_pairs={{0,4},{2,6},{4,8},{6,10},{8,12},{10,14},{12,16},{14,18},{16,20},{1... | collective-permute-start | bytes 1179656 | tf_op jit(solution)/shard_map/ppermute | solution.py:24
  68.0 11.5 %collective-permute-done.4 = bf16[256,768]{1,0:T(8,128)(2,1)S(1)} collective-permute-done((bf16[256,768]{1,0:T(8,128)(2,1)}, bf16[256,768]{1,0:T(8,128)(2,1)S(1)}, u32[]{:S(2)}, u32[]{:S(2)}) %collective-permute-start.4) | collective-permute-done | bytes 393248 | tf_op jit(solution)/shard_map/ppermute | solution.py:24
  79.5 2.6 %convolution_multiply_fusion = f32[256,1536]{1,0:T(8,128)S(1)} fusion(bf16[256,768]{1,0:T(8,128)(2,1)} %collective-permute-done.5, bf16[3,1536,768]{2,1,0:T(8,128)(2,1)} %param.11, f32[256]{0:T(256)S(1)} %get-tuple-element.52), kind=kOutput, calls=%fused_computation.10 | convolution fusion | flops 604372992 | bytes 4326400 | tf_op jit(solution)/shard_map/dot_general | solution.py:179
  82.2 2.6 %convolution_multiply_fusion.1 = f32[256,1536]{1,0:T(8,128)S(1)} fusion(bf16[256,768]{1,0:T(8,128)(2,1)S(1)} %collective-permute-done.4, bf16[3,1536,768]{2,1,0:T(8,128)(2,1)} %param.11, f32[256]{0:T(256)S(1)} %get-tuple-element.58), kind=kOutput, calls=%fused_computation.11 | convolution fusion | flops 604372992 | bytes 4326400 | tf_op jit(solution)/shard_map/dot_general | solution.py:176
  84.9 3.5 %fusion.49 = f32[256,1536]{1,0:T(8,128)S(1)} fusion(f32[256,1536]{1,0:T(8,128)S(1)} %convolution_multiply_fusion, f32[256,1536]{1,0:T(8,128)S(1)} %convolution_multiply_fusion.1, bf16[256,768]{1,0:T(8,128)(2,1)S(1)} %copy-done.16, bf16[3,1536,768]{2,1,0:T(8,128)(2,1)} %param.11, f32[256]{0:T(256)S(1)} %fusion.109, f32[1536]{0:T(1024)S(1)} %copy-done.7, ...), kind=kOutput, calls=%fused_computation.71 | convolution fusion | flops 613416960 | bytes 8264704 | tf_op jit(solution)/shard_map/dot_general | solution.py:175
  90.3 2.5 %fusion.43 = (f32[1536]{0:T(1024)S(1)}, f32[256]{0:T(256)S(1)}, f32[256]{0:T(256)S(1)}, f32[1536]{0:T(1024)S(1)}, f32[256,1536]{1,0:T(8,128)S(1)}) fusion(f32[256]{0:T(256)S(1)} %fusion.108, bf16[1,512,1536]{2,1,0:T(8,128)(2,1)S(1)} %copy-done.2, f32[1536]{0:T(1024)S(1)} %copy-done.7, f32[256,1536]{1,0:T(8,128)S(1)} %fusion.49, f32[256]{0:T(256)S(1)} %fusion.109, ...), kind=kOutput, calls=%fused_computation.65 | convolution fusion | flops 618131968 | bytes 10641408 | tf_op jit(solution)/shard_map/dot_general | solution.py:175
  92.8 3.4 %collective-permute-start.8 = (f32[2304]{0:T(1024)S(1)}, f32[2304]{0:T(1024)S(1)}, u32[]{:S(2)}, u32[]{:S(2)}) collective-permute-start(f32[2304]{0:T(1024)S(1)} %pad_maximum_fusion), channel_id=1, source_target_pairs={{0,16},{1,17},{2,18},{3,19},{4,20},{5,21},{6,22},{7,23},{8,24},{9,... | collective-permute-start | bytes 27656 | tf_op jit(solution)/shard_map/ppermute | solution.py:82
  98.0 1.8 %collective-permute-start.9 = (f32[2304]{0:T(1024)S(1)}, f32[2304]{0:T(1024)S(1)}, u32[]{:S(2)}, u32[]{:S(2)}) collective-permute-start(f32[2304]{0:T(1024)S(1)} %fusion.110), channel_id=1, source_target_pairs={{0,8},{1,9},{2,10},{3,11},{4,12},{5,13},{6,14},{7,15},{8,0},{9,1},... | collective-permute-start | bytes 27656 | tf_op jit(solution)/shard_map/ppermute | solution.py:82
  100.6 1.2 %collective-permute-done.9 = f32[2304]{0:T(1024)S(1)} collective-permute-done((f32[2304]{0:T(1024)S(1)}, f32[2304]{0:T(1024)S(1)}, u32[]{:S(2)}, u32[]{:S(2)}) %collective-permute-start.9) | collective-permute-done | bytes 9248 | tf_op jit(solution)/shard_map/ppermute | solution.py:82
  101.8 1.8 %collective-permute-start.11 = (f32[2304]{0:T(1024)S(1)}, f32[2304]{0:T(1024)S(1)}, u32[]{:S(2)}, u32[]{:S(2)}) collective-permute-start(f32[2304]{0:T(1024)S(1)} %add.201), channel_id=1, source_target_pairs={{0,4},{1,5},{2,6},{3,7},{4,0},{5,1},{6,2},{7,3},{8,12},{9,13},{10,... | collective-permute-start | bytes 27656 | tf_op jit(solution)/shard_map/ppermute | solution.py:82
  103.7 1.2 %maximum_bitcast_fusion.1 = bf16[1,512,1536]{2,1,0:T(8,128)(2,1)} fusion(bf16[256,1536]{1,0:T(8,128)(2,1)S(1)} %get-tuple-element.55, bf16[256,1536]{1,0:T(8,128)(2,1)S(1)} %get-tuple-element.54), kind=kLoop, calls=%fused_computation.81 | loop fusion | flops 3145728 | bytes 3145728 | tf_op jit(solution)/shard_map/broadcast_in_dim | solution.py:191
  106.7 1.5 %collective-permute-start.13 = (f32[2304]{0:T(1024)S(1)}, f32[2304]{0:T(1024)S(1)}, u32[]{:S(2)}, u32[]{:S(2)}) collective-permute-start(f32[2304]{0:T(1024)S(1)} %add_add_fusion.2), channel_id=1, source_target_pairs={{0,1},{1,0},{2,3},{3,2},{4,5},{5,4},{6,7},{7,6},{8,9},{9,8},{10,11... | collective-permute-start | bytes 27656 | tf_op jit(solution)/shard_map/ppermute | solution.py:82
  108.2 1.2 %maximum_bitcast_fusion = bf16[1,512,1536]{2,1,0:T(8,128)(2,1)} fusion(bf16[256,1536]{1,0:T(8,128)(2,1)S(1)} %fusion.3, bf16[256,1536]{1,0:T(8,128)(2,1)S(1)} %fusion.2), kind=kLoop, calls=%fused_computation.80 | loop fusion | flops 3145728 | bytes 3145728 | tf_op jit(solution)/shard_map/broadcast_in_dim | solution.py:190
  (88 shorter events, 19.4 us)
Async XLA Ops:
  0.6 38.2 %copy-start = (bf16[768,1536]{1,0:T(8,128)(2,1)S(1)}, bf16[768,1536]{1,0:T(8,128)(2,1)}, u32[]{:S(2)}) copy-start(bf16[768,1536]{1,0:T(8,128)(2,1)} %param.13) | copy-start | bytes 7077892
  0.6 2.5 %copy-start.1 = (bf16[1,512,1536]{2,1,0:T(8,128)(2,1)S(1)}, bf16[1,512,1536]{2,1,0:T(8,128)(2,1)}, u32[]{:S(2)}) copy-start(bf16[1,512,1536]{2,1,0:T(8,128)(2,1)} %param.7) | copy-start | bytes 4718596
  0.7 2.5 %copy-start.7 = (f32[1536]{0:T(1024)S(1)}, f32[1536]{0:T(1024)}, u32[]{:S(2)}) copy-start(f32[1536]{0:T(1024)} %param.10) | copy-start | bytes 18436
  3.2 11.1 %copy-start.13 = (bf16[3,1536,768]{2,1,0:T(8,128)(2,1)S(1)}, bf16[3,1536,768]{2,1,0:T(8,128)(2,1)}, u32[]{:S(2)}) copy-start(bf16[3,1536,768]{2,1,0:T(8,128)(2,1)} %param.11) | copy-start | bytes 21233668
  4.6 9.7 %copy-start.5 = (bf16[256,1536]{1,0:T(8,128)(2,1)}, bf16[256,1536]{1,0:T(8,128)(2,1)S(1)}, u32[]{:S(2)}) copy-start(bf16[256,1536]{1,0:T(8,128)(2,1)S(1)} %get-tuple-element.56) | copy-start | bytes 2359300
  8.7 36.1 %collective-permute-start.2 = (bf16[256,768]{1,0:T(8,128)(2,1)}, bf16[256,768]{1,0:T(8,128)(2,1)}, u32[]{:S(2)}, u32[]{:S(2)}) collective-permute-start(bf16[256,768]{1,0:T(8,128)(2,1)} %fusion.77), channel_id=1, source_target_pairs={{0,4},{2,6},{4,8},{6,10},{8,12},{10,14},{12,16},{14,18},{16,20},{1... | collective-permute-start | bytes 1179656 | tf_op jit(solution)/shard_map/ppermute | solution.py:24
  15.8 29.0 %collective-permute-start.3 = (bf16[256,768]{1,0:T(8,128)(2,1)}, bf16[256,768]{1,0:T(8,128)(2,1)}, u32[]{:S(2)}, u32[]{:S(2)}) collective-permute-start(bf16[256,768]{1,0:T(8,128)(2,1)} %fusion.83), channel_id=1, source_target_pairs={{4,0},{6,2},{8,4},{10,6},{12,8},{14,10},{16,12},{18,14},{20,16},{2... | collective-permute-start | bytes 1179656 | tf_op jit(solution)/shard_map/ppermute | solution.py:24
  18.6 37.0 %collective-permute-start = (bf16[256,768]{1,0:T(8,128)(2,1)}, bf16[256,768]{1,0:T(8,128)(2,1)S(1)}, u32[]{:S(2)}, u32[]{:S(2)}) collective-permute-start(bf16[256,768]{1,0:T(8,128)(2,1)} %fusion.74), channel_id=1, source_target_pairs={{0,4},{2,6},{4,8},{6,10},{8,12},{10,14},{12,16},{14,18},{16,20},{1... | collective-permute-start | bytes 1179656 | tf_op jit(solution)/shard_map/ppermute | solution.py:24
  24.7 30.9 %collective-permute-start.1 = (bf16[256,768]{1,0:T(8,128)(2,1)}, bf16[256,768]{1,0:T(8,128)(2,1)}, u32[]{:S(2)}, u32[]{:S(2)}) collective-permute-start(bf16[256,768]{1,0:T(8,128)(2,1)} %fusion.80), channel_id=1, source_target_pairs={{4,0},{6,2},{8,4},{10,6},{12,8},{14,10},{16,12},{18,14},{20,16},{2... | collective-permute-start | bytes 1179656 | tf_op jit(solution)/shard_map/ppermute | solution.py:24
  38.8 2.9 %copy-start.12 = (f32[768]{0:T(1024)S(1)}, f32[768]{0:T(1024)}, u32[]{:S(2)}) copy-start(f32[768]{0:T(1024)} %param.12) | copy-start | bytes 9220
  38.8 4.3 %copy-start.3 = (bf16[1,512,1536]{2,1,0:T(8,128)(2,1)S(1)}, bf16[1,512,1536]{2,1,0:T(8,128)(2,1)}, u32[]{:S(2)}) copy-start(bf16[1,512,1536]{2,1,0:T(8,128)(2,1)} %param.8) | copy-start | bytes 4718596
  48.3 31.3 %collective-permute-start.4 = (bf16[256,768]{1,0:T(8,128)(2,1)}, bf16[256,768]{1,0:T(8,128)(2,1)S(1)}, u32[]{:S(2)}, u32[]{:S(2)}) collective-permute-start(bf16[256,768]{1,0:T(8,128)(2,1)} %get-tuple-element.24), channel_id=1, source_target_pairs={{0,4},{2,6},{4,8},{6,10},{8,12},{10,14},{12,16},{14,18},{16,20},{1... | collective-permute-start | bytes 1179656 | tf_op jit(solution)/shard_map/ppermute | solution.py:24
  52.8 26.7 %collective-permute-start.5 = (bf16[256,768]{1,0:T(8,128)(2,1)}, bf16[256,768]{1,0:T(8,128)(2,1)}, u32[]{:S(2)}, u32[]{:S(2)}) collective-permute-start(bf16[256,768]{1,0:T(8,128)(2,1)} %get-tuple-element.24), channel_id=1, source_target_pairs={{4,0},{6,2},{8,4},{10,6},{12,8},{14,10},{16,12},{18,14},{20,16},{2... | collective-permute-start | bytes 1179656 | tf_op jit(solution)/shard_map/ppermute | solution.py:24
  55.7 0.7 copy-start.6
  59.9 28.5 %collective-permute-start.7 = (bf16[256,768]{1,0:T(8,128)(2,1)}, bf16[256,768]{1,0:T(8,128)(2,1)S(1)}, u32[]{:S(2)}, u32[]{:S(2)}) collective-permute-start(bf16[256,768]{1,0:T(8,128)(2,1)} %get-tuple-element.27), channel_id=1, source_target_pairs={{4,0},{6,2},{8,4},{10,6},{12,8},{14,10},{16,12},{18,14},{20,16},{2... | collective-permute-start | bytes 1179656 | tf_op jit(solution)/shard_map/ppermute | solution.py:24
  61.2 28.1 %collective-permute-start.6 = (bf16[256,768]{1,0:T(8,128)(2,1)}, bf16[256,768]{1,0:T(8,128)(2,1)S(1)}, u32[]{:S(2)}, u32[]{:S(2)}) collective-permute-start(bf16[256,768]{1,0:T(8,128)(2,1)} %get-tuple-element.27), channel_id=1, source_target_pairs={{0,4},{2,6},{4,8},{6,10},{8,12},{10,14},{12,16},{14,18},{16,20},{1... | collective-permute-start | bytes 1179656 | tf_op jit(solution)/shard_map/ppermute | solution.py:24
  79.5 5.3 %copy-start.16 = (bf16[256,768]{1,0:T(8,128)(2,1)S(1)}, bf16[256,768]{1,0:T(8,128)(2,1)}, u32[]{:S(2)}) copy-start(bf16[256,768]{1,0:T(8,128)(2,1)} %get-tuple-element.24) | copy-start | bytes 1179652
  82.2 2.7 %copy-start.2 = (bf16[1,512,1536]{2,1,0:T(8,128)(2,1)S(1)}, bf16[1,512,1536]{2,1,0:T(8,128)(2,1)}, u32[]{:S(2)}) copy-start(bf16[1,512,1536]{2,1,0:T(8,128)(2,1)} %param.7) | copy-start | bytes 4718596
  82.2 6.2 %slice-start = ((s8[7077888]{0:T(1024)(128)(4,1)}), s8[4194304]{0:T(1024)(128)(4,1)S(1)}, s32[]{:S(2)}) async-start(s8[7077888]{0:T(1024)(128)(4,1)} %bitcast.96), calls=%async_computation | async-start | bytes 8388608
  84.9 3.6 %slice-start.1 = ((s8[7077888]{0:T(1024)(128)(4,1)}), s8[2883584]{0:T(1024)(128)(4,1)S(1)}, s32[]{:S(2)}) async-start(s8[7077888]{0:T(1024)(128)(4,1)} %bitcast.96), calls=%async_computation.1 | async-start | bytes 5767168
  89.3 1.0 copy-start.17
  90.3 5.9 %copy-start.9 = (f32[256]{0:T(256)S(1)}, f32[256]{0:T(256)}, u32[]{:S(2)}) copy-start(f32[256]{0:T(256)} %copy-done.8) | copy-start | bytes 3076
  90.3 5.9 %copy-start.11 = (f32[256]{0:T(256)S(1)}, f32[256]{0:T(256)}, u32[]{:S(2)}) copy-start(f32[256]{0:T(256)} %copy-done.10) | copy-start | bytes 3076
  90.3 5.9 %copy-start.4 = (bf16[1,512,1536]{2,1,0:T(8,128)(2,1)S(1)}, bf16[1,512,1536]{2,1,0:T(8,128)(2,1)}, u32[]{:S(2)}) copy-start(bf16[1,512,1536]{2,1,0:T(8,128)(2,1)} %param.8) | copy-start | bytes 4718596
  92.8 5.2 %collective-permute-start.8 = (f32[2304]{0:T(1024)S(1)}, f32[2304]{0:T(1024)S(1)}, u32[]{:S(2)}, u32[]{:S(2)}) collective-permute-start(f32[2304]{0:T(1024)S(1)} %pad_maximum_fusion), channel_id=1, source_target_pairs={{0,16},{1,17},{2,18},{3,19},{4,20},{5,21},{6,22},{7,23},{8,24},{9,... | collective-permute-start | bytes 27656 | tf_op jit(solution)/shard_map/ppermute | solution.py:82
  96.2 1.0 copy-start.15
  97.2 2.6 %copy-start.14 = (bf16[256,768]{1,0:T(8,128)(2,1)S(1)}, bf16[256,768]{1,0:T(8,128)(2,1)}, u32[]{:S(2)}) copy-start(bf16[256,768]{1,0:T(8,128)(2,1)} %get-tuple-element.26) | copy-start | bytes 1179652
  98.0 3.8 %collective-permute-start.9 = (f32[2304]{0:T(1024)S(1)}, f32[2304]{0:T(1024)S(1)}, u32[]{:S(2)}, u32[]{:S(2)}) collective-permute-start(f32[2304]{0:T(1024)S(1)} %fusion.110), channel_id=1, source_target_pairs={{0,8},{1,9},{2,10},{3,11},{4,12},{5,13},{6,14},{7,15},{8,0},{9,1},... | collective-permute-start | bytes 27656 | tf_op jit(solution)/shard_map/ppermute | solution.py:82
  101.8 3.2 %collective-permute-start.10 = (f32[2304]{0:T(1024)S(1)}, f32[2304]{0:T(1024)S(1)}, u32[]{:S(2)}, u32[]{:S(2)}) collective-permute-start(f32[2304]{0:T(1024)S(1)} %add.201), channel_id=1, source_target_pairs={{0,2},{1,3},{2,0},{3,1},{4,6},{5,7},{6,4},{7,5},{8,10},{9,11},{10,... | collective-permute-start | bytes 27656 | tf_op jit(solution)/shard_map/ppermute | solution.py:82
  101.8 3.7 %collective-permute-start.11 = (f32[2304]{0:T(1024)S(1)}, f32[2304]{0:T(1024)S(1)}, u32[]{:S(2)}, u32[]{:S(2)}) collective-permute-start(f32[2304]{0:T(1024)S(1)} %add.201), channel_id=1, source_target_pairs={{0,4},{1,5},{2,6},{3,7},{4,0},{5,1},{6,2},{7,3},{8,12},{9,13},{10,... | collective-permute-start | bytes 27656 | tf_op jit(solution)/shard_map/ppermute | solution.py:82
  103.5 3.1 %collective-permute-start.12 = (f32[2304]{0:T(1024)S(1)}, f32[2304]{0:T(1024)S(1)}, u32[]{:S(2)}, u32[]{:S(2)}) collective-permute-start(f32[2304]{0:T(1024)S(1)} %add.201), channel_id=1, source_target_pairs={{0,6},{1,7},{2,4},{3,5},{4,2},{5,3},{6,0},{7,1},{8,14},{9,15},{10,... | collective-permute-start | bytes 27656 | tf_op jit(solution)/shard_map/ppermute | solution.py:82
  106.7 3.7 %collective-permute-start.13 = (f32[2304]{0:T(1024)S(1)}, f32[2304]{0:T(1024)S(1)}, u32[]{:S(2)}, u32[]{:S(2)}) collective-permute-start(f32[2304]{0:T(1024)S(1)} %add_add_fusion.2), channel_id=1, source_target_pairs={{0,1},{1,0},{2,3},{3,2},{4,5},{5,4},{6,7},{7,6},{8,9},{9,8},{10,11... | collective-permute-start | bytes 27656 | tf_op jit(solution)/shard_map/ppermute | solution.py:82
  (2 other events, 1.2 us)
